TPU v7x, 512 devices: a whole 4x8x8 slice. The times are simulated.
512 devices in a mesh: gx: 16 (over y, core), gy: 32 (over x, z).
Axes of the slice: x: 4, y: 8, z: 8, core: 2. Of those that a mesh axis runs over, the one named last changes fastest.
Arguments:
- adjoint_in: float32 [19, 4, 256, 4096], P(None, None, 'gx', 'gy'), may hold values from -6 to 6
- forward_pops: bfloat16 [2, 19, 4, 256, 4096], P(None, None, None, 'gx', 'gy'), may hold values from 0 to 0.42, as said below
- solid_mask: int32 [4, 256, 4096], P(None, 'gx', 'gy'), may hold values 0 or 1
- region_label: int32 [256, 4096], P('gx', 'gy'), may hold values from 0 to 2
- design: float32 [256, 4096], P('gx', 'gy'), may hold values from 0 to 1
Outputs:
- adjoint_out: float32 [19, 4, 256, 4096], P(None, None, 'gx', 'gy')
- sensitivity: float32 [256, 4096], P('gx', 'gy')
Inputs may be any that keep to these rules, and one draw needn't show every extreme that they name: `forward_pops`: each population lies between 0.75 and 1.25 times its lattice weight.
All inputs are finite; a program needn't handle non-finite values. No bound on the sum of `solid_mask` on one device may be relied on, other than what follows from the above.
Results may differ from a plain program's by a relative error of at most 0.0004.
Values sent between devices are 32-bit elements; how exact they have to be, the bound alone decides.
No kernel may reach another device: no remote copies, remote signals or barrier semaphores. Data moves between devices by JAX's collectives and lax.ppermute only.
A program may use at most 128 MiB of HBM per device.

v0:
```python
import jax
import jax.numpy as jnp
from jax import lax
from jax.sharding import PartitionSpec as P

SWEEPS = 4


VELOCITIES = [
    (0, 0, 0),
    (1, 0, 0),
    (-1, 0, 0),
    (0, 1, 0),
    (0, -1, 0),
    (0, 0, 1),
    (0, 0, -1),
    (1, 1, 0),
    (-1, -1, 0),
    (1, -1, 0),
    (-1, 1, 0),
    (1, 0, 1),
    (-1, 0, -1),
    (1, 0, -1),
    (-1, 0, 1),
    (0, 1, 1),
    (0, -1, -1),
    (0, 1, -1),
    (0, -1, 1),
]
OPPOSITE = [0, 2, 1, 4, 3, 6, 5, 8, 7, 10, 9, 12, 11, 14, 13, 16, 15, 18, 17]
WEIGHTS = [1.0 / 3.0] + [1.0 / 18.0] * 6 + [1.0 / 36.0] * 12
RELAX_RATES = [0.0] * 4 + [1.6] * 6 + [1.4] * 6 + [1.2] * 3
EXPONENTS = [
    (0, 0, 0),
    (1, 0, 0),
    (0, 1, 0),
    (0, 0, 1),
    (2, 0, 0),
    (0, 2, 0),
    (0, 0, 2),
    (1, 1, 0),
    (1, 0, 1),
    (0, 1, 1),
    (2, 1, 0),
    (2, 0, 1),
    (1, 2, 0),
    (0, 2, 1),
    (1, 0, 2),
    (0, 1, 2),
    (2, 2, 0),
    (2, 0, 2),
    (0, 2, 2),
]
BLOCK_LIMIT = 0.5
SENSE_SCALE = 20.0
FILTER_WEIGHT = 16.0


def extended(cells, sides, width):
    for axis, dim in sides:
        count = lax.axis_size(axis)
        ends = count - 1
        head = lax.slice_in_dim(cells, 0, width, axis=dim)
        tail = lax.slice_in_dim(cells, cells.shape[dim] - width, cells.shape[dim], axis=dim)
        cells = jnp.concatenate(
            [
                lax.ppermute(tail, axis, [(i, (i + 1) % count) for i in range(ends)]),
                cells,
                lax.ppermute(head, axis, [((i + 1) % count, i) for i in range(ends)]),
            ],
            axis=dim,
        )
    return cells


def moment_table():
    rows_out = []
    for expo in EXPONENTS:
        vector = [
            float(vel[0] ** expo[0] * vel[1] ** expo[1] * vel[2] ** expo[2]) for vel in VELOCITIES
        ]
        for prior in rows_out:
            factor = sum((a * b for a, b in zip(vector, prior))) / sum((b * b for b in prior))
            vector = [a - factor * b for a, b in zip(vector, prior)]
        rows_out.append(vector)
    norms = [sum((b * b for b in row)) for row in rows_out]
    table = []
    for first in range(19):
        line = []
        for second in range(19):
            line.append(
                sum(
                    (
                        rows_out[k][first] / norms[k] * RELAX_RATES[k] * rows_out[k][second]
                        for k in range(19)
                    )
                )
            )
        table.append(line)
    return table


def collide(popul, blocking):
    relax_matrix = jnp.asarray(moment_table(), jnp.float32)
    veloc = jnp.asarray(VELOCITIES, jnp.float32)
    weights = jnp.asarray(WEIGHTS, jnp.float32)
    density = jnp.sum(popul, axis=0)
    momentum = jnp.dot(veloc.T, popul, precision=lax.Precision.HIGHEST)
    velocity = momentum / density
    along_u = jnp.dot(veloc, velocity, precision=lax.Precision.HIGHEST)
    speed_sq = jnp.sum(velocity * velocity, axis=0)
    equilib = (
        weights[:, None]
        * density
        * (1.0 + 3.0 * along_u + 4.5 * along_u * along_u - 1.5 * speed_sq)
    )
    relaxed = popul - jnp.dot(relax_matrix, popul - equilib, precision=lax.Precision.HIGHEST)
    reflected = popul[jnp.asarray(OPPOSITE, jnp.int32)]
    return ((1.0 - blocking) * relaxed + blocking * reflected, reflected - relaxed)


def adjoint_cell(saved_now, pulled, blocking, lever):

    def forward(popul):
        return collide(popul, blocking)

    _, back_fn, change = jax.vjp(forward, saved_now, has_aux=True)
    (result,) = back_fn(pulled)
    term = jnp.sum(pulled * change, axis=0) * lever
    return (result, term)


def pull_back(padded, width_x, width_y):
    pieces = []
    for slot in range(19):
        step_x, step_y, step_z = VELOCITIES[slot]
        piece = padded[
            slot, :, 1 + step_x : 1 + step_x + width_x, 1 + step_y : 1 + step_y + width_y
        ]
        pieces.append(jnp.roll(piece, -step_z, axis=0))
    return jnp.stack(pieces)


def framed_adjoint(adjoint):
    return extended(adjoint, (("gx", 2), ("gy", 3)), 1)


def helmholtz(raw):
    scale_den = 1.0 + 4.0 * FILTER_WEIGHT
    smooth = raw
    for sweep in range(SWEEPS):
        framed = extended(smooth, (("gx", 0), ("gy", 1)), 1)
        beside_all = framed[:-2, 1:-1] + framed[2:, 1:-1] + framed[1:-1, :-2] + framed[1:-1, 2:]
        smooth = (raw + FILTER_WEIGHT * beside_all) / scale_den
    return smooth


def per_device(adjoint_in, forward_pops, solid_mask, region_label, design):
    planes, width_x, width_y = solid_mask.shape
    inside = region_label > 0
    blocking = jnp.where(
        solid_mask == 1, 1.0, jnp.where(inside[None], BLOCK_LIMIT * design[None], 0.0)
    )
    lever = jnp.where((solid_mask == 0) & inside[None], BLOCK_LIMIT, 0.0).astype(jnp.float32)
    adjoint = adjoint_in
    raw = jnp.zeros((width_x, width_y), jnp.float32)
    for section in (1, 0):
        pulled = pull_back(framed_adjoint(adjoint), width_x, width_y)
        saved_now = forward_pops[section].astype(jnp.float32)
        result, term = adjoint_cell(
            saved_now.reshape(19, -1),
            pulled.reshape(19, -1),
            blocking.reshape(-1),
            lever.reshape(-1),
        )
        adjoint = result.reshape(19, planes, width_x, width_y)
        raw = raw + jnp.sum(term.reshape(planes, width_x, width_y), axis=0)
    raw = SENSE_SCALE * raw
    smooth = helmholtz(raw)
    region_one = (region_label == 1).astype(jnp.float32)
    region_two = (region_label == 2).astype(jnp.float32)
    region_sums, region_counts = lax.psum(
        (
            jnp.stack([jnp.sum(smooth * region_one), jnp.sum(smooth * region_two)]),
            jnp.stack([jnp.sum(region_one), jnp.sum(region_two)]),
        ),
        ("gx", "gy"),
    )
    means = region_sums / jnp.maximum(region_counts, 1.0)
    sensitivity = region_one * (smooth - means[0]) + region_two * (smooth - means[1])
    return (adjoint, sensitivity)


def solution(mesh):
    in_specs = (
        P(None, None, "gx", "gy"),
        P(None, None, None, "gx", "gy"),
        P(None, "gx", "gy"),
        P("gx", "gy"),
        P("gx", "gy"),
    )
    out_specs = (P(None, None, "gx", "gy"), P("gx", "gy"))
    return jax.shard_map(
        per_device, mesh=mesh, in_specs=in_specs, out_specs=out_specs, check_vma=False
    )
```

profile of v0, /device:TPU:1, one launch (start us, length us, event | category | flops | bytes accessed | tf_op | source)
XLA Modules:
  0.0 312.4 jit_solution(11993003291786837664)
XLA Ops:
  2.5 4.6 %collective-permute-start.1 = (f32[19,4,1,128]{3,0,2,1:T(8,128)}, f32[19,4,1,128]{3,0,2,1:T(8,128)}, u32[]{:S(2)}, u32[]{:S(2)}) collective-permute-start(f32[19,4,1,128]{3,0,2,1:T(8,128)} %copy.101), channel_id=1, source_target_pairs={{0,32},{32,64},{64,96},{96,128},{128,160},{160,192},{192,224},{224... | collective-permute-start | bytes 116744 | tf_op jit(solution)/shard_map/ppermute | solution.py:67
  7.7 6.1 %collective-permute-start = (f32[19,4,1,128]{3,0,2,1:T(8,128)}, f32[19,4,1,128]{3,0,2,1:T(8,128)}, u32[]{:S(2)}, u32[]{:S(2)}) collective-permute-start(f32[19,4,1,128]{3,0,2,1:T(8,128)} %copy.100), channel_id=1, source_target_pairs={{32,0},{64,32},{96,64},{128,96},{160,128},{192,160},{224,192},{256... | collective-permute-start | bytes 116744 | tf_op jit(solution)/shard_map/ppermute | solution.py:69
  13.8 2.0 constant_dynamic-update-slice_fusion
  20.0 2.4 fusion.112
  23.6 1.7 fusion.113
  26.6 4.1 %copy.90 = f32[19,4,16,128]{2,0,3,1:T(8,128)} copy(f32[19,4,16,128]{3,2,1,0:T(8,128)S(1)} %copy-done.1) | data formatting | bytes 1245184 | tf_op args[0]
  35.8 2.6 dynamic-update-slice.3
  40.6 5.0 %copy.89 = f32[19,4,1,128]{2,0,3,1:T(8,128)} copy(f32[19,4,1,128]{3,0,2,1:T(8,128)} %collective-permute-done.1) | data formatting | bytes 77824 | tf_op jit(solution)/shard_map/ppermute | solution.py:67
  45.6 4.9 %copy.91 = f32[19,4,1,128]{2,0,3,1:T(8,128)} copy(f32[19,4,1,128]{3,0,2,1:T(8,128)} %collective-permute-done) | data formatting | bytes 77824 | tf_op jit(solution)/shard_map/ppermute | solution.py:69
  50.5 8.1 %pad_maximum_fusion = f32[19,4,18,128]{2,0,3,1:T(8,128)S(1)} fusion(f32[19,4,1,128]{2,0,3,1:T(8,128)} %copy.91, f32[19,4,16,128]{2,0,3,1:T(8,128)} %copy.90, f32[19,4,1,128]{2,0,3,1:T(8,128)} %copy.89), kind=kLoop, calls=%fused_computation.16 | loop fusion | flops 350208 | bytes 1400832 | tf_op jit(solution)/shard_map/concatenate | solution.py:65
  58.7 2.7 copy-done
  62.6 4.6 %collective-permute-start.3 = (f32[19,4,18,1]{2,0,3,1:T(8,128)S(1)}, f32[19,4,18,1]{2,0,3,1:T(8,128)}, u32[]{:S(2)}, u32[]{:S(2)}) collective-permute-start(f32[19,4,18,1]{2,0,3,1:T(8,128)S(1)} %get-tuple-element.21), channel_id=1, source_target_pairs={{0,1},{1,2},{2,3},{3,4},{4,5},{5,6},{6,7},{7,8},{8,9},{9,10},{10,1... | collective-permute-start | bytes 16424 | tf_op jit(solution)/shard_map/ppermute | solution.py:67
  69.1 4.5 %copy.92 = f32[19,4,18,128]{3,0,2,1:T(8,128)S(1)} copy(f32[19,4,18,128]{2,0,3,1:T(8,128)} %copy-done) | data formatting | bytes 1400832 | tf_op jit(solution)/shard_map/concatenate | solution.py:65
  79.1 2.6 stack.155
  81.7 2.4 fusion.38
  84.2 2.1 multiply_reduce_fusion.4
  87.9 1.8 scatter_custom_fusion
  91.6 1.9 collective-permute-start.4
  93.5 3.6 %collective-permute-start.5 = (f32[19,4,1,128]{3,2,1,0:T(1,128)S(1)}, f32[19,4,1,128]{3,2,1,0:T(1,128)S(1)}, u32[]{:S(2)}, u32[]{:S(2)}) collective-permute-start(f32[19,4,1,128]{3,2,1,0:T(1,128)S(1)} %get-tuple-element.85), channel_id=1, source_target_pairs={{0,32},{32,64},{64,96},{96,128},{128,160},{160,192},{192,224},{224... | collective-permute-start | bytes 116744 | tf_op jit(solution)/shard_map/ppermute | solution.py:67
  97.2 2.5 fusion.7
  99.8 2.6 dynamic-update-slice.1
  106.9 4.6 %collective-permute-start.7 = (f32[19,4,18,1]{0,1,3,2:T(4,128)S(1)}, f32[19,4,18,1]{0,1,3,2:T(4,128)}, u32[]{:S(2)}, u32[]{:S(2)}) collective-permute-start(f32[19,4,18,1]{0,1,3,2:T(4,128)S(1)} %copy.98), channel_id=1, source_target_pairs={{0,1},{1,2},{2,3},{3,4},{4,5},{5,6},{6,7},{7,8},{8,9},{9,10},{10,1... | collective-permute-start | bytes 16424 | tf_op jit(solution)/shard_map/ppermute | solution.py:67
  113.4 1.8 copy.99
  117.6 2.5 stack.174
  120.2 2.3 fusion.39
  122.6 2.3 fusion.6
  124.9 2.5 collective-permute-start.8
  127.4 1.9 collective-permute-start.9
  129.4 2.9 collective-permute-done.9
  132.4 3.1 collective-permute-start.10
  136.8 3.1 %collective-permute-done.11 = f32[18,1]{1,0:T(8,128)S(1)} collective-permute-done((f32[18,1]{1,0:T(8,128)S(1)}, f32[18,1]{1,0:T(8,128)S(1)}, u32[]{:S(2)}, u32[]{:S(2)}) %collective-permute-start.11) | collective-permute-done | bytes 104 | tf_op jit(solution)/shard_map/ppermute | solution.py:69
  140.0 3.5 %collective-permute-start.12 = (f32[1,128]{1,0:T(1,128)S(1)}, f32[1,128]{1,0:T(1,128)S(1)}, u32[]{:S(2)}, u32[]{:S(2)}) collective-permute-start(f32[1,128]{1,0:T(1,128)S(1)} %get-tuple-element.107), channel_id=1, source_target_pairs={{0,32},{32,64},{64,96},{96,128},{128,160},{160,192},{192,224},{224... | collective-permute-start | bytes 1544 | tf_op jit(solution)/shard_map/ppermute | solution.py:67
  143.5 1.9 collective-permute-start.13
  145.4 2.1 multiply_reduce_fusion.2
  148.5 4.0 %collective-permute-start.14 = (f32[18,1]{1,0:T(8,128)S(1)}, f32[18,1]{1,0:T(8,128)S(1)}, u32[]{:S(2)}, u32[]{:S(2)}) collective-permute-start(f32[18,1]{1,0:T(8,128)S(1)} %get-tuple-element.99), channel_id=1, source_target_pairs={{0,1},{1,2},{2,3},{3,4},{4,5},{5,6},{6,7},{7,8},{8,9},{9,10},{10,1... | collective-permute-start | bytes 224 | tf_op jit(solution)/shard_map/ppermute | solution.py:67
  153.8 4.8 %collective-permute-done.15 = f32[18,1]{1,0:T(8,128)S(1)} collective-permute-done((f32[18,1]{1,0:T(8,128)S(1)}, f32[18,1]{1,0:T(8,128)S(1)}, u32[]{:S(2)}, u32[]{:S(2)}) %collective-permute-start.15) | collective-permute-done | bytes 104 | tf_op jit(solution)/shard_map/ppermute | solution.py:69
  158.7 3.9 %collective-permute-start.16 = (f32[1,128]{1,0:T(1,128)S(1)}, f32[1,128]{1,0:T(1,128)S(1)}, u32[]{:S(2)}, u32[]{:S(2)}) collective-permute-start(f32[1,128]{1,0:T(1,128)S(1)} %get-tuple-element.105), channel_id=1, source_target_pairs={{0,32},{32,64},{64,96},{96,128},{128,160},{160,192},{192,224},{224... | collective-permute-start | bytes 1544 | tf_op jit(solution)/shard_map/ppermute | solution.py:67
  162.7 1.9 collective-permute-start.17
  164.6 2.9 collective-permute-done.17
  167.6 4.8 %collective-permute-start.18 = (f32[18,1]{1,0:T(8,128)S(1)}, f32[18,1]{1,0:T(8,128)S(1)}, u32[]{:S(2)}, u32[]{:S(2)}) collective-permute-start(f32[18,1]{1,0:T(8,128)S(1)} %get-tuple-element.97), channel_id=1, source_target_pairs={{0,1},{1,2},{2,3},{3,4},{4,5},{5,6},{6,7},{7,8},{8,9},{9,10},{10,1... | collective-permute-start | bytes 224 | tf_op jit(solution)/shard_map/ppermute | solution.py:67
  173.8 3.4 %collective-permute-done.19 = f32[18,1]{1,0:T(8,128)S(1)} collective-permute-done((f32[18,1]{1,0:T(8,128)S(1)}, f32[18,1]{1,0:T(8,128)S(1)}, u32[]{:S(2)}, u32[]{:S(2)}) %collective-permute-start.19) | collective-permute-done | bytes 104 | tf_op jit(solution)/shard_map/ppermute | solution.py:69
  177.3 3.1 collective-permute-start.20
  180.4 1.9 collective-permute-start.21
  183.2 1.8 scatter_custom_fusion.1
  185.4 3.6 %collective-permute-start.22 = (f32[18,1]{1,0:T(8,128)S(1)}, f32[18,1]{1,0:T(8,128)S(1)}, u32[]{:S(2)}, u32[]{:S(2)}) collective-permute-start(f32[18,1]{1,0:T(8,128)S(1)} %get-tuple-element.95), channel_id=1, source_target_pairs={{0,1},{1,2},{2,3},{3,4},{4,5},{5,6},{6,7},{7,8},{8,9},{9,10},{10,1... | collective-permute-start | bytes 224 | tf_op jit(solution)/shard_map/ppermute | solution.py:67
  190.3 4.5 %collective-permute-done.23 = f32[18,1]{1,0:T(8,128)S(1)} collective-permute-done((f32[18,1]{1,0:T(8,128)S(1)}, f32[18,1]{1,0:T(8,128)S(1)}, u32[]{:S(2)}, u32[]{:S(2)}) %collective-permute-start.23) | collective-permute-done | bytes 104 | tf_op jit(solution)/shard_map/ppermute | solution.py:69
  199.2 110.6 %all-reduce = (f32[2]{0:T(128)S(1)}, f32[2]{0:T(128)S(1)}) all-reduce(f32[2]{0:T(128)S(1)} %pad_maximum_fusion.88, f32[2]{0:T(128)S(1)} %pad_maximum_fusion.89), channel_id=1, replica_groups=mesh['gx'=16,'gy'=32] {'gx','gy'}, use_global_device_ids=true, to_apply=%region_18.19 | all-reduce | flops 4 | bytes 32 | tf_op jit(solution)/shard_map/psum | solution.py:182
  310.5 1.9 select_add_fusion
  (161 shorter events, 50.1 us)
Async XLA Ops:
  0.6 22.6 %copy-start.4 = (f32[19,3]{1,0:T(8,128)S(1)}, f32[19,3]{1,0:T(8,128)}, u32[]{:S(2)}) copy-start(f32[19,3]{1,0:T(8,128)} %constant.52.clone) | copy-start | bytes 688
  0.6 26.0 %copy-start.17 = (s32[19]{0:T(128)S(1)}, s32[19]{0:T(128)}, u32[]{:S(2)}) copy-start(s32[19]{0:T(128)} %constant.59) | copy-start | bytes 232
  0.7 26.0 %copy-start.1 = (f32[19,4,16,128]{3,2,1,0:T(8,128)S(1)}, f32[19,4,16,128]{3,2,1,0:T(8,128)}, u32[]{:S(2)}) copy-start(f32[19,4,16,128]{3,2,1,0:T(8,128)} %param.13) | copy-start | bytes 1867780
  0.7 25.3 %copy-start.13 = (s32[16,128]{1,0:T(8,128)S(1)}, s32[16,128]{1,0:T(8,128)}, u32[]{:S(2)}) copy-start(s32[16,128]{1,0:T(8,128)} %param.16) | copy-start | bytes 24580
  0.7 25.3 %copy-start.15 = (f32[16,128]{1,0:T(8,128)S(1)}, f32[16,128]{1,0:T(8,128)}, u32[]{:S(2)}) copy-start(f32[16,128]{1,0:T(8,128)} %param.17) | copy-start | bytes 24580
  0.7 25.3 %copy-start.7 = (s32[4,16,128]{2,1,0:T(8,128)S(1)}, s32[4,16,128]{2,1,0:T(8,128)}, u32[]{:S(2)}) copy-start(s32[4,16,128]{2,1,0:T(8,128)} %param.15) | copy-start | bytes 98308
  2.5 31.6 %collective-permute-start.1 = (f32[19,4,1,128]{3,0,2,1:T(8,128)}, f32[19,4,1,128]{3,0,2,1:T(8,128)}, u32[]{:S(2)}, u32[]{:S(2)}) collective-permute-start(f32[19,4,1,128]{3,0,2,1:T(8,128)} %copy.101), channel_id=1, source_target_pairs={{0,32},{32,64},{64,96},{96,128},{128,160},{160,192},{192,224},{224... | collective-permute-start | bytes 116744 | tf_op jit(solution)/shard_map/ppermute | solution.py:67
  7.7 27.3 %collective-permute-start = (f32[19,4,1,128]{3,0,2,1:T(8,128)}, f32[19,4,1,128]{3,0,2,1:T(8,128)}, u32[]{:S(2)}, u32[]{:S(2)}) collective-permute-start(f32[19,4,1,128]{3,0,2,1:T(8,128)} %copy.100), channel_id=1, source_target_pairs={{32,0},{64,32},{96,64},{128,96},{160,128},{192,160},{224,192},{256... | collective-permute-start | bytes 116744 | tf_op jit(solution)/shard_map/ppermute | solution.py:69
  20.0 10.9 %copy-start.11 = (f32[3,8192]{1,0:T(4,128)}, f32[3,8192]{1,0:T(4,128)S(1)}, u32[]{:S(2)}) copy-start(f32[3,8192]{1,0:T(4,128)S(1)} %get-tuple-element.114) | copy-start | bytes 294916
  23.6 8.8 %copy-start.10 = (f32[3,8192]{1,0:T(4,128)}, f32[3,8192]{1,0:T(4,128)S(1)}, u32[]{:S(2)}) copy-start(f32[3,8192]{1,0:T(4,128)S(1)} %get-tuple-element.119) | copy-start | bytes 294916
  58.7 2.7 copy-start
  61.3 13.7 %collective-permute-start.2 = (f32[19,4,18,1]{2,0,3,1:T(8,128)S(1)}, f32[19,4,18,1]{2,0,3,1:T(8,128)S(1)}, u32[]{:S(2)}, u32[]{:S(2)}) collective-permute-start(f32[19,4,18,1]{2,0,3,1:T(8,128)S(1)} %get-tuple-element.22), channel_id=1, source_target_pairs={{1,0},{2,1},{3,2},{4,3},{5,4},{6,5},{7,6},{8,7},{9,8},{10,9},{11,1... | collective-permute-start | bytes 16424 | tf_op jit(solution)/shard_map/ppermute | solution.py:69
  62.6 13.1 %collective-permute-start.3 = (f32[19,4,18,1]{2,0,3,1:T(8,128)S(1)}, f32[19,4,18,1]{2,0,3,1:T(8,128)}, u32[]{:S(2)}, u32[]{:S(2)}) collective-permute-start(f32[19,4,18,1]{2,0,3,1:T(8,128)S(1)} %get-tuple-element.21), channel_id=1, source_target_pairs={{0,1},{1,2},{2,3},{3,4},{4,5},{5,6},{6,7},{7,8},{8,9},{9,10},{10,1... | collective-permute-start | bytes 16424 | tf_op jit(solution)/shard_map/ppermute | solution.py:67
  84.2 13.0 %copy-start.6 = (f32[8192]{0:T(1024)S(1)}, f32[8192]{0:T(1024)}, u32[]{:S(2)}) copy-start(f32[8192]{0:T(1024)} %get-tuple-element.129) | copy-start | bytes 98308
  84.2 13.0 %copy-start.12 = (f32[19,19]{1,0:T(8,128)S(1)}, f32[19,19]{1,0:T(8,128)}, u32[]{:S(2)}) copy-start(f32[19,19]{1,0:T(8,128)} %constant.16.clone) | copy-start | bytes 4336
  84.2 13.0 %copy-start.16 = (f32[19]{0:T(128)S(1)}, f32[19]{0:T(128)}, u32[]{:S(2)}) copy-start(f32[19]{0:T(128)} %constant.53.clone) | copy-start | bytes 232
  91.6 8.2 %collective-permute-start.4 = (f32[19,4,1,128]{3,2,1,0:T(1,128)S(1)}, f32[19,4,1,128]{3,2,1,0:T(1,128)S(1)}, u32[]{:S(2)}, u32[]{:S(2)}) collective-permute-start(f32[19,4,1,128]{3,2,1,0:T(1,128)S(1)} %get-tuple-element.86), channel_id=1, source_target_pairs={{32,0},{64,32},{96,64},{128,96},{160,128},{192,160},{224,192},{256... | collective-permute-start | bytes 116744 | tf_op jit(solution)/shard_map/ppermute | solution.py:69
  93.5 10.4 %collective-permute-start.5 = (f32[19,4,1,128]{3,2,1,0:T(1,128)S(1)}, f32[19,4,1,128]{3,2,1,0:T(1,128)S(1)}, u32[]{:S(2)}, u32[]{:S(2)}) collective-permute-start(f32[19,4,1,128]{3,2,1,0:T(1,128)S(1)} %get-tuple-element.85), channel_id=1, source_target_pairs={{0,32},{32,64},{64,96},{96,128},{128,160},{160,192},{192,224},{224... | collective-permute-start | bytes 116744 | tf_op jit(solution)/shard_map/ppermute | solution.py:67
  105.0 7.4 %collective-permute-start.6 = (f32[19,4,18,1]{0,1,3,2:T(4,128)S(1)}, f32[19,4,18,1]{0,1,3,2:T(4,128)S(1)}, u32[]{:S(2)}, u32[]{:S(2)}) collective-permute-start(f32[19,4,18,1]{0,1,3,2:T(4,128)S(1)} %copy.96), channel_id=1, source_target_pairs={{1,0},{2,1},{3,2},{4,3},{5,4},{6,5},{7,6},{8,7},{9,8},{10,9},{11,1... | collective-permute-start | bytes 16424 | tf_op jit(solution)/shard_map/ppermute | solution.py:69
  106.9 6.5 %collective-permute-start.7 = (f32[19,4,18,1]{0,1,3,2:T(4,128)S(1)}, f32[19,4,18,1]{0,1,3,2:T(4,128)}, u32[]{:S(2)}, u32[]{:S(2)}) collective-permute-start(f32[19,4,18,1]{0,1,3,2:T(4,128)S(1)} %copy.98), channel_id=1, source_target_pairs={{0,1},{1,2},{2,3},{3,4},{4,5},{5,6},{6,7},{7,8},{8,9},{9,10},{10,1... | collective-permute-start | bytes 16424 | tf_op jit(solution)/shard_map/ppermute | solution.py:67
  111.5 6.2 %copy-start.9 = (f32[1,8192]{1,0:T(1,128)S(1)}, f32[1,8192]{1,0:T(1,128)}, u32[]{:S(2)}) copy-start(f32[1,8192]{1,0:T(1,128)} %slice.694) | copy-start | bytes 98308
  111.5 8.6 %copy-start.3 = (f32[8192]{0:T(1024)S(1)}, f32[8192]{0:T(1024)}, u32[]{:S(2)}) copy-start(f32[8192]{0:T(1024)} %get-tuple-element.130) | copy-start | bytes 98308
  111.5 8.6 %copy-start.5 = (f32[8192]{0:T(1024)S(1)}, f32[8192]{0:T(1024)}, u32[]{:S(2)}) copy-start(f32[8192]{0:T(1024)} %broadcast_multiply_fusion) | copy-start | bytes 98308
  115.4 9.5 %copy-start.8 = (s32[4,16,128]{2,1,0:T(8,128)S(1)}, s32[4,16,128]{2,1,0:T(8,128)}, u32[]{:S(2)}) copy-start(s32[4,16,128]{2,1,0:T(8,128)} %param.15) | copy-start | bytes 98308
  117.5 5.1 %copy-start.2 = (f32[19,8192]{1,0:T(8,128)S(1)}, f32[19,8192]{1,0:T(8,128)}, u32[]{:S(2)}) copy-start(f32[19,8192]{1,0:T(8,128)} %gather_fusion.1) | copy-start | bytes 1867780
  122.6 72.3 %copy-start.14 = (s32[16,128]{1,0:T(8,128)S(1)}, s32[16,128]{1,0:T(8,128)}, u32[]{:S(2)}) copy-start(s32[16,128]{1,0:T(8,128)} %param.16) | copy-start | bytes 24580
  124.9 4.4 %collective-permute-start.8 = (f32[1,128]{1,0:T(1,128)S(1)}, f32[1,128]{1,0:T(1,128)S(1)}, u32[]{:S(2)}, u32[]{:S(2)}) collective-permute-start(f32[1,128]{1,0:T(1,128)S(1)} %get-tuple-element.109), channel_id=1, source_target_pairs={{0,32},{32,64},{64,96},{96,128},{128,160},{160,192},{192,224},{224... | collective-permute-start | bytes 1544 | tf_op jit(solution)/shard_map/ppermute | solution.py:67
  127.4 4.9 %collective-permute-start.9 = (f32[1,128]{1,0:T(1,128)S(1)}, f32[1,128]{1,0:T(1,128)S(1)}, u32[]{:S(2)}, u32[]{:S(2)}) collective-permute-start(f32[1,128]{1,0:T(1,128)S(1)} %get-tuple-element.110), channel_id=1, source_target_pairs={{32,0},{64,32},{96,64},{128,96},{160,128},{192,160},{224,192},{256... | collective-permute-start | bytes 1544 | tf_op jit(solution)/shard_map/ppermute | solution.py:69
  132.4 4.4 %collective-permute-start.10 = (f32[18,1]{1,0:T(8,128)S(1)}, f32[18,1]{1,0:T(8,128)S(1)}, u32[]{:S(2)}, u32[]{:S(2)}) collective-permute-start(f32[18,1]{1,0:T(8,128)S(1)} %get-tuple-element.101), channel_id=1, source_target_pairs={{0,1},{1,2},{2,3},{3,4},{4,5},{5,6},{6,7},{7,8},{8,9},{9,10},{10,1... | collective-permute-start | bytes 224 | tf_op jit(solution)/shard_map/ppermute | solution.py:67
  135.5 4.4 %collective-permute-start.11 = (f32[18,1]{1,0:T(8,128)S(1)}, f32[18,1]{1,0:T(8,128)S(1)}, u32[]{:S(2)}, u32[]{:S(2)}) collective-permute-start(f32[18,1]{1,0:T(8,128)S(1)} %get-tuple-element.102), channel_id=1, source_target_pairs={{1,0},{2,1},{3,2},{4,3},{5,4},{6,5},{7,6},{8,7},{9,8},{10,9},{11,1... | collective-permute-start | bytes 224 | tf_op jit(solution)/shard_map/ppermute | solution.py:69
  140.0 7.5 %collective-permute-start.12 = (f32[1,128]{1,0:T(1,128)S(1)}, f32[1,128]{1,0:T(1,128)S(1)}, u32[]{:S(2)}, u32[]{:S(2)}) collective-permute-start(f32[1,128]{1,0:T(1,128)S(1)} %get-tuple-element.107), channel_id=1, source_target_pairs={{0,32},{32,64},{64,96},{96,128},{128,160},{160,192},{192,224},{224... | collective-permute-start | bytes 1544 | tf_op jit(solution)/shard_map/ppermute | solution.py:67
  143.5 4.9 %collective-permute-start.13 = (f32[1,128]{1,0:T(1,128)S(1)}, f32[1,128]{1,0:T(1,128)S(1)}, u32[]{:S(2)}, u32[]{:S(2)}) collective-permute-start(f32[1,128]{1,0:T(1,128)S(1)} %get-tuple-element.108), channel_id=1, source_target_pairs={{32,0},{64,32},{96,64},{128,96},{160,128},{192,160},{224,192},{256... | collective-permute-start | bytes 1544 | tf_op jit(solution)/shard_map/ppermute | solution.py:69
  148.5 5.3 %collective-permute-start.14 = (f32[18,1]{1,0:T(8,128)S(1)}, f32[18,1]{1,0:T(8,128)S(1)}, u32[]{:S(2)}, u32[]{:S(2)}) collective-permute-start(f32[18,1]{1,0:T(8,128)S(1)} %get-tuple-element.99), channel_id=1, source_target_pairs={{0,1},{1,2},{2,3},{3,4},{4,5},{5,6},{6,7},{7,8},{8,9},{9,10},{10,1... | collective-permute-start | bytes 224 | tf_op jit(solution)/shard_map/ppermute | solution.py:67
  152.5 6.1 %collective-permute-start.15 = (f32[18,1]{1,0:T(8,128)S(1)}, f32[18,1]{1,0:T(8,128)S(1)}, u32[]{:S(2)}, u32[]{:S(2)}) collective-permute-start(f32[18,1]{1,0:T(8,128)S(1)} %get-tuple-element.100), channel_id=1, source_target_pairs={{1,0},{2,1},{3,2},{4,3},{5,4},{6,5},{7,6},{8,7},{9,8},{10,9},{11,1... | collective-permute-start | bytes 224 | tf_op jit(solution)/shard_map/ppermute | solution.py:69
  158.7 5.9 %collective-permute-start.16 = (f32[1,128]{1,0:T(1,128)S(1)}, f32[1,128]{1,0:T(1,128)S(1)}, u32[]{:S(2)}, u32[]{:S(2)}) collective-permute-start(f32[1,128]{1,0:T(1,128)S(1)} %get-tuple-element.105), channel_id=1, source_target_pairs={{0,32},{32,64},{64,96},{96,128},{128,160},{160,192},{192,224},{224... | collective-permute-start | bytes 1544 | tf_op jit(solution)/shard_map/ppermute | solution.py:67
  162.7 4.9 %collective-permute-start.17 = (f32[1,128]{1,0:T(1,128)S(1)}, f32[1,128]{1,0:T(1,128)S(1)}, u32[]{:S(2)}, u32[]{:S(2)}) collective-permute-start(f32[1,128]{1,0:T(1,128)S(1)} %get-tuple-element.106), channel_id=1, source_target_pairs={{32,0},{64,32},{96,64},{128,96},{160,128},{192,160},{224,192},{256... | collective-permute-start | bytes 1544 | tf_op jit(solution)/shard_map/ppermute | solution.py:69
  167.6 6.1 %collective-permute-start.18 = (f32[18,1]{1,0:T(8,128)S(1)}, f32[18,1]{1,0:T(8,128)S(1)}, u32[]{:S(2)}, u32[]{:S(2)}) collective-permute-start(f32[18,1]{1,0:T(8,128)S(1)} %get-tuple-element.97), channel_id=1, source_target_pairs={{0,1},{1,2},{2,3},{3,4},{4,5},{5,6},{6,7},{7,8},{8,9},{9,10},{10,1... | collective-permute-start | bytes 224 | tf_op jit(solution)/shard_map/ppermute | solution.py:67
  172.5 4.7 %collective-permute-start.19 = (f32[18,1]{1,0:T(8,128)S(1)}, f32[18,1]{1,0:T(8,128)S(1)}, u32[]{:S(2)}, u32[]{:S(2)}) collective-permute-start(f32[18,1]{1,0:T(8,128)S(1)} %get-tuple-element.98), channel_id=1, source_target_pairs={{1,0},{2,1},{3,2},{4,3},{5,4},{6,5},{7,6},{8,7},{9,8},{10,9},{11,1... | collective-permute-start | bytes 224 | tf_op jit(solution)/shard_map/ppermute | solution.py:69
  177.3 7.8 %collective-permute-start.20 = (f32[1,128]{1,0:T(1,128)S(1)}, f32[1,128]{1,0:T(1,128)S(1)}, u32[]{:S(2)}, u32[]{:S(2)}) collective-permute-start(f32[1,128]{1,0:T(1,128)S(1)} %get-tuple-element.103), channel_id=1, source_target_pairs={{0,32},{32,64},{64,96},{96,128},{128,160},{160,192},{192,224},{224... | collective-permute-start | bytes 1544 | tf_op jit(solution)/shard_map/ppermute | solution.py:67
  180.4 4.9 %collective-permute-start.21 = (f32[1,128]{1,0:T(1,128)S(1)}, f32[1,128]{1,0:T(1,128)S(1)}, u32[]{:S(2)}, u32[]{:S(2)}) collective-permute-start(f32[1,128]{1,0:T(1,128)S(1)} %get-tuple-element.104), channel_id=1, source_target_pairs={{32,0},{64,32},{96,64},{128,96},{160,128},{192,160},{224,192},{256... | collective-permute-start | bytes 1544 | tf_op jit(solution)/shard_map/ppermute | solution.py:69
  185.4 4.9 %collective-permute-start.22 = (f32[18,1]{1,0:T(8,128)S(1)}, f32[18,1]{1,0:T(8,128)S(1)}, u32[]{:S(2)}, u32[]{:S(2)}) collective-permute-start(f32[18,1]{1,0:T(8,128)S(1)} %get-tuple-element.95), channel_id=1, source_target_pairs={{0,1},{1,2},{2,3},{3,4},{4,5},{5,6},{6,7},{7,8},{8,9},{9,10},{10,1... | collective-permute-start | bytes 224 | tf_op jit(solution)/shard_map/ppermute | solution.py:67
  189.0 5.8 %collective-permute-start.23 = (f32[18,1]{1,0:T(8,128)S(1)}, f32[18,1]{1,0:T(8,128)S(1)}, u32[]{:S(2)}, u32[]{:S(2)}) collective-permute-start(f32[18,1]{1,0:T(8,128)S(1)} %get-tuple-element.96), channel_id=1, source_target_pairs={{1,0},{2,1},{3,2},{4,3},{5,4},{6,5},{7,6},{8,7},{9,8},{10,9},{11,1... | collective-permute-start | bytes 224 | tf_op jit(solution)/shard_map/ppermute | solution.py:69
where the time goes:
time: 315 us; the launch traced here: 312 us
  blocking collectives  111 us (35%)
  starting transfers between devices  69.4 us (22%)
  local copies, waits for them, and re-layouts  58.2 us (18%)
  other arithmetic  28.2 us (9%)
  waiting for transfers between devices  22.8 us (7%)
  matrix products  21.7 us (7%)
    psum x1, blocking collectives, per_device(): lax.psum((jnp.stack([jnp.sum(smooth * region_one), jnp.sum(smooth * regio...  111 us
    ppermute x12, starting transfers between devices, extended(): lax.ppermute(tail, axis, [(i, (i + 1) % count) for i in range(ends)])  46 us
    ppermute x12, starting transfers between devices, extended(): lax.ppermute(head, axis, [((i + 1) % count, i) for i in range(ends)])  23.4 us
    ppermute x12, waiting for transfers between devices, extended(): lax.ppermute(head, axis, [((i + 1) % count, i) for i in range(ends)])  22.7 us
    unnamed x45, local copies, waits for them, and re-layouts  12.3 us
    concatenate x3, local copies, waits for them, and re-layouts, extended(): jnp.concatenate([lax.ppermute(tail, axis, [(i, (i + 1) % count) for i in...  9.7 us
    dot_general x4, matrix products, collide(): jnp.dot(relax_matrix, popul - equilib, precision=lax.Precision.HIGHEST)  9.56 us
    ppermute x4, local copies, waits for them, and re-layouts, extended(): lax.ppermute(tail, axis, [(i, (i + 1) % count) for i in range(ends)])  9.16 us
  transfers between devices with their start and end apart: 24, of which 8 were waited for; matrix products, arithmetic and copies ran while one was open for 14% of the time, Pallas kernels for 0%

commit v1 on v0

v1 whole, which is shorter than its diff:
```python
import jax
import jax.numpy as jnp
from jax import lax
from jax.sharding import PartitionSpec as P

SWEEPS = 4


VELOCITIES = [
    (0, 0, 0),
    (1, 0, 0),
    (-1, 0, 0),
    (0, 1, 0),
    (0, -1, 0),
    (0, 0, 1),
    (0, 0, -1),
    (1, 1, 0),
    (-1, -1, 0),
    (1, -1, 0),
    (-1, 1, 0),
    (1, 0, 1),
    (-1, 0, -1),
    (1, 0, -1),
    (-1, 0, 1),
    (0, 1, 1),
    (0, -1, -1),
    (0, 1, -1),
    (0, -1, 1),
]
OPPOSITE = [0, 2, 1, 4, 3, 6, 5, 8, 7, 10, 9, 12, 11, 14, 13, 16, 15, 18, 17]
WEIGHTS = [1.0 / 3.0] + [1.0 / 18.0] * 6 + [1.0 / 36.0] * 12
RELAX_RATES = [0.0] * 4 + [1.6] * 6 + [1.4] * 6 + [1.2] * 3
EXPONENTS = [
    (0, 0, 0),
    (1, 0, 0),
    (0, 1, 0),
    (0, 0, 1),
    (2, 0, 0),
    (0, 2, 0),
    (0, 0, 2),
    (1, 1, 0),
    (1, 0, 1),
    (0, 1, 1),
    (2, 1, 0),
    (2, 0, 1),
    (1, 2, 0),
    (0, 2, 1),
    (1, 0, 2),
    (0, 1, 2),
    (2, 2, 0),
    (2, 0, 2),
    (0, 2, 2),
]
BLOCK_LIMIT = 0.5
SENSE_SCALE = 20.0
FILTER_WEIGHT = 16.0

import functools

from jax.experimental import pallas as pl
from jax.experimental.pallas import tpu as pltpu

def moment_table():
    rows_out = []
    for expo in EXPONENTS:
        vector = [
            float(vel[0] ** expo[0] * vel[1] ** expo[1] * vel[2] ** expo[2]) for vel in VELOCITIES
        ]
        for prior in rows_out:
            factor = sum((a * b for a, b in zip(vector, prior))) / sum((b * b for b in prior))
            vector = [a - factor * b for a, b in zip(vector, prior)]
        rows_out.append(vector)
    norms = [sum((b * b for b in row)) for row in rows_out]
    table = []
    for first in range(19):
        line = []
        for second in range(19):
            line.append(
                sum(
                    (
                        rows_out[k][first] / norms[k] * RELAX_RATES[k] * rows_out[k][second]
                        for k in range(19)
                    )
                )
            )
        table.append(line)
    return table


RELAX = moment_table()


def neighbour_pairs(dx, dy, nx, ny):
    pairs = []
    for i in range(nx):
        for j in range(ny):
            ti, tj = i + dx, j + dy
            if 0 <= ti < nx and 0 <= tj < ny:
                pairs.append((i * ny + j, ti * ny + tj))
    return pairs


def halo(cells, w):
    nx = lax.axis_size("gx")
    ny = lax.axis_size("gy")
    axes = ("gx", "gy")

    def send(piece, dx, dy):
        return lax.ppermute(piece, axes, neighbour_pairs(dx, dy, nx, ny))

    top = cells[..., :w, :]
    bottom = cells[..., -w:, :]
    left = cells[..., :, :w]
    right = cells[..., :, -w:]
    low_x = send(bottom, 1, 0)
    high_x = send(top, -1, 0)
    low_y = send(right, 0, 1)
    high_y = send(left, 0, -1)
    c_ll = send(cells[..., -w:, -w:], 1, 1)
    c_lh = send(cells[..., -w:, :w], 1, -1)
    c_hl = send(cells[..., :w, -w:], -1, 1)
    c_hh = send(cells[..., :w, :w], -1, -1)
    rows_lo = jnp.concatenate([c_ll, low_x, c_lh], axis=-1)
    rows_mid = jnp.concatenate([low_y, cells, high_y], axis=-1)
    rows_hi = jnp.concatenate([c_hl, high_x, c_hh], axis=-1)
    return jnp.concatenate([rows_lo, rows_mid, rows_hi], axis=-2)


def pull_back(ext, width_x, width_y):
    pieces = []
    for slot in range(19):
        step_x, step_y, step_z = VELOCITIES[slot]
        piece = ext[slot, :, 1 + step_x : 1 + step_x + width_x, 1 + step_y : 1 + step_y + width_y]
        pieces.append(jnp.roll(piece, -step_z, axis=0))
    return jnp.stack(pieces)


def cell_math(g, f, b, lev):
    rho = f[0]
    for i in range(1, 19):
        rho = rho + f[i]
    mom = []
    for d in range(3):
        acc = None
        for i in range(19):
            c = VELOCITIES[i][d]
            if c == 0:
                continue
            acc = (f[i] if acc is None else acc + f[i]) if c > 0 else (-f[i] if acc is None else acc - f[i])
        mom.append(acc)
    u = [m / rho for m in mom]
    usq = u[0] * u[0] + u[1] * u[1] + u[2] * u[2]
    one_b = 1.0 - b
    q = []
    for j in range(19):
        acc = None
        for l in range(19):
            t = RELAX[j][l] * g[l]
            acc = t if acc is None else acc + t
        q.append(acc)
    tsum = None
    for i in range(19):
        cu = None
        for d in range(3):
            c = VELOCITIES[i][d]
            if c == 0:
                continue
            cu = (u[d] if c > 0 else -u[d]) if cu is None else (cu + u[d] if c > 0 else cu - u[d])
        if cu is None:
            phi = 1.0 - 1.5 * usq
        else:
            phi = 1.0 + 3.0 * cu + 4.5 * cu * cu - 1.5 * usq
        eq = WEIGHTS[i] * rho * phi
        t = g[i] * (f[OPPOSITE[i]] - f[i]) + q[i] * (f[i] - eq)
        tsum = t if tsum is None else tsum + t
    term = lev * tsum
    k = [one_b * qj for qj in q]
    wk = [WEIGHTS[i] * k[i] for i in range(19)]
    a_sum = wk[0]
    for i in range(1, 19):
        a_sum = a_sum + wk[i]
    bvec = []
    for d in range(3):
        acc = None
        for i in range(19):
            c = VELOCITIES[i][d]
            if c == 0:
                continue
            acc = (wk[i] if acc is None else acc + wk[i]) if c > 0 else (-wk[i] if acc is None else acc - wk[i])
        bvec.append(acc)
    cmat = {}
    for d in range(3):
        for e in range(d, 3):
            acc = None
            for i in range(19):
                c = VELOCITIES[i][d] * VELOCITIES[i][e]
                if c == 0:
                    continue
                acc = (wk[i] if acc is None else acc + wk[i]) if c > 0 else (-wk[i] if acc is None else acc - wk[i])
            cmat[(d, e)] = acc
            cmat[(e, d)] = acc
    cu_vec = [cmat[(d, 0)] * u[0] + cmat[(d, 1)] * u[1] + cmat[(d, 2)] * u[2] for d in range(3)]
    ucu = u[0] * cu_vec[0] + u[1] * cu_vec[1] + u[2] * cu_vec[2]
    e_val = a_sum - 4.5 * ucu + 1.5 * a_sum * usq
    gvec = [3.0 * bvec[d] + 9.0 * cu_vec[d] - 3.0 * a_sum * u[d] for d in range(3)]
    result = []
    for j in range(19):
        r = one_b * g[j] - k[j] + e_val + b * g[OPPOSITE[j]]
        for d in range(3):
            c = VELOCITIES[j][d]
            if c > 0:
                r = r + gvec[d]
            elif c < 0:
                r = r - gvec[d]
        result.append(r)
    return result, term


def step_kernel(section, rows, g_ref, f_ref, b_ref, l_ref, res_ref, term_ref):
    planes, width_x, _ = b_ref.shape
    chunks = width_x // rows

    def body(idx, acc):
        z = idx // chunks
        x0 = pl.multiple_of((idx % chunks) * rows, rows)
        xs = pl.ds(x0, rows)
        g = [g_ref[i, z, xs, :] for i in range(19)]
        f = [f_ref[section, i, z, xs, :].astype(jnp.float32) for i in range(19)]
        b = b_ref[z, xs, :]
        lev = l_ref[z, xs, :]
        result, term = cell_math(g, f, b, lev)
        for j in range(19):
            res_ref[j, z, xs, :] = result[j]
        term_ref[xs, :] = term_ref[xs, :] + term
        return acc

    term_ref[...] = jnp.zeros_like(term_ref)
    lax.fori_loop(0, planes * chunks, body, 0)


def adjoint_step(section, pulled, forward_pops, blocking, lever):
    _, planes, width_x, width_y = pulled.shape
    rows = 8 if width_x % 8 == 0 else width_x
    vmem = pl.BlockSpec(memory_space=pltpu.VMEM)
    return pl.pallas_call(
        functools.partial(step_kernel, section, rows),
        out_shape=(
            jax.ShapeDtypeStruct(pulled.shape, jnp.float32),
            jax.ShapeDtypeStruct((width_x, width_y), jnp.float32),
        ),
        in_specs=[vmem] * 4,
        out_specs=(vmem, vmem),
    )(pulled, forward_pops, blocking, lever)


def helmholtz(raw, w):
    scale_den = 1.0 + 4.0 * FILTER_WEIGHT
    width_x, width_y = raw.shape
    nx = lax.axis_size("gx")
    ny = lax.axis_size("gy")
    gxi = lax.axis_index("gx")
    gyi = lax.axis_index("gy")
    raw_ext = halo(raw, w)
    xs = gxi * width_x - w + lax.broadcasted_iota(jnp.int32, raw_ext.shape, 0)
    ys = gyi * width_y - w + lax.broadcasted_iota(jnp.int32, raw_ext.shape, 1)
    valid = (xs >= 0) & (xs < nx * width_x) & (ys >= 0) & (ys < ny * width_y)
    smooth = raw_ext
    for sweep in range(SWEEPS):
        framed = jnp.pad(smooth, 1)
        beside_all = framed[:-2, 1:-1] + framed[2:, 1:-1] + framed[1:-1, :-2] + framed[1:-1, 2:]
        smooth = jnp.where(valid, (raw_ext + FILTER_WEIGHT * beside_all) / scale_den, 0.0)
    return smooth[w:-w, w:-w]


def per_device(adjoint_in, forward_pops, solid_mask, region_label, design):
    planes, width_x, width_y = solid_mask.shape
    inside = region_label > 0
    blocking = jnp.where(
        solid_mask == 1, 1.0, jnp.where(inside[None], BLOCK_LIMIT * design[None], 0.0)
    ).astype(jnp.float32)
    lever = jnp.where((solid_mask == 0) & inside[None], BLOCK_LIMIT, 0.0).astype(jnp.float32)
    adjoint = adjoint_in
    raw = jnp.zeros((width_x, width_y), jnp.float32)
    for section in (1, 0):
        pulled = pull_back(halo(adjoint, 1), width_x, width_y)
        adjoint, term = adjoint_step(section, pulled, forward_pops, blocking, lever)
        raw = raw + term
    raw = SENSE_SCALE * raw
    smooth = helmholtz(raw, SWEEPS)
    region_one = (region_label == 1).astype(jnp.float32)
    region_two = (region_label == 2).astype(jnp.float32)
    stats = jnp.stack(
        [
            jnp.sum(smooth * region_one),
            jnp.sum(smooth * region_two),
            jnp.sum(region_one),
            jnp.sum(region_two),
        ]
    )
    stats = lax.psum(stats, ("gx", "gy"))
    means = stats[:2] / jnp.maximum(stats[2:], 1.0)
    sensitivity = region_one * (smooth - means[0]) + region_two * (smooth - means[1])
    return (adjoint, sensitivity)


def solution(mesh):
    in_specs = (
        P(None, None, "gx", "gy"),
        P(None, None, None, "gx", "gy"),
        P(None, "gx", "gy"),
        P("gx", "gy"),
        P("gx", "gy"),
    )
    out_specs = (P(None, None, "gx", "gy"), P("gx", "gy"))
    return jax.shard_map(
        per_device, mesh=mesh, in_specs=in_specs, out_specs=out_specs, check_vma=False
    )
```

time: 315 us -> 233 us (0.74)
  local copies, waits for them, and re-layouts: 58.2 us -> 14.6 us
  matrix products: 21.7 us -> 0 us
  waiting for transfers between devices: 22.8 us -> 2.59 us
  other arithmetic: 28.2 us -> 9.28 us
  starting transfers between devices: 69.4 us -> 79.2 us
  Pallas kernels: 0 us -> 7.22 us
  blocking collectives: 111 us -> 117 us
    dot_general x12 -> x0, matrix products: 21.7 us -> none  [the longest x4 9.56 us: collide(): jnp.dot(relax_matrix, popul - equilib, precision=lax.Precision.HIGHEST)]
    ppermute x24, waiting for transfers between devices: 22.8 us -> 2.59 us  [send(): return lax.ppermute(piece, axes, neighbour_pairs(dx, dy, nx, ny))]
    ppermute x8 -> x4, local copies, waits for them, and re-layouts: 16.6 us -> 2.84 us  [send(): return lax.ppermute(piece, axes, neighbour_pairs(dx, dy, nx, ny))]
    concatenate x24 -> x1, other arithmetic: 11.6 us -> 0.08 us  [halo(): return jnp.concatenate([rows_lo, rows_mid, rows_hi], axis=-2)]
    ppermute x24, starting transfers between devices: 69.4 us -> 79.2 us  [send(): return lax.ppermute(piece, axes, neighbour_pairs(dx, dy, nx, ny))]
    concatenate x3 -> x0, local copies, waits for them, and re-layouts: 9.7 us -> none  [extended(): jnp.concatenate([lax.ppermute(tail, axis, [(i, (i + 1) % count) for i in...]
    unnamed x45 -> x20, local copies, waits for them, and re-layouts: 12.3 us -> 3.41 us
    pallas_call x0 -> x2, Pallas kernels: none -> 7.22 us  [adjoint_step(): pl.pallas_call(functools.partial(step_kernel, section, rows), out_shape=(...]
  transfers between devices with their start and end apart: 24 -> 24, of which waited for: 8 -> 3; matrix products, arithmetic and copies ran while one was open for 14% -> 3% of each run, Pallas kernels for 0% -> 0%
where the time goes in v1:
time: 233 us; the launch traced here: 231 us
  blocking collectives  117 us (50%)
  starting transfers between devices  79.2 us (34%)
  local copies, waits for them, and re-layouts  14.6 us (6%)
  other arithmetic  9.28 us (4%)
  Pallas kernels  7.22 us (3%)
  waiting for transfers between devices  2.59 us (1%)
    psum x1, blocking collectives, per_device(): stats = lax.psum(stats, ('gx', 'gy'))  117 us
    ppermute x24, starting transfers between devices, send(): return lax.ppermute(piece, axes, neighbour_pairs(dx, dy, nx, ny))  79.2 us
    pallas_call x2, Pallas kernels, adjoint_step(): pl.pallas_call(functools.partial(step_kernel, section, rows), out_shape=(...  7.22 us
  transfers between devices with their start and end apart: 24, of which 3 were waited for; matrix products, arithmetic and copies ran while one was open for 3% of the time, Pallas kernels for 0%

profile of v1, /device:TPU:1, one launch (start us, length us, event | category | flops | bytes accessed | tf_op | source)
XLA Modules:
  0.0 231.4 jit_solution(9657144804102730790)
XLA Ops:
  0.6 1.6 fusion.43
  2.2 1.3 collective-permute-start.4
  3.5 1.6 fusion.45
  5.2 0.5 copy.20
  5.7 1.3 collective-permute-start.1
  7.1 8.7 %collective-permute-start.3 = (f32[19,4,1,128]{3,2,1,0:T(1,128)S(1)}, f32[19,4,1,128]{3,2,1,0:T(1,128)S(1)}, u32[]{:S(2)}, u32[]{:S(2)}) collective-permute-start(f32[19,4,1,128]{3,2,1,0:T(1,128)S(1)} %get-tuple-element.80), channel_id=1, source_target_pairs={{32,0},{33,1},{34,2},{35,3},{36,4},{37,5},{38,6},{39,7},{40,8},{41... | collective-permute-start | bytes 116744 | tf_op jit(solution)/shard_map/ppermute | solution.py:109
  15.9 3.5 %collective-permute-start.2 = (f32[19,4,1,1]{3,2,1,0:T(1,128)S(1)}, f32[19,4,1,1]{3,2,1,0:T(1,128)S(1)}, u32[]{:S(2)}, u32[]{:S(2)}) collective-permute-start(f32[19,4,1,1]{3,2,1,0:T(1,128)S(1)} %get-tuple-element.78), channel_id=1, source_target_pairs={{32,1},{33,2},{34,3},{35,4},{36,5},{37,6},{38,7},{39,8},{40,9},{41... | collective-permute-start | bytes 920 | tf_op jit(solution)/shard_map/ppermute | solution.py:109
  19.9 2.9 %collective-permute-start = (f32[19,4,16,1]{0,2,3,1:T(8,128)S(1)}, f32[19,4,16,1]{0,2,3,1:T(8,128)S(1)}, u32[]{:S(2)}, u32[]{:S(2)}) collective-permute-start(f32[19,4,16,1]{0,2,3,1:T(8,128)S(1)} %copy.19), channel_id=1, source_target_pairs={{0,1},{1,2},{2,3},{3,4},{4,5},{5,6},{6,7},{7,8},{8,9},{9,10},{10,1... | collective-permute-start | bytes 14600 | tf_op jit(solution)/shard_map/ppermute | solution.py:109
  22.9 0.7 copy-done.7
  23.6 0.6 and_select_fusion
  24.2 1.3 collective-permute-start.7
  25.5 0.7 copy.10
  26.3 5.1 %collective-permute-start.6 = (f32[19,4,1,128]{3,2,1,0:T(1,128)S(1)}, f32[19,4,1,128]{3,2,1,0:T(1,128)S(1)}, u32[]{:S(2)}, u32[]{:S(2)}) collective-permute-start(f32[19,4,1,128]{3,2,1,0:T(1,128)S(1)} %get-tuple-element.79), channel_id=1, source_target_pairs={{0,32},{1,33},{2,34},{3,35},{4,36},{5,37},{6,38},{7,39},{8,40},{9,... | collective-permute-start | bytes 116744 | tf_op jit(solution)/shard_map/ppermute | solution.py:109
  31.4 0.7 copy.9
  32.1 4.0 %collective-permute-start.5 = (f32[19,4,1,1]{3,2,1,0:T(1,128)S(1)}, f32[19,4,1,1]{3,2,1,0:T(1,128)S(1)}, u32[]{:S(2)}, u32[]{:S(2)}) collective-permute-start(f32[19,4,1,1]{3,2,1,0:T(1,128)S(1)} %get-tuple-element.75), channel_id=1, source_target_pairs={{0,33},{1,34},{2,35},{3,36},{4,37},{5,38},{6,39},{7,40},{8,41},{9,... | collective-permute-start | bytes 920 | tf_op jit(solution)/shard_map/ppermute | solution.py:109
  36.2 0.9 collective-permute-done.5
  38.3 0.8 copy-done.2
  39.2 3.6 %shard_map.68 = (f32[19,4,16,128]{3,2,1,0:T(8,128)}, f32[16,128]{1,0:T(8,128)}) custom-call(f32[19,4,16,128]{3,2,1,0:T(8,128)} %copy-done.2, bf16[2,19,4,16,128]{4,3,2,1,0:T(8,128)(2,1)} %f_ref.3, f32[4,16,128]{2,1,0:T(8,128)} %get-tuple-element.84.b_ref, f32[4,16,128]{2,1,0:T(8,128)} %get-tuple-element.83.l_ref), custom_call_target="tpu_custom_call" | custom-call | tf_op jit(solution)/shard_map/pallas_call | solution.py:245
  42.8 1.6 fusion.40
  44.3 1.6 fusion.42
  46.5 1.3 collective-permute-start.9
  47.8 3.1 %collective-permute-start.11 = (f32[19,4,1,128]{3,2,1,0:T(1,128)S(1)}, f32[19,4,1,128]{3,2,1,0:T(1,128)S(1)}, u32[]{:S(2)}, u32[]{:S(2)}) collective-permute-start(f32[19,4,1,128]{3,2,1,0:T(1,128)S(1)} %get-tuple-element.68), channel_id=1, source_target_pairs={{32,0},{33,1},{34,2},{35,3},{36,4},{37,5},{38,6},{39,7},{40,8},{41... | collective-permute-start | bytes 116744 | tf_op jit(solution)/shard_map/ppermute | solution.py:109
  51.5 4.3 %collective-permute-start.8 = (f32[19,4,16,1]{0,2,3,1:T(8,128)S(1)}, f32[19,4,16,1]{0,2,3,1:T(8,128)S(1)}, u32[]{:S(2)}, u32[]{:S(2)}) collective-permute-start(f32[19,4,16,1]{0,2,3,1:T(8,128)S(1)} %copy.13), channel_id=1, source_target_pairs={{0,1},{1,2},{2,3},{3,4},{4,5},{5,6},{6,7},{7,8},{8,9},{9,10},{10,1... | collective-permute-start | bytes 14600 | tf_op jit(solution)/shard_map/ppermute | solution.py:109
  55.8 1.3 collective-permute-start.12
  57.1 1.5 collective-permute-start.10
  58.6 1.3 collective-permute-start.15
  59.9 0.7 copy.16
  60.6 5.5 %collective-permute-start.14 = (f32[19,4,1,128]{3,2,1,0:T(1,128)S(1)}, f32[19,4,1,128]{3,2,1,0:T(1,128)S(1)}, u32[]{:S(2)}, u32[]{:S(2)}) collective-permute-start(f32[19,4,1,128]{3,2,1,0:T(1,128)S(1)} %get-tuple-element.67), channel_id=1, source_target_pairs={{0,32},{1,33},{2,34},{3,35},{4,36},{5,37},{6,38},{7,39},{8,40},{9,... | collective-permute-start | bytes 116744 | tf_op jit(solution)/shard_map/ppermute | solution.py:109
  66.2 0.7 copy.15
  66.9 5.8 %collective-permute-start.13 = (f32[19,4,1,1]{3,2,1,0:T(1,128)S(1)}, f32[19,4,1,1]{3,2,1,0:T(1,128)S(1)}, u32[]{:S(2)}, u32[]{:S(2)}) collective-permute-start(f32[19,4,1,1]{3,2,1,0:T(1,128)S(1)} %get-tuple-element.63), channel_id=1, source_target_pairs={{0,33},{1,34},{2,35},{3,36},{4,37},{5,38},{6,39},{7,40},{8,41},{9,... | collective-permute-start | bytes 920 | tf_op jit(solution)/shard_map/ppermute | solution.py:109
  72.8 0.9 collective-permute-done.13
  75.0 0.8 copy-done.3
  75.8 3.6 %shard_map.69 = (f32[19,4,16,128]{3,2,1,0:T(8,128)}, f32[16,128]{1,0:T(8,128)}) custom-call(f32[19,4,16,128]{3,2,1,0:T(8,128)} %copy-done.3, bf16[2,19,4,16,128]{4,3,2,1,0:T(8,128)(2,1)} %f_ref.3, f32[4,16,128]{2,1,0:T(8,128)} %get-tuple-element.84.b_ref, f32[4,16,128]{2,1,0:T(8,128)} %get-tuple-element.83.l_ref), custom_call_target="tpu_custom_call" | custom-call | tf_op jit(solution)/shard_map/pallas_call | solution.py:245
  79.4 0.7 add_multiply_fusion
  80.3 1.3 collective-permute-start.23
  81.6 1.9 collective-permute-start.22
  83.5 3.0 %collective-permute-start.21 = (f32[4,4]{1,0:T(4,128)S(1)}, f32[4,4]{1,0:T(4,128)S(1)}, u32[]{:S(2)}, u32[]{:S(2)}) collective-permute-start(f32[4,4]{1,0:T(4,128)S(1)} %get-tuple-element.90), channel_id=1, source_target_pairs={{32,1},{33,2},{34,3},{35,4},{36,5},{37,6},{38,7},{39,8},{40,9},{41... | collective-permute-start | bytes 200 | tf_op jit(solution)/shard_map/ppermute | solution.py:109
  86.5 1.3 collective-permute-start.20
  87.8 5.1 %collective-permute-start.19 = (f32[16,4]{1,0:T(8,128)S(1)}, f32[16,4]{1,0:T(8,128)S(1)}, u32[]{:S(2)}, u32[]{:S(2)}) collective-permute-start(f32[16,4]{1,0:T(8,128)S(1)} %get-tuple-element.94), channel_id=1, source_target_pairs={{0,1},{1,2},{2,3},{3,4},{4,5},{5,6},{6,7},{7,8},{8,9},{9,10},{10,1... | collective-permute-start | bytes 776 | tf_op jit(solution)/shard_map/ppermute | solution.py:109
  92.9 1.3 collective-permute-start.18
  94.2 4.9 %collective-permute-start.17 = (f32[4,128]{1,0:T(4,128)S(1)}, f32[4,128]{1,0:T(4,128)S(1)}, u32[]{:S(2)}, u32[]{:S(2)}) collective-permute-start(f32[4,128]{1,0:T(4,128)S(1)} %get-tuple-element.92), channel_id=1, source_target_pairs={{0,32},{1,33},{2,34},{3,35},{4,36},{5,37},{6,38},{7,39},{8,40},{9,... | collective-permute-start | bytes 6152 | tf_op jit(solution)/shard_map/ppermute | solution.py:109
  99.1 8.2 %collective-permute-start.16 = (f32[4,4]{1,0:T(4,128)S(1)}, f32[4,4]{1,0:T(4,128)S(1)}, u32[]{:S(2)}, u32[]{:S(2)}) collective-permute-start(f32[4,4]{1,0:T(4,128)S(1)} %get-tuple-element.88), channel_id=1, source_target_pairs={{0,33},{1,34},{2,35},{3,36},{4,37},{5,38},{6,39},{7,40},{8,41},{9,... | collective-permute-start | bytes 200 | tf_op jit(solution)/shard_map/ppermute | solution.py:109
  107.4 0.6 collective-permute-done.16
  108.6 0.7 select_reduce_fusion.1
  109.3 2.5 %pad_maximum_fusion.20 = f32[4]{0:T(128)S(1)} fusion(f32[1]{0:T(128)} %bitcast.63, f32[1]{0:T(128)} %bitcast.62, f32[1]{0:T(128)} %bitcast.61, f32[1]{0:T(128)} %bitcast.60), kind=kLoop, calls=%fused_computation.184 | loop fusion | flops 12 | bytes 32 | tf_op jit(solution)/shard_map/stack | solution.py:292
  111.8 117.0 %psum.7 = f32[4]{0:T(128)S(1)} all-reduce(f32[4]{0:T(128)S(1)} %pad_maximum_fusion.20), channel_id=1, replica_groups=mesh['gx'=16,'gy'=32] {'gx','gy'}, use_global_device_ids=true, to_apply=%region_4.5 | all-reduce | flops 4 | bytes 32 | tf_op jit(solution)/shard_map/psum | solution.py:300
  229.0 0.6 fusion.49
  229.6 1.8 select_add_fusion
  (98 shorter events, 4.8 us)
Async XLA Ops:
  2.2 29.8 %collective-permute-start.4 = (f32[19,4,1,1]{3,2,1,0:T(1,128)S(1)}, f32[19,4,1,1]{3,2,1,0:T(1,128)S(1)}, u32[]{:S(2)}, u32[]{:S(2)}) collective-permute-start(f32[19,4,1,1]{3,2,1,0:T(1,128)S(1)} %get-tuple-element.77), channel_id=1, source_target_pairs={{33,0},{34,1},{35,2},{36,3},{37,4},{38,5},{39,6},{40,7},{41,8},{42... | collective-permute-start | bytes 920 | tf_op jit(solution)/shard_map/ppermute | solution.py:109
  5.2 1.8 copy-start
  5.7 18.5 %collective-permute-start.1 = (f32[19,4,16,1]{0,2,3,1:T(8,128)S(1)}, f32[19,4,16,1]{0,2,3,1:T(8,128)S(1)}, u32[]{:S(2)}, u32[]{:S(2)}) collective-permute-start(f32[19,4,16,1]{0,2,3,1:T(8,128)S(1)} %copy.20), channel_id=1, source_target_pairs={{1,0},{2,1},{3,2},{4,3},{5,4},{6,5},{7,6},{8,7},{9,8},{10,9},{11,1... | collective-permute-start | bytes 14600 | tf_op jit(solution)/shard_map/ppermute | solution.py:109
  7.1 29.0 %collective-permute-start.3 = (f32[19,4,1,128]{3,2,1,0:T(1,128)S(1)}, f32[19,4,1,128]{3,2,1,0:T(1,128)S(1)}, u32[]{:S(2)}, u32[]{:S(2)}) collective-permute-start(f32[19,4,1,128]{3,2,1,0:T(1,128)S(1)} %get-tuple-element.80), channel_id=1, source_target_pairs={{32,0},{33,1},{34,2},{35,3},{36,4},{37,5},{38,6},{39,7},{40,8},{41... | collective-permute-start | bytes 116744 | tf_op jit(solution)/shard_map/ppermute | solution.py:109
  15.9 20.2 %collective-permute-start.2 = (f32[19,4,1,1]{3,2,1,0:T(1,128)S(1)}, f32[19,4,1,1]{3,2,1,0:T(1,128)S(1)}, u32[]{:S(2)}, u32[]{:S(2)}) collective-permute-start(f32[19,4,1,1]{3,2,1,0:T(1,128)S(1)} %get-tuple-element.78), channel_id=1, source_target_pairs={{32,1},{33,2},{34,3},{35,4},{36,5},{37,6},{38,7},{39,8},{40,9},{41... | collective-permute-start | bytes 920 | tf_op jit(solution)/shard_map/ppermute | solution.py:109
  19.9 6.3 %collective-permute-start = (f32[19,4,16,1]{0,2,3,1:T(8,128)S(1)}, f32[19,4,16,1]{0,2,3,1:T(8,128)S(1)}, u32[]{:S(2)}, u32[]{:S(2)}) collective-permute-start(f32[19,4,16,1]{0,2,3,1:T(8,128)S(1)} %copy.19), channel_id=1, source_target_pairs={{0,1},{1,2},{2,3},{3,4},{4,5},{5,6},{6,7},{7,8},{8,9},{9,10},{10,1... | collective-permute-start | bytes 14600 | tf_op jit(solution)/shard_map/ppermute | solution.py:109
  22.8 0.8 copy-start.5
  22.9 0.7 copy-start.7
  22.9 0.7 copy-start.4
  24.2 12.0 %collective-permute-start.7 = (f32[19,4,1,1]{3,2,1,0:T(1,128)S(1)}, f32[19,4,1,1]{3,2,1,0:T(1,128)S(1)}, u32[]{:S(2)}, u32[]{:S(2)}) collective-permute-start(f32[19,4,1,1]{3,2,1,0:T(1,128)S(1)} %get-tuple-element.76), channel_id=1, source_target_pairs={{1,32},{2,33},{3,34},{4,35},{5,36},{6,37},{7,38},{8,39},{9,40},{10... | collective-permute-start | bytes 920 | tf_op jit(solution)/shard_map/ppermute | solution.py:109
  26.3 10.9 %collective-permute-start.6 = (f32[19,4,1,128]{3,2,1,0:T(1,128)S(1)}, f32[19,4,1,128]{3,2,1,0:T(1,128)S(1)}, u32[]{:S(2)}, u32[]{:S(2)}) collective-permute-start(f32[19,4,1,128]{3,2,1,0:T(1,128)S(1)} %get-tuple-element.79), channel_id=1, source_target_pairs={{0,32},{1,33},{2,34},{3,35},{4,36},{5,37},{6,38},{7,39},{8,40},{9,... | collective-permute-start | bytes 116744 | tf_op jit(solution)/shard_map/ppermute | solution.py:109
  32.1 5.1 %collective-permute-start.5 = (f32[19,4,1,1]{3,2,1,0:T(1,128)S(1)}, f32[19,4,1,1]{3,2,1,0:T(1,128)S(1)}, u32[]{:S(2)}, u32[]{:S(2)}) collective-permute-start(f32[19,4,1,1]{3,2,1,0:T(1,128)S(1)} %get-tuple-element.75), channel_id=1, source_target_pairs={{0,33},{1,34},{2,35},{3,36},{4,37},{5,38},{6,39},{7,40},{8,41},{9,... | collective-permute-start | bytes 920 | tf_op jit(solution)/shard_map/ppermute | solution.py:109
  38.3 0.8 copy-start.2
  44.3 1.6 copy-start.1
  46.5 12.0 %collective-permute-start.9 = (f32[19,4,16,1]{0,2,3,1:T(8,128)S(1)}, f32[19,4,16,1]{0,2,3,1:T(8,128)S(1)}, u32[]{:S(2)}, u32[]{:S(2)}) collective-permute-start(f32[19,4,16,1]{0,2,3,1:T(8,128)S(1)} %copy.14), channel_id=1, source_target_pairs={{1,0},{2,1},{3,2},{4,3},{5,4},{6,5},{7,6},{8,7},{9,8},{10,9},{11,1... | collective-permute-start | bytes 14600 | tf_op jit(solution)/shard_map/ppermute | solution.py:109
  47.8 24.9 %collective-permute-start.11 = (f32[19,4,1,128]{3,2,1,0:T(1,128)S(1)}, f32[19,4,1,128]{3,2,1,0:T(1,128)S(1)}, u32[]{:S(2)}, u32[]{:S(2)}) collective-permute-start(f32[19,4,1,128]{3,2,1,0:T(1,128)S(1)} %get-tuple-element.68), channel_id=1, source_target_pairs={{32,0},{33,1},{34,2},{35,3},{36,4},{37,5},{38,6},{39,7},{40,8},{41... | collective-permute-start | bytes 116744 | tf_op jit(solution)/shard_map/ppermute | solution.py:109
  51.5 9.1 %collective-permute-start.8 = (f32[19,4,16,1]{0,2,3,1:T(8,128)S(1)}, f32[19,4,16,1]{0,2,3,1:T(8,128)S(1)}, u32[]{:S(2)}, u32[]{:S(2)}) collective-permute-start(f32[19,4,16,1]{0,2,3,1:T(8,128)S(1)} %copy.13), channel_id=1, source_target_pairs={{0,1},{1,2},{2,3},{3,4},{4,5},{5,6},{6,7},{7,8},{8,9},{9,10},{10,1... | collective-permute-start | bytes 14600 | tf_op jit(solution)/shard_map/ppermute | solution.py:109
  55.8 11.1 %collective-permute-start.12 = (f32[19,4,1,1]{3,2,1,0:T(1,128)S(1)}, f32[19,4,1,1]{3,2,1,0:T(1,128)S(1)}, u32[]{:S(2)}, u32[]{:S(2)}) collective-permute-start(f32[19,4,1,1]{3,2,1,0:T(1,128)S(1)} %get-tuple-element.65), channel_id=1, source_target_pairs={{33,0},{34,1},{35,2},{36,3},{37,4},{38,5},{39,6},{40,7},{41,8},{42... | collective-permute-start | bytes 920 | tf_op jit(solution)/shard_map/ppermute | solution.py:109
  57.1 15.6 %collective-permute-start.10 = (f32[19,4,1,1]{3,2,1,0:T(1,128)S(1)}, f32[19,4,1,1]{3,2,1,0:T(1,128)S(1)}, u32[]{:S(2)}, u32[]{:S(2)}) collective-permute-start(f32[19,4,1,1]{3,2,1,0:T(1,128)S(1)} %get-tuple-element.66), channel_id=1, source_target_pairs={{32,1},{33,2},{34,3},{35,4},{36,5},{37,6},{38,7},{39,8},{40,9},{41... | collective-permute-start | bytes 920 | tf_op jit(solution)/shard_map/ppermute | solution.py:109
  58.6 14.2 %collective-permute-start.15 = (f32[19,4,1,1]{3,2,1,0:T(1,128)S(1)}, f32[19,4,1,1]{3,2,1,0:T(1,128)S(1)}, u32[]{:S(2)}, u32[]{:S(2)}) collective-permute-start(f32[19,4,1,1]{3,2,1,0:T(1,128)S(1)} %get-tuple-element.64), channel_id=1, source_target_pairs={{1,32},{2,33},{3,34},{4,35},{5,36},{6,37},{7,38},{8,39},{9,40},{10... | collective-permute-start | bytes 920 | tf_op jit(solution)/shard_map/ppermute | solution.py:109
  60.6 13.2 %collective-permute-start.14 = (f32[19,4,1,128]{3,2,1,0:T(1,128)S(1)}, f32[19,4,1,128]{3,2,1,0:T(1,128)S(1)}, u32[]{:S(2)}, u32[]{:S(2)}) collective-permute-start(f32[19,4,1,128]{3,2,1,0:T(1,128)S(1)} %get-tuple-element.67), channel_id=1, source_target_pairs={{0,32},{1,33},{2,34},{3,35},{4,36},{5,37},{6,38},{7,39},{8,40},{9,... | collective-permute-start | bytes 116744 | tf_op jit(solution)/shard_map/ppermute | solution.py:109
  66.9 6.9 %collective-permute-start.13 = (f32[19,4,1,1]{3,2,1,0:T(1,128)S(1)}, f32[19,4,1,1]{3,2,1,0:T(1,128)S(1)}, u32[]{:S(2)}, u32[]{:S(2)}) collective-permute-start(f32[19,4,1,1]{3,2,1,0:T(1,128)S(1)} %get-tuple-element.63), channel_id=1, source_target_pairs={{0,33},{1,34},{2,35},{3,36},{4,37},{5,38},{6,39},{7,40},{8,41},{9,... | collective-permute-start | bytes 920 | tf_op jit(solution)/shard_map/ppermute | solution.py:109
  75.0 0.8 copy-start.3
  75.8 3.6 %copy-start.6 = (f32[16,128]{1,0:T(8,128)S(1)}, f32[16,128]{1,0:T(8,128)}, u32[]{:S(2)}) copy-start(f32[16,128]{1,0:T(8,128)} %get-tuple-element.8) | copy-start | bytes 24580
  80.3 12.6 %collective-permute-start.23 = (f32[4,4]{1,0:T(4,128)S(1)}, f32[4,4]{1,0:T(4,128)S(1)}, u32[]{:S(2)}, u32[]{:S(2)}) collective-permute-start(f32[4,4]{1,0:T(4,128)S(1)} %get-tuple-element.89), channel_id=1, source_target_pairs={{33,0},{34,1},{35,2},{36,3},{37,4},{38,5},{39,6},{40,7},{41,8},{42... | collective-permute-start | bytes 200 | tf_op jit(solution)/shard_map/ppermute | solution.py:109
  81.6 26.5 %collective-permute-start.22 = (f32[4,128]{1,0:T(4,128)S(1)}, f32[4,128]{1,0:T(4,128)S(1)}, u32[]{:S(2)}, u32[]{:S(2)}) collective-permute-start(f32[4,128]{1,0:T(4,128)S(1)} %get-tuple-element.93), channel_id=1, source_target_pairs={{32,0},{33,1},{34,2},{35,3},{36,4},{37,5},{38,6},{39,7},{40,8},{41... | collective-permute-start | bytes 6152 | tf_op jit(solution)/shard_map/ppermute | solution.py:109
  83.5 10.7 %collective-permute-start.21 = (f32[4,4]{1,0:T(4,128)S(1)}, f32[4,4]{1,0:T(4,128)S(1)}, u32[]{:S(2)}, u32[]{:S(2)}) collective-permute-start(f32[4,4]{1,0:T(4,128)S(1)} %get-tuple-element.90), channel_id=1, source_target_pairs={{32,1},{33,2},{34,3},{35,4},{36,5},{37,6},{38,7},{39,8},{40,9},{41... | collective-permute-start | bytes 200 | tf_op jit(solution)/shard_map/ppermute | solution.py:109
  86.5 21.6 %collective-permute-start.20 = (f32[16,4]{1,0:T(8,128)S(1)}, f32[16,4]{1,0:T(8,128)S(1)}, u32[]{:S(2)}, u32[]{:S(2)}) collective-permute-start(f32[16,4]{1,0:T(8,128)S(1)} %get-tuple-element.95), channel_id=1, source_target_pairs={{1,0},{2,1},{3,2},{4,3},{5,4},{6,5},{7,6},{8,7},{9,8},{10,9},{11,1... | collective-permute-start | bytes 776 | tf_op jit(solution)/shard_map/ppermute | solution.py:109
  87.8 20.3 %collective-permute-start.19 = (f32[16,4]{1,0:T(8,128)S(1)}, f32[16,4]{1,0:T(8,128)S(1)}, u32[]{:S(2)}, u32[]{:S(2)}) collective-permute-start(f32[16,4]{1,0:T(8,128)S(1)} %get-tuple-element.94), channel_id=1, source_target_pairs={{0,1},{1,2},{2,3},{3,4},{4,5},{5,6},{6,7},{7,8},{8,9},{9,10},{10,1... | collective-permute-start | bytes 776 | tf_op jit(solution)/shard_map/ppermute | solution.py:109
  92.9 6.2 %collective-permute-start.18 = (f32[4,4]{1,0:T(4,128)S(1)}, f32[4,4]{1,0:T(4,128)S(1)}, u32[]{:S(2)}, u32[]{:S(2)}) collective-permute-start(f32[4,4]{1,0:T(4,128)S(1)} %get-tuple-element.91), channel_id=1, source_target_pairs={{1,32},{2,33},{3,34},{4,35},{5,36},{6,37},{7,38},{8,39},{9,40},{10... | collective-permute-start | bytes 200 | tf_op jit(solution)/shard_map/ppermute | solution.py:109
  94.2 13.9 %collective-permute-start.17 = (f32[4,128]{1,0:T(4,128)S(1)}, f32[4,128]{1,0:T(4,128)S(1)}, u32[]{:S(2)}, u32[]{:S(2)}) collective-permute-start(f32[4,128]{1,0:T(4,128)S(1)} %get-tuple-element.92), channel_id=1, source_target_pairs={{0,32},{1,33},{2,34},{3,35},{4,36},{5,37},{6,38},{7,39},{8,40},{9,... | collective-permute-start | bytes 6152 | tf_op jit(solution)/shard_map/ppermute | solution.py:109
  99.1 9.0 %collective-permute-start.16 = (f32[4,4]{1,0:T(4,128)S(1)}, f32[4,4]{1,0:T(4,128)S(1)}, u32[]{:S(2)}, u32[]{:S(2)}) collective-permute-start(f32[4,4]{1,0:T(4,128)S(1)} %get-tuple-element.88), channel_id=1, source_target_pairs={{0,33},{1,34},{2,35},{3,36},{4,37},{5,38},{6,39},{7,40},{8,41},{9,... | collective-permute-start | bytes 200 | tf_op jit(solution)/shard_map/ppermute | solution.py:109

commit v2 on v1

--- a/solution.py
+++ b/solution.py
@@ -90,40 +90,27 @@
 RELAX = moment_table()
 
 
-def neighbour_pairs(dx, dy, nx, ny):
-    pairs = []
-    for i in range(nx):
-        for j in range(ny):
-            ti, tj = i + dx, j + dy
-            if 0 <= ti < nx and 0 <= tj < ny:
-                pairs.append((i * ny + j, ti * ny + tj))
-    return pairs
-
-
 def halo(cells, w):
+    for axis, dim in (("gx", -2), ("gy", -1)):
+        count = lax.axis_size(axis)
+        size = cells.shape[dim]
+        head = lax.slice_in_dim(cells, 0, w, axis=cells.ndim + dim)
+        tail = lax.slice_in_dim(cells, size - w, size, axis=cells.ndim + dim)
+        low = lax.ppermute(tail, axis, [(i, i + 1) for i in range(count - 1)])
+        high = lax.ppermute(head, axis, [(i + 1, i) for i in range(count - 1)])
+        cells = jnp.concatenate([low, cells, high], axis=dim)
+    return cells
+
+
+def global_sum(values):
     nx = lax.axis_size("gx")
     ny = lax.axis_size("gy")
-    axes = ("gx", "gy")
-
-    def send(piece, dx, dy):
-        return lax.ppermute(piece, axes, neighbour_pairs(dx, dy, nx, ny))
-
-    top = cells[..., :w, :]
-    bottom = cells[..., -w:, :]
-    left = cells[..., :, :w]
-    right = cells[..., :, -w:]
-    low_x = send(bottom, 1, 0)
-    high_x = send(top, -1, 0)
-    low_y = send(right, 0, 1)
-    high_y = send(left, 0, -1)
-    c_ll = send(cells[..., -w:, -w:], 1, 1)
-    c_lh = send(cells[..., -w:, :w], 1, -1)
-    c_hl = send(cells[..., :w, -w:], -1, 1)
-    c_hh = send(cells[..., :w, :w], -1, -1)
-    rows_lo = jnp.concatenate([c_ll, low_x, c_lh], axis=-1)
-    rows_mid = jnp.concatenate([low_y, cells, high_y], axis=-1)
-    rows_hi = jnp.concatenate([c_hl, high_x, c_hh], axis=-1)
-    return jnp.concatenate([rows_lo, rows_mid, rows_hi], axis=-2)
+    total = nx * ny
+    bits = total.bit_length() - 1
+    assert 1 << bits == total
+    for k in range(bits):
+        values = values + lax.ppermute(values, ("gx", "gy"), [(i, i ^ (1 << k)) for i in range(total)])
+    return values
 
 
 def pull_back(ext, width_x, width_y):
@@ -297,7 +284,7 @@
             jnp.sum(region_two),
         ]
     )
-    stats = lax.psum(stats, ("gx", "gy"))
+    stats = global_sum(stats)
     means = stats[:2] / jnp.maximum(stats[2:], 1.0)
     sensitivity = region_one * (smooth - means[0]) + region_two * (smooth - means[1])
     return (adjoint, sensitivity)

time: 233 us -> 162 us (0.70)
  the two profiles are of different devices: /device:TPU:1 before, /device:TPU:38 now
where the time goes in v2:
time: 162 us; the launch traced here: 161 us
  starting transfers between devices  63.7 us (39%)
  waiting for transfers between devices  53.3 us (33%)
  local copies, waits for them, and re-layouts  20.7 us (13%)
  other arithmetic  14.4 us (9%)
  Pallas kernels  7.22 us (4%)
    ppermute x9, waiting for transfers between devices, global_sum(): lax.ppermute(values, ('gx', 'gy'), [(i, i ^ 1 << k) for i in range(total)])  38.9 us
    ppermute x6, starting transfers between devices, halo(): high = lax.ppermute(head, axis, [(i + 1, i) for i in range(count - 1)])  30.9 us
    ppermute x9, starting transfers between devices, global_sum(): lax.ppermute(values, ('gx', 'gy'), [(i, i ^ 1 << k) for i in range(total)])  18.8 us
    ppermute x6, starting transfers between devices, halo(): low = lax.ppermute(tail, axis, [(i, i + 1) for i in range(count - 1)])  14 us
    ppermute x6, waiting for transfers between devices, halo(): low = lax.ppermute(tail, axis, [(i, i + 1) for i in range(count - 1)])  11.8 us
    pallas_call x2, Pallas kernels, adjoint_step(): pl.pallas_call(functools.partial(step_kernel, section, rows), out_shape=(...  7.22 us
    unnamed x22, local copies, waits for them, and re-layouts  6.23 us
    add x9, other arithmetic, global_sum(): values + lax.ppermute(values, ('gx', 'gy'), [(i, i ^ 1 << k) for i in ran...  5.3 us
  transfers between devices with their start and end apart: 21, of which 14 were waited for; matrix products, arithmetic and copies ran while one was open for 6% of the time, Pallas kernels for 0%

profile of v2, /device:TPU:38, one launch (start us, length us, event | category | flops | bytes accessed | tf_op | source)
XLA Modules:
  0.0 160.7 jit_solution(15196741868636597308)
XLA Ops:
  0.6 1.1 fusion.37
  1.8 1.9 %collective-permute-start.1 = (f32[19,4,1,128]{3,2,1,0:T(1,128)S(1)}, f32[19,4,1,128]{3,2,1,0:T(1,128)S(1)}, u32[]{:S(2)}, u32[]{:S(2)}) collective-permute-start(f32[19,4,1,128]{3,2,1,0:T(1,128)S(1)} %get-tuple-element.73), channel_id=1, source_target_pairs={{0,32},{32,64},{64,96},{96,128},{128,160},{160,192},{192,224},{224... | collective-permute-start | bytes 116744 | tf_op jit(solution)/shard_map/ppermute | solution.py:99
  3.7 4.9 %collective-permute-start = (f32[19,4,1,128]{3,2,1,0:T(1,128)S(1)}, f32[19,4,1,128]{3,2,1,0:T(1,128)S(1)}, u32[]{:S(2)}, u32[]{:S(2)}) collective-permute-start(f32[19,4,1,128]{3,2,1,0:T(1,128)S(1)} %get-tuple-element.74), channel_id=1, source_target_pairs={{32,0},{64,32},{96,64},{128,96},{160,128},{192,160},{224,192},{256... | collective-permute-start | bytes 116744 | tf_op jit(solution)/shard_map/ppermute | solution.py:100
  9.3 1.2 constant_dynamic-update-slice_fusion
  11.9 2.2 %dynamic-update-slice.41 = f32[19,4,17,128]{3,2,1,0:T(8,128)S(1)} dynamic-update-slice(f32[19,4,17,128]{3,2,1,0:T(8,128)S(1)} %constant_dynamic-update-slice_fusion, f32[19,4,1,128]{3,2,1,0:T(1,128)S(1)} %collective-permute-done, s32[]{} %constant.65, s32[]{} %constant.65, s32[]{} %constant.81, s32[]{} %constant.65) | dynamic-update-slice | bytes 77828 | tf_op jit(solution)/shard_map/concatenate | solution.py:101
  15.8 11.2 %collective-permute-start.2 = (f32[19,4,18,1]{0,1,3,2:T(4,128)S(1)}, f32[19,4,18,1]{0,1,3,2:T(4,128)S(1)}, u32[]{:S(2)}, u32[]{:S(2)}) collective-permute-start(f32[19,4,18,1]{0,1,3,2:T(4,128)S(1)} %copy.7), channel_id=1, source_target_pairs={{1,0},{2,1},{3,2},{4,3},{5,4},{6,5},{7,6},{8,7},{9,8},{10,9},{11,1... | collective-permute-start | bytes 16424 | tf_op jit(solution)/shard_map/ppermute | solution.py:100
  27.0 1.9 %collective-permute-start.3 = (f32[19,4,18,1]{0,1,3,2:T(4,128)S(1)}, f32[19,4,18,1]{0,1,3,2:T(4,128)S(1)}, u32[]{:S(2)}, u32[]{:S(2)}) collective-permute-start(f32[19,4,18,1]{0,1,3,2:T(4,128)S(1)} %copy.9), channel_id=1, source_target_pairs={{0,1},{1,2},{2,3},{3,4},{4,5},{5,6},{6,7},{7,8},{8,9},{9,10},{10,1... | collective-permute-start | bytes 16424 | tf_op jit(solution)/shard_map/ppermute | solution.py:99
  29.0 6.0 %collective-permute-done.3 = f32[19,4,18,1]{0,1,3,2:T(4,128)S(1)} collective-permute-done((f32[19,4,18,1]{0,1,3,2:T(4,128)S(1)}, f32[19,4,18,1]{0,1,3,2:T(4,128)S(1)}, u32[]{:S(2)}, u32[]{:S(2)}) %collective-permute-start.3) | collective-permute-done | bytes 5504 | tf_op jit(solution)/shard_map/ppermute | solution.py:99
  36.0 1.1 copy.8
  38.8 3.6 %shard_map.68 = (f32[19,4,16,128]{3,2,1,0:T(8,128)}, f32[16,128]{1,0:T(8,128)}) custom-call(f32[19,4,16,128]{3,2,1,0:T(8,128)} %copy-done.2, bf16[2,19,4,16,128]{4,3,2,1,0:T(8,128)(2,1)} %f_ref.3, f32[4,16,128]{2,1,0:T(8,128)} %get-tuple-element.76.b_ref, f32[4,16,128]{2,1,0:T(8,128)} %get-tuple-element.75.l_ref), custom_call_target="tpu_custom_call" | custom-call | tf_op jit(solution)/shard_map/pallas_call | solution.py:232
  42.4 1.1 fusion.36
  44.3 2.0 %collective-permute-start.4 = (f32[19,4,1,128]{3,2,1,0:T(1,128)S(1)}, f32[19,4,1,128]{3,2,1,0:T(1,128)S(1)}, u32[]{:S(2)}, u32[]{:S(2)}) collective-permute-start(f32[19,4,1,128]{3,2,1,0:T(1,128)S(1)} %get-tuple-element.66), channel_id=1, source_target_pairs={{32,0},{64,32},{96,64},{128,96},{160,128},{192,160},{224,192},{256... | collective-permute-start | bytes 116744 | tf_op jit(solution)/shard_map/ppermute | solution.py:100
  46.4 1.1 constant_dynamic-update-slice_fusion.20
  47.5 2.4 %collective-permute-start.5 = (f32[19,4,1,128]{3,2,1,0:T(1,128)S(1)}, f32[19,4,1,128]{3,2,1,0:T(1,128)S(1)}, u32[]{:S(2)}, u32[]{:S(2)}) collective-permute-start(f32[19,4,1,128]{3,2,1,0:T(1,128)S(1)} %get-tuple-element.65), channel_id=1, source_target_pairs={{0,32},{32,64},{64,96},{96,128},{128,160},{160,192},{192,224},{224... | collective-permute-start | bytes 116744 | tf_op jit(solution)/shard_map/ppermute | solution.py:99
  49.9 2.2 %dynamic-update-slice.20 = f32[19,4,17,128]{3,2,1,0:T(8,128)S(1)} dynamic-update-slice(f32[19,4,17,128]{3,2,1,0:T(8,128)S(1)} %constant_dynamic-update-slice_fusion.20, f32[19,4,1,128]{3,2,1,0:T(1,128)S(1)} %collective-permute-done.4, s32[]{} %constant.65, s32[]{} %constant.65, s32[]{} %constant.81, s32[]{} %constant.65) | dynamic-update-slice | bytes 77828 | tf_op jit(solution)/shard_map/concatenate | solution.py:101
  52.1 1.9 %collective-permute-done.5 = f32[19,4,1,128]{3,2,1,0:T(1,128)S(1)} collective-permute-done((f32[19,4,1,128]{3,2,1,0:T(1,128)S(1)}, f32[19,4,1,128]{3,2,1,0:T(1,128)S(1)}, u32[]{:S(2)}, u32[]{:S(2)}) %collective-permute-start.5) | collective-permute-done | bytes 38944 | tf_op jit(solution)/shard_map/ppermute | solution.py:99
  55.7 1.9 %collective-permute-start.6 = (f32[19,4,18,1]{0,1,3,2:T(4,128)S(1)}, f32[19,4,18,1]{0,1,3,2:T(4,128)S(1)}, u32[]{:S(2)}, u32[]{:S(2)}) collective-permute-start(f32[19,4,18,1]{0,1,3,2:T(4,128)S(1)} %copy.11), channel_id=1, source_target_pairs={{1,0},{2,1},{3,2},{4,3},{5,4},{6,5},{7,6},{8,7},{9,8},{10,9},{11,1... | collective-permute-start | bytes 16424 | tf_op jit(solution)/shard_map/ppermute | solution.py:100
  57.6 3.9 %collective-permute-start.7 = (f32[19,4,18,1]{0,1,3,2:T(4,128)S(1)}, f32[19,4,18,1]{0,1,3,2:T(4,128)S(1)}, u32[]{:S(2)}, u32[]{:S(2)}) collective-permute-start(f32[19,4,18,1]{0,1,3,2:T(4,128)S(1)} %copy.13), channel_id=1, source_target_pairs={{0,1},{1,2},{2,3},{3,4},{4,5},{5,6},{6,7},{7,8},{8,9},{9,10},{10,1... | collective-permute-start | bytes 16424 | tf_op jit(solution)/shard_map/ppermute | solution.py:99
  61.6 4.0 %collective-permute-done.7 = f32[19,4,18,1]{0,1,3,2:T(4,128)S(1)} collective-permute-done((f32[19,4,18,1]{0,1,3,2:T(4,128)S(1)}, f32[19,4,18,1]{0,1,3,2:T(4,128)S(1)}, u32[]{:S(2)}, u32[]{:S(2)}) %collective-permute-start.7) | collective-permute-done | bytes 5504 | tf_op jit(solution)/shard_map/ppermute | solution.py:99
  69.4 3.6 %shard_map.69 = (f32[19,4,16,128]{3,2,1,0:T(8,128)}, f32[16,128]{1,0:T(8,128)}) custom-call(f32[19,4,16,128]{3,2,1,0:T(8,128)} %copy-done.3, bf16[2,19,4,16,128]{4,3,2,1,0:T(8,128)(2,1)} %f_ref.3, f32[4,16,128]{2,1,0:T(8,128)} %get-tuple-element.76.b_ref, f32[4,16,128]{2,1,0:T(8,128)} %get-tuple-element.75.l_ref), custom_call_target="tpu_custom_call" | custom-call | tf_op jit(solution)/shard_map/pallas_call | solution.py:232
  73.7 1.9 %collective-permute-start.8 = (f32[4,128]{1,0:T(4,128)S(1)}, f32[4,128]{1,0:T(4,128)S(1)}, u32[]{:S(2)}, u32[]{:S(2)}) collective-permute-start(f32[4,128]{1,0:T(4,128)S(1)} %get-tuple-element.82), channel_id=1, source_target_pairs={{0,32},{32,64},{64,96},{96,128},{128,160},{160,192},{192,224},{224... | collective-permute-start | bytes 6152 | tf_op jit(solution)/shard_map/ppermute | solution.py:99
  75.6 4.9 %collective-permute-start.9 = (f32[4,128]{1,0:T(4,128)S(1)}, f32[4,128]{1,0:T(4,128)S(1)}, u32[]{:S(2)}, u32[]{:S(2)}) collective-permute-start(f32[4,128]{1,0:T(4,128)S(1)} %get-tuple-element.83), channel_id=1, source_target_pairs={{32,0},{64,32},{96,64},{128,96},{160,128},{192,160},{224,192},{256... | collective-permute-start | bytes 6152 | tf_op jit(solution)/shard_map/ppermute | solution.py:100
  80.5 1.3 collective-permute-done.9
  81.9 1.9 %collective-permute-start.10 = (f32[24,4]{1,0:T(8,128)S(1)}, f32[24,4]{1,0:T(8,128)S(1)}, u32[]{:S(2)}, u32[]{:S(2)}) collective-permute-start(f32[24,4]{1,0:T(8,128)S(1)} %get-tuple-element.80), channel_id=1, source_target_pairs={{0,1},{1,2},{2,3},{3,4},{4,5},{5,6},{6,7},{7,8},{8,9},{9,10},{10,1... | collective-permute-start | bytes 1160 | tf_op jit(solution)/shard_map/ppermute | solution.py:99
  83.8 6.0 %collective-permute-start.11 = (f32[24,4]{1,0:T(8,128)S(1)}, f32[24,4]{1,0:T(8,128)S(1)}, u32[]{:S(2)}, u32[]{:S(2)}) collective-permute-start(f32[24,4]{1,0:T(8,128)S(1)} %get-tuple-element.81), channel_id=1, source_target_pairs={{1,0},{2,1},{3,2},{4,3},{5,4},{6,5},{7,6},{8,7},{9,8},{10,9},{11,1... | collective-permute-start | bytes 1160 | tf_op jit(solution)/shard_map/ppermute | solution.py:100
  89.9 1.3 collective-permute-done.11
  92.5 2.6 %pad_maximum_fusion.18 = f32[4]{0:T(128)S(1)} fusion(f32[1]{0:T(128)} %bitcast.63, f32[1]{0:T(128)} %bitcast.62, f32[1]{0:T(128)} %bitcast.61, f32[1]{0:T(128)} %bitcast.60), kind=kLoop, calls=%fused_computation.179 | loop fusion | flops 12 | bytes 32 | tf_op jit(solution)/shard_map/stack | solution.py:279
  95.1 1.9 %collective-permute-start.12 = (f32[4]{0:T(128)S(1)}, f32[4]{0:T(128)S(1)}, u32[]{:S(2)}, u32[]{:S(2)}) collective-permute-start(f32[4]{0:T(128)S(1)} %pad_maximum_fusion.18), channel_id=1, source_target_pairs={{0,1},{1,0},{2,3},{3,2},{4,5},{5,4},{6,7},{7,6},{8,9},{9,8},{10,11... | collective-permute-start | bytes 56 | tf_op jit(solution)/shard_map/ppermute | solution.py:112
  97.0 3.5 %collective-permute-done.12 = f32[4]{0:T(128)S(1)} collective-permute-done((f32[4]{0:T(128)S(1)}, f32[4]{0:T(128)S(1)}, u32[]{:S(2)}, u32[]{:S(2)}) %collective-permute-start.12) | collective-permute-done | bytes 48 | tf_op jit(solution)/shard_map/ppermute | solution.py:112
  100.5 2.6 %fusion.41 = f32[4]{0:T(128)S(1)} fusion(f32[4]{0:T(128)S(1)} %collective-permute-done.12, f32[1]{0:T(128)} %bitcast.63, f32[1]{0:T(128)} %bitcast.62, f32[1]{0:T(128)} %bitcast.61, f32[1]{0:T(128)} %bitcast.60), kind=kLoop, calls=%fused_computation.188 | loop fusion | flops 16 | bytes 48 | tf_op jit(solution)/shard_map/add | solution.py:112
  103.2 1.9 %collective-permute-start.13 = (f32[4]{0:T(128)S(1)}, f32[4]{0:T(128)S(1)}, u32[]{:S(2)}, u32[]{:S(2)}) collective-permute-start(f32[4]{0:T(128)S(1)} %fusion.41), channel_id=1, source_target_pairs={{0,2},{1,3},{2,0},{3,1},{4,6},{5,7},{6,4},{7,5},{8,10},{9,11},{10,... | collective-permute-start | bytes 56 | tf_op jit(solution)/shard_map/ppermute | solution.py:112
  105.1 4.4 %collective-permute-done.13 = f32[4]{0:T(128)S(1)} collective-permute-done((f32[4]{0:T(128)S(1)}, f32[4]{0:T(128)S(1)}, u32[]{:S(2)}, u32[]{:S(2)}) %collective-permute-start.13) | collective-permute-done | bytes 48 | tf_op jit(solution)/shard_map/ppermute | solution.py:112
  109.5 2.6 %fusion.42 = f32[4]{0:T(128)S(1)} fusion(f32[4]{0:T(128)S(1)} %collective-permute-done.13, f32[4]{0:T(128)S(1)} %collective-permute-done.12, f32[1]{0:T(128)} %bitcast.63, f32[1]{0:T(128)} %bitcast.62, f32[1]{0:T(128)} %bitcast.61, f32[1]{0:T(128)} %bitcast.60), kind=kLoop, calls=%fused_computation.189 | loop fusion | flops 20 | bytes 64 | tf_op jit(solution)/shard_map/add | solution.py:112
  112.2 1.9 %collective-permute-start.14 = (f32[4]{0:T(128)S(1)}, f32[4]{0:T(128)S(1)}, u32[]{:S(2)}, u32[]{:S(2)}) collective-permute-start(f32[4]{0:T(128)S(1)} %fusion.42), channel_id=1, source_target_pairs={{0,4},{1,5},{2,6},{3,7},{4,0},{5,1},{6,2},{7,3},{8,12},{9,13},{10,... | collective-permute-start | bytes 56 | tf_op jit(solution)/shard_map/ppermute | solution.py:112
  114.1 7.4 %collective-permute-done.14 = f32[4]{0:T(128)S(1)} collective-permute-done((f32[4]{0:T(128)S(1)}, f32[4]{0:T(128)S(1)}, u32[]{:S(2)}, u32[]{:S(2)}) %collective-permute-start.14) | collective-permute-done | bytes 48 | tf_op jit(solution)/shard_map/ppermute | solution.py:112
  121.5 2.4 %collective-permute-start.15 = (f32[4]{0:T(128)S(1)}, f32[4]{0:T(128)S(1)}, u32[]{:S(2)}, u32[]{:S(2)}) collective-permute-start(f32[4]{0:T(128)S(1)} %add.128), channel_id=1, source_target_pairs={{0,8},{1,9},{2,10},{3,11},{4,12},{5,13},{6,14},{7,15},{8,0},{9,1},... | collective-permute-start | bytes 56 | tf_op jit(solution)/shard_map/ppermute | solution.py:112
  124.0 3.0 %collective-permute-done.15 = f32[4]{0:T(128)S(1)} collective-permute-done((f32[4]{0:T(128)S(1)}, f32[4]{0:T(128)S(1)}, u32[]{:S(2)}, u32[]{:S(2)}) %collective-permute-start.15) | collective-permute-done | bytes 48 | tf_op jit(solution)/shard_map/ppermute | solution.py:112
  127.0 3.0 %collective-permute-start.16 = (f32[4]{0:T(128)S(1)}, f32[4]{0:T(128)S(1)}, u32[]{:S(2)}, u32[]{:S(2)}) collective-permute-start(f32[4]{0:T(128)S(1)} %add.129), channel_id=1, source_target_pairs={{0,16},{1,17},{2,18},{3,19},{4,20},{5,21},{6,22},{7,23},{8,24},{9,... | collective-permute-start | bytes 56 | tf_op jit(solution)/shard_map/ppermute | solution.py:112
  130.0 3.9 %collective-permute-done.16 = f32[4]{0:T(128)S(1)} collective-permute-done((f32[4]{0:T(128)S(1)}, f32[4]{0:T(128)S(1)}, u32[]{:S(2)}, u32[]{:S(2)}) %collective-permute-start.16) | collective-permute-done | bytes 48 | tf_op jit(solution)/shard_map/ppermute | solution.py:112
  134.0 1.9 %collective-permute-start.17 = (f32[4]{0:T(128)S(1)}, f32[4]{0:T(128)S(1)}, u32[]{:S(2)}, u32[]{:S(2)}) collective-permute-start(f32[4]{0:T(128)S(1)} %add.130), channel_id=1, source_target_pairs={{0,32},{1,33},{2,34},{3,35},{4,36},{5,37},{6,38},{7,39},{8,40},{9,... | collective-permute-start | bytes 56 | tf_op jit(solution)/shard_map/ppermute | solution.py:112
  135.9 1.1 collective-permute-done.17
  137.0 1.9 %collective-permute-start.18 = (f32[4]{0:T(128)S(1)}, f32[4]{0:T(128)S(1)}, u32[]{:S(2)}, u32[]{:S(2)}) collective-permute-start(f32[4]{0:T(128)S(1)} %add.131), channel_id=1, source_target_pairs={{0,64},{1,65},{2,66},{3,67},{4,68},{5,69},{6,70},{7,71},{8,72},{9,... | collective-permute-start | bytes 56 | tf_op jit(solution)/shard_map/ppermute | solution.py:112
  138.9 3.5 %collective-permute-done.18 = f32[4]{0:T(128)S(1)} collective-permute-done((f32[4]{0:T(128)S(1)}, f32[4]{0:T(128)S(1)}, u32[]{:S(2)}, u32[]{:S(2)}) %collective-permute-start.18) | collective-permute-done | bytes 48 | tf_op jit(solution)/shard_map/ppermute | solution.py:112
  142.5 1.9 %collective-permute-start.19 = (f32[4]{0:T(128)S(1)}, f32[4]{0:T(128)S(1)}, u32[]{:S(2)}, u32[]{:S(2)}) collective-permute-start(f32[4]{0:T(128)S(1)} %add.132), channel_id=1, source_target_pairs={{0,128},{1,129},{2,130},{3,131},{4,132},{5,133},{6,134},{7,135},{8... | collective-permute-start | bytes 56 | tf_op jit(solution)/shard_map/ppermute | solution.py:112
  144.4 4.4 %collective-permute-done.19 = f32[4]{0:T(128)S(1)} collective-permute-done((f32[4]{0:T(128)S(1)}, f32[4]{0:T(128)S(1)}, u32[]{:S(2)}, u32[]{:S(2)}) %collective-permute-start.19) | collective-permute-done | bytes 48 | tf_op jit(solution)/shard_map/ppermute | solution.py:112
  148.8 1.9 %collective-permute-start.20 = (f32[4]{0:T(128)S(1)}, f32[4]{0:T(128)S(1)}, u32[]{:S(2)}, u32[]{:S(2)}) collective-permute-start(f32[4]{0:T(128)S(1)} %add.133), channel_id=1, source_target_pairs={{0,256},{1,257},{2,258},{3,259},{4,260},{5,261},{6,262},{7,263},{8... | collective-permute-start | bytes 56 | tf_op jit(solution)/shard_map/ppermute | solution.py:112
  150.7 7.4 %collective-permute-done.20 = f32[4]{0:T(128)S(1)} collective-permute-done((f32[4]{0:T(128)S(1)}, f32[4]{0:T(128)S(1)}, u32[]{:S(2)}, u32[]{:S(2)}) %collective-permute-start.20) | collective-permute-done | bytes 48 | tf_op jit(solution)/shard_map/ppermute | solution.py:112
  158.9 1.8 %select_add_fusion = f32[16,128]{1,0:T(8,128)} fusion(pred[16,128]{1,0:T(8,128)(4,1)S(1)} %get-tuple-element.16, f32[16,128]{1,0:T(8,128)S(1)} %get-tuple-element.15, pred[16,128]{1,0:T(8,128)(4,1)S(1)} %get-tuple-element.14, f32[]{:T(128)} %bitcast.65, f32[]{:T(128)} %bitcast.64), kind=kLoop, calls=%fused_computation.161 | loop fusion | flops 10240 | bytes 20488 | tf_op jit(solution)/shard_map/add | solution.py:289
  (108 shorter events, 15.4 us)
Async XLA Ops:
  1.8 12.4 %collective-permute-start.1 = (f32[19,4,1,128]{3,2,1,0:T(1,128)S(1)}, f32[19,4,1,128]{3,2,1,0:T(1,128)S(1)}, u32[]{:S(2)}, u32[]{:S(2)}) collective-permute-start(f32[19,4,1,128]{3,2,1,0:T(1,128)S(1)} %get-tuple-element.73), channel_id=1, source_target_pairs={{0,32},{32,64},{64,96},{96,128},{128,160},{160,192},{192,224},{224... | collective-permute-start | bytes 116744 | tf_op jit(solution)/shard_map/ppermute | solution.py:99
  3.7 8.2 %collective-permute-start = (f32[19,4,1,128]{3,2,1,0:T(1,128)S(1)}, f32[19,4,1,128]{3,2,1,0:T(1,128)S(1)}, u32[]{:S(2)}, u32[]{:S(2)}) collective-permute-start(f32[19,4,1,128]{3,2,1,0:T(1,128)S(1)} %get-tuple-element.74), channel_id=1, source_target_pairs={{32,0},{64,32},{96,64},{128,96},{160,128},{192,160},{224,192},{256... | collective-permute-start | bytes 116744 | tf_op jit(solution)/shard_map/ppermute | solution.py:100
  9.3 1.2 copy-start.4
  9.3 1.2 copy-start.7
  9.3 4.8 %copy-start = (f32[19,4,16,128]{3,2,1,0:T(8,128)S(1)}, f32[19,4,16,128]{3,2,1,0:T(8,128)}, u32[]{:S(2)}) copy-start(f32[19,4,16,128]{3,2,1,0:T(8,128)} %param.5) | copy-start | bytes 1867780
  10.5 0.8 copy-start.5
  15.8 20.2 %collective-permute-start.2 = (f32[19,4,18,1]{0,1,3,2:T(4,128)S(1)}, f32[19,4,18,1]{0,1,3,2:T(4,128)S(1)}, u32[]{:S(2)}, u32[]{:S(2)}) collective-permute-start(f32[19,4,18,1]{0,1,3,2:T(4,128)S(1)} %copy.7), channel_id=1, source_target_pairs={{1,0},{2,1},{3,2},{4,3},{5,4},{6,5},{7,6},{8,7},{9,8},{10,9},{11,1... | collective-permute-start | bytes 16424 | tf_op jit(solution)/shard_map/ppermute | solution.py:100
  27.0 8.0 %collective-permute-start.3 = (f32[19,4,18,1]{0,1,3,2:T(4,128)S(1)}, f32[19,4,18,1]{0,1,3,2:T(4,128)S(1)}, u32[]{:S(2)}, u32[]{:S(2)}) collective-permute-start(f32[19,4,18,1]{0,1,3,2:T(4,128)S(1)} %copy.9), channel_id=1, source_target_pairs={{0,1},{1,2},{2,3},{3,4},{4,5},{5,6},{6,7},{7,8},{8,9},{9,10},{10,1... | collective-permute-start | bytes 16424 | tf_op jit(solution)/shard_map/ppermute | solution.py:99
  38.0 0.8 copy-start.2
  44.3 9.7 %copy-start.1 = (f32[19,4,16,128]{3,2,1,0:T(8,128)S(1)}, f32[19,4,16,128]{3,2,1,0:T(8,128)}, u32[]{:S(2)}) copy-start(f32[19,4,16,128]{3,2,1,0:T(8,128)} %get-tuple-element.6) | copy-start | bytes 1867780
  44.3 5.6 %collective-permute-start.4 = (f32[19,4,1,128]{3,2,1,0:T(1,128)S(1)}, f32[19,4,1,128]{3,2,1,0:T(1,128)S(1)}, u32[]{:S(2)}, u32[]{:S(2)}) collective-permute-start(f32[19,4,1,128]{3,2,1,0:T(1,128)S(1)} %get-tuple-element.66), channel_id=1, source_target_pairs={{32,0},{64,32},{96,64},{128,96},{160,128},{192,160},{224,192},{256... | collective-permute-start | bytes 116744 | tf_op jit(solution)/shard_map/ppermute | solution.py:100
  47.5 6.5 %collective-permute-start.5 = (f32[19,4,1,128]{3,2,1,0:T(1,128)S(1)}, f32[19,4,1,128]{3,2,1,0:T(1,128)S(1)}, u32[]{:S(2)}, u32[]{:S(2)}) collective-permute-start(f32[19,4,1,128]{3,2,1,0:T(1,128)S(1)} %get-tuple-element.65), channel_id=1, source_target_pairs={{0,32},{32,64},{64,96},{96,128},{128,160},{160,192},{192,224},{224... | collective-permute-start | bytes 116744 | tf_op jit(solution)/shard_map/ppermute | solution.py:99
  55.7 10.9 %collective-permute-start.6 = (f32[19,4,18,1]{0,1,3,2:T(4,128)S(1)}, f32[19,4,18,1]{0,1,3,2:T(4,128)S(1)}, u32[]{:S(2)}, u32[]{:S(2)}) collective-permute-start(f32[19,4,18,1]{0,1,3,2:T(4,128)S(1)} %copy.11), channel_id=1, source_target_pairs={{1,0},{2,1},{3,2},{4,3},{5,4},{6,5},{7,6},{8,7},{9,8},{10,9},{11,1... | collective-permute-start | bytes 16424 | tf_op jit(solution)/shard_map/ppermute | solution.py:100
  57.6 8.0 %collective-permute-start.7 = (f32[19,4,18,1]{0,1,3,2:T(4,128)S(1)}, f32[19,4,18,1]{0,1,3,2:T(4,128)S(1)}, u32[]{:S(2)}, u32[]{:S(2)}) collective-permute-start(f32[19,4,18,1]{0,1,3,2:T(4,128)S(1)} %copy.13), channel_id=1, source_target_pairs={{0,1},{1,2},{2,3},{3,4},{4,5},{5,6},{6,7},{7,8},{8,9},{9,10},{10,1... | collective-permute-start | bytes 16424 | tf_op jit(solution)/shard_map/ppermute | solution.py:99
  68.6 0.8 copy-start.3
  69.4 3.6 %copy-start.6 = (f32[16,128]{1,0:T(8,128)S(1)}, f32[16,128]{1,0:T(8,128)}, u32[]{:S(2)}) copy-start(f32[16,128]{1,0:T(8,128)} %get-tuple-element.8) | copy-start | bytes 24580
  73.7 6.8 %collective-permute-start.8 = (f32[4,128]{1,0:T(4,128)S(1)}, f32[4,128]{1,0:T(4,128)S(1)}, u32[]{:S(2)}, u32[]{:S(2)}) collective-permute-start(f32[4,128]{1,0:T(4,128)S(1)} %get-tuple-element.82), channel_id=1, source_target_pairs={{0,32},{32,64},{64,96},{96,128},{128,160},{160,192},{192,224},{224... | collective-permute-start | bytes 6152 | tf_op jit(solution)/shard_map/ppermute | solution.py:99
  75.6 6.1 %collective-permute-start.9 = (f32[4,128]{1,0:T(4,128)S(1)}, f32[4,128]{1,0:T(4,128)S(1)}, u32[]{:S(2)}, u32[]{:S(2)}) collective-permute-start(f32[4,128]{1,0:T(4,128)S(1)} %get-tuple-element.83), channel_id=1, source_target_pairs={{32,0},{64,32},{96,64},{128,96},{160,128},{192,160},{224,192},{256... | collective-permute-start | bytes 6152 | tf_op jit(solution)/shard_map/ppermute | solution.py:100
  81.9 8.0 %collective-permute-start.10 = (f32[24,4]{1,0:T(8,128)S(1)}, f32[24,4]{1,0:T(8,128)S(1)}, u32[]{:S(2)}, u32[]{:S(2)}) collective-permute-start(f32[24,4]{1,0:T(8,128)S(1)} %get-tuple-element.80), channel_id=1, source_target_pairs={{0,1},{1,2},{2,3},{3,4},{4,5},{5,6},{6,7},{7,8},{8,9},{9,10},{10,1... | collective-permute-start | bytes 1160 | tf_op jit(solution)/shard_map/ppermute | solution.py:99
  83.8 7.4 %collective-permute-start.11 = (f32[24,4]{1,0:T(8,128)S(1)}, f32[24,4]{1,0:T(8,128)S(1)}, u32[]{:S(2)}, u32[]{:S(2)}) collective-permute-start(f32[24,4]{1,0:T(8,128)S(1)} %get-tuple-element.81), channel_id=1, source_target_pairs={{1,0},{2,1},{3,2},{4,3},{5,4},{6,5},{7,6},{8,7},{9,8},{10,9},{11,1... | collective-permute-start | bytes 1160 | tf_op jit(solution)/shard_map/ppermute | solution.py:100
  95.1 5.5 %collective-permute-start.12 = (f32[4]{0:T(128)S(1)}, f32[4]{0:T(128)S(1)}, u32[]{:S(2)}, u32[]{:S(2)}) collective-permute-start(f32[4]{0:T(128)S(1)} %pad_maximum_fusion.18), channel_id=1, source_target_pairs={{0,1},{1,0},{2,3},{3,2},{4,5},{5,4},{6,7},{7,6},{8,9},{9,8},{10,11... | collective-permute-start | bytes 56 | tf_op jit(solution)/shard_map/ppermute | solution.py:112
  103.2 6.4 %collective-permute-start.13 = (f32[4]{0:T(128)S(1)}, f32[4]{0:T(128)S(1)}, u32[]{:S(2)}, u32[]{:S(2)}) collective-permute-start(f32[4]{0:T(128)S(1)} %fusion.41), channel_id=1, source_target_pairs={{0,2},{1,3},{2,0},{3,1},{4,6},{5,7},{6,4},{7,5},{8,10},{9,11},{10,... | collective-permute-start | bytes 56 | tf_op jit(solution)/shard_map/ppermute | solution.py:112
  112.2 9.4 %collective-permute-start.14 = (f32[4]{0:T(128)S(1)}, f32[4]{0:T(128)S(1)}, u32[]{:S(2)}, u32[]{:S(2)}) collective-permute-start(f32[4]{0:T(128)S(1)} %fusion.42), channel_id=1, source_target_pairs={{0,4},{1,5},{2,6},{3,7},{4,0},{5,1},{6,2},{7,3},{8,12},{9,13},{10,... | collective-permute-start | bytes 56 | tf_op jit(solution)/shard_map/ppermute | solution.py:112
  121.5 5.5 %collective-permute-start.15 = (f32[4]{0:T(128)S(1)}, f32[4]{0:T(128)S(1)}, u32[]{:S(2)}, u32[]{:S(2)}) collective-permute-start(f32[4]{0:T(128)S(1)} %add.128), channel_id=1, source_target_pairs={{0,8},{1,9},{2,10},{3,11},{4,12},{5,13},{6,14},{7,15},{8,0},{9,1},... | collective-permute-start | bytes 56 | tf_op jit(solution)/shard_map/ppermute | solution.py:112
  127.0 7.0 %collective-permute-start.16 = (f32[4]{0:T(128)S(1)}, f32[4]{0:T(128)S(1)}, u32[]{:S(2)}, u32[]{:S(2)}) collective-permute-start(f32[4]{0:T(128)S(1)} %add.129), channel_id=1, source_target_pairs={{0,16},{1,17},{2,18},{3,19},{4,20},{5,21},{6,22},{7,23},{8,24},{9,... | collective-permute-start | bytes 56 | tf_op jit(solution)/shard_map/ppermute | solution.py:112
  134.0 3.0 %collective-permute-start.17 = (f32[4]{0:T(128)S(1)}, f32[4]{0:T(128)S(1)}, u32[]{:S(2)}, u32[]{:S(2)}) collective-permute-start(f32[4]{0:T(128)S(1)} %add.130), channel_id=1, source_target_pairs={{0,32},{1,33},{2,34},{3,35},{4,36},{5,37},{6,38},{7,39},{8,40},{9,... | collective-permute-start | bytes 56 | tf_op jit(solution)/shard_map/ppermute | solution.py:112
  137.0 5.5 %collective-permute-start.18 = (f32[4]{0:T(128)S(1)}, f32[4]{0:T(128)S(1)}, u32[]{:S(2)}, u32[]{:S(2)}) collective-permute-start(f32[4]{0:T(128)S(1)} %add.131), channel_id=1, source_target_pairs={{0,64},{1,65},{2,66},{3,67},{4,68},{5,69},{6,70},{7,71},{8,72},{9,... | collective-permute-start | bytes 56 | tf_op jit(solution)/shard_map/ppermute | solution.py:112
  142.5 6.3 %collective-permute-start.19 = (f32[4]{0:T(128)S(1)}, f32[4]{0:T(128)S(1)}, u32[]{:S(2)}, u32[]{:S(2)}) collective-permute-start(f32[4]{0:T(128)S(1)} %add.132), channel_id=1, source_target_pairs={{0,128},{1,129},{2,130},{3,131},{4,132},{5,133},{6,134},{7,135},{8... | collective-permute-start | bytes 56 | tf_op jit(solution)/shard_map/ppermute | solution.py:112
  148.8 9.4 %collective-permute-start.20 = (f32[4]{0:T(128)S(1)}, f32[4]{0:T(128)S(1)}, u32[]{:S(2)}, u32[]{:S(2)}) collective-permute-start(f32[4]{0:T(128)S(1)} %add.133), channel_id=1, source_target_pairs={{0,256},{1,257},{2,258},{3,259},{4,260},{5,261},{6,262},{7,263},{8... | collective-permute-start | bytes 56 | tf_op jit(solution)/shard_map/ppermute | solution.py:112

commit v3 on v2

--- a/solution.py
+++ b/solution.py
@@ -103,13 +103,12 @@
 
 
 def global_sum(values):
-    nx = lax.axis_size("gx")
+    values = lax.psum(values, "gx")
     ny = lax.axis_size("gy")
-    total = nx * ny
-    bits = total.bit_length() - 1
-    assert 1 << bits == total
+    bits = ny.bit_length() - 1
+    assert 1 << bits == ny
     for k in range(bits):
-        values = values + lax.ppermute(values, ("gx", "gy"), [(i, i ^ (1 << k)) for i in range(total)])
+        values = values + lax.ppermute(values, "gy", [(i, i ^ (1 << k)) for i in range(ny)])
     return values
 
 

time: 162 us -> 158 us (0.975)
  blocking collectives: 0 us -> 25.3 us
  waiting for transfers between devices: 53.3 us -> 36.8 us
  starting transfers between devices: 63.7 us -> 56.1 us
  other arithmetic: 14.4 us -> 9.23 us
    psum x0 -> x1, blocking collectives: none -> 25.3 us  [global_sum(): values = lax.psum(values, 'gx')]
    ppermute x9 -> x5, waiting for transfers between devices: 38.9 us -> 22.4 us  [global_sum(): lax.ppermute(values, 'gy', [(i, i ^ 1 << k) for i in range(ny)])]
    ppermute x9 -> x5, starting transfers between devices: 18.8 us -> 11.2 us  [global_sum(): lax.ppermute(values, 'gy', [(i, i ^ 1 << k) for i in range(ny)])]
    add x9 -> x5, other arithmetic: 5.3 us -> 0.02 us  [global_sum(): values + lax.ppermute(values, 'gy', [(i, i ^ 1 << k) for i in range(ny)])]
  transfers between devices with their start and end apart: 21 -> 17, of which waited for: 14 -> 10; matrix products, arithmetic and copies ran while one was open for 6% -> 7% of each run, Pallas kernels for 0% -> 0%
where the time goes in v3:
time: 158 us; the launch traced here: 157 us
  starting transfers between devices  56.1 us (36%)
  waiting for transfers between devices  36.8 us (23%)
  blocking collectives  25.3 us (16%)
  local copies, waits for them, and re-layouts  20.8 us (13%)
  other arithmetic  9.23 us (6%)
  Pallas kernels  7.21 us (5%)
    ppermute x6, starting transfers between devices, halo(): high = lax.ppermute(head, axis, [(i + 1, i) for i in range(count - 1)])  30.9 us
    psum x1, blocking collectives, global_sum(): values = lax.psum(values, 'gx')  25.3 us
    ppermute x5, waiting for transfers between devices, global_sum(): lax.ppermute(values, 'gy', [(i, i ^ 1 << k) for i in range(ny)])  22.4 us
    ppermute x6, starting transfers between devices, halo(): low = lax.ppermute(tail, axis, [(i, i + 1) for i in range(count - 1)])  14 us
    ppermute x6, waiting for transfers between devices, halo(): low = lax.ppermute(tail, axis, [(i, i + 1) for i in range(count - 1)])  11.8 us
    ppermute x5, starting transfers between devices, global_sum(): lax.ppermute(values, 'gy', [(i, i ^ 1 << k) for i in range(ny)])  11.2 us
    pallas_call x2, Pallas kernels, adjoint_step(): pl.pallas_call(functools.partial(step_kernel, section, rows), out_shape=(...  7.21 us
    unnamed x22, local copies, waits for them, and re-layouts  6.22 us
  transfers between devices with their start and end apart: 17, of which 10 were waited for; matrix products, arithmetic and copies ran while one was open for 7% of the time, Pallas kernels for 0%

profile of v3, /device:TPU:38, one launch (start us, length us, event | category | flops | bytes accessed | tf_op | source)
XLA Modules:
  0.0 156.7 jit_solution(16422066971649390722)
XLA Ops:
  0.6 1.1 fusion.37
  1.8 1.9 %collective-permute-start.1 = (f32[19,4,1,128]{3,2,1,0:T(1,128)S(1)}, f32[19,4,1,128]{3,2,1,0:T(1,128)S(1)}, u32[]{:S(2)}, u32[]{:S(2)}) collective-permute-start(f32[19,4,1,128]{3,2,1,0:T(1,128)S(1)} %get-tuple-element.73), channel_id=1, source_target_pairs={{0,32},{32,64},{64,96},{96,128},{128,160},{160,192},{192,224},{224... | collective-permute-start | bytes 116744 | tf_op jit(solution)/shard_map/ppermute | solution.py:99
  3.7 4.9 %collective-permute-start = (f32[19,4,1,128]{3,2,1,0:T(1,128)S(1)}, f32[19,4,1,128]{3,2,1,0:T(1,128)S(1)}, u32[]{:S(2)}, u32[]{:S(2)}) collective-permute-start(f32[19,4,1,128]{3,2,1,0:T(1,128)S(1)} %get-tuple-element.74), channel_id=1, source_target_pairs={{32,0},{64,32},{96,64},{128,96},{160,128},{192,160},{224,192},{256... | collective-permute-start | bytes 116744 | tf_op jit(solution)/shard_map/ppermute | solution.py:100
  8.6 0.8 constant_dynamic-update-slice_fusion.19
  9.3 1.2 constant_dynamic-update-slice_fusion
  10.6 0.7 copy-done.5
  11.9 2.2 %dynamic-update-slice.41 = f32[19,4,17,128]{3,2,1,0:T(8,128)S(1)} dynamic-update-slice(f32[19,4,17,128]{3,2,1,0:T(8,128)S(1)} %constant_dynamic-update-slice_fusion, f32[19,4,1,128]{3,2,1,0:T(1,128)S(1)} %collective-permute-done, s32[]{} %constant.65, s32[]{} %constant.65, s32[]{} %constant.81, s32[]{} %constant.65) | dynamic-update-slice | bytes 77828 | tf_op jit(solution)/shard_map/concatenate | solution.py:101
  15.8 11.2 %collective-permute-start.2 = (f32[19,4,18,1]{0,1,3,2:T(4,128)S(1)}, f32[19,4,18,1]{0,1,3,2:T(4,128)S(1)}, u32[]{:S(2)}, u32[]{:S(2)}) collective-permute-start(f32[19,4,18,1]{0,1,3,2:T(4,128)S(1)} %copy.7), channel_id=1, source_target_pairs={{1,0},{2,1},{3,2},{4,3},{5,4},{6,5},{7,6},{8,7},{9,8},{10,9},{11,1... | collective-permute-start | bytes 16424 | tf_op jit(solution)/shard_map/ppermute | solution.py:100
  27.1 1.9 %collective-permute-start.3 = (f32[19,4,18,1]{0,1,3,2:T(4,128)S(1)}, f32[19,4,18,1]{0,1,3,2:T(4,128)S(1)}, u32[]{:S(2)}, u32[]{:S(2)}) collective-permute-start(f32[19,4,18,1]{0,1,3,2:T(4,128)S(1)} %copy.9), channel_id=1, source_target_pairs={{0,1},{1,2},{2,3},{3,4},{4,5},{5,6},{6,7},{7,8},{8,9},{9,10},{10,1... | collective-permute-start | bytes 16424 | tf_op jit(solution)/shard_map/ppermute | solution.py:99
  29.0 6.0 %collective-permute-done.3 = f32[19,4,18,1]{0,1,3,2:T(4,128)S(1)} collective-permute-done((f32[19,4,18,1]{0,1,3,2:T(4,128)S(1)}, f32[19,4,18,1]{0,1,3,2:T(4,128)S(1)}, u32[]{:S(2)}, u32[]{:S(2)}) %collective-permute-start.3) | collective-permute-done | bytes 5504 | tf_op jit(solution)/shard_map/ppermute | solution.py:99
  35.0 1.0 copy.10
  36.1 1.1 copy.8
  38.0 0.8 copy-done.2
  38.8 3.6 %shard_map.68 = (f32[19,4,16,128]{3,2,1,0:T(8,128)}, f32[16,128]{1,0:T(8,128)}) custom-call(f32[19,4,16,128]{3,2,1,0:T(8,128)} %copy-done.2, bf16[2,19,4,16,128]{4,3,2,1,0:T(8,128)(2,1)} %f_ref.3, f32[4,16,128]{2,1,0:T(8,128)} %get-tuple-element.76.b_ref, f32[4,16,128]{2,1,0:T(8,128)} %get-tuple-element.75.l_ref), custom_call_target="tpu_custom_call" | custom-call | tf_op jit(solution)/shard_map/pallas_call | solution.py:231
  42.4 1.1 fusion.36
  43.6 0.8 constant_dynamic-update-slice_fusion.39
  44.3 2.0 %collective-permute-start.4 = (f32[19,4,1,128]{3,2,1,0:T(1,128)S(1)}, f32[19,4,1,128]{3,2,1,0:T(1,128)S(1)}, u32[]{:S(2)}, u32[]{:S(2)}) collective-permute-start(f32[19,4,1,128]{3,2,1,0:T(1,128)S(1)} %get-tuple-element.66), channel_id=1, source_target_pairs={{32,0},{64,32},{96,64},{128,96},{160,128},{192,160},{224,192},{256... | collective-permute-start | bytes 116744 | tf_op jit(solution)/shard_map/ppermute | solution.py:100
  46.4 1.1 constant_dynamic-update-slice_fusion.20
  47.5 2.4 %collective-permute-start.5 = (f32[19,4,1,128]{3,2,1,0:T(1,128)S(1)}, f32[19,4,1,128]{3,2,1,0:T(1,128)S(1)}, u32[]{:S(2)}, u32[]{:S(2)}) collective-permute-start(f32[19,4,1,128]{3,2,1,0:T(1,128)S(1)} %get-tuple-element.65), channel_id=1, source_target_pairs={{0,32},{32,64},{64,96},{96,128},{128,160},{160,192},{192,224},{224... | collective-permute-start | bytes 116744 | tf_op jit(solution)/shard_map/ppermute | solution.py:99
  49.9 2.2 %dynamic-update-slice.20 = f32[19,4,17,128]{3,2,1,0:T(8,128)S(1)} dynamic-update-slice(f32[19,4,17,128]{3,2,1,0:T(8,128)S(1)} %constant_dynamic-update-slice_fusion.20, f32[19,4,1,128]{3,2,1,0:T(1,128)S(1)} %collective-permute-done.4, s32[]{} %constant.65, s32[]{} %constant.65, s32[]{} %constant.81, s32[]{} %constant.65) | dynamic-update-slice | bytes 77828 | tf_op jit(solution)/shard_map/concatenate | solution.py:101
  52.1 1.9 %collective-permute-done.5 = f32[19,4,1,128]{3,2,1,0:T(1,128)S(1)} collective-permute-done((f32[19,4,1,128]{3,2,1,0:T(1,128)S(1)}, f32[19,4,1,128]{3,2,1,0:T(1,128)S(1)}, u32[]{:S(2)}, u32[]{:S(2)}) %collective-permute-start.5) | collective-permute-done | bytes 38944 | tf_op jit(solution)/shard_map/ppermute | solution.py:99
  55.7 1.9 %collective-permute-start.6 = (f32[19,4,18,1]{0,1,3,2:T(4,128)S(1)}, f32[19,4,18,1]{0,1,3,2:T(4,128)S(1)}, u32[]{:S(2)}, u32[]{:S(2)}) collective-permute-start(f32[19,4,18,1]{0,1,3,2:T(4,128)S(1)} %copy.11), channel_id=1, source_target_pairs={{1,0},{2,1},{3,2},{4,3},{5,4},{6,5},{7,6},{8,7},{9,8},{10,9},{11,1... | collective-permute-start | bytes 16424 | tf_op jit(solution)/shard_map/ppermute | solution.py:100
  57.6 3.9 %collective-permute-start.7 = (f32[19,4,18,1]{0,1,3,2:T(4,128)S(1)}, f32[19,4,18,1]{0,1,3,2:T(4,128)S(1)}, u32[]{:S(2)}, u32[]{:S(2)}) collective-permute-start(f32[19,4,18,1]{0,1,3,2:T(4,128)S(1)} %copy.13), channel_id=1, source_target_pairs={{0,1},{1,2},{2,3},{3,4},{4,5},{5,6},{6,7},{7,8},{8,9},{9,10},{10,1... | collective-permute-start | bytes 16424 | tf_op jit(solution)/shard_map/ppermute | solution.py:99
  61.6 4.0 %collective-permute-done.7 = f32[19,4,18,1]{0,1,3,2:T(4,128)S(1)} collective-permute-done((f32[19,4,18,1]{0,1,3,2:T(4,128)S(1)}, f32[19,4,18,1]{0,1,3,2:T(4,128)S(1)}, u32[]{:S(2)}, u32[]{:S(2)}) %collective-permute-start.7) | collective-permute-done | bytes 5504 | tf_op jit(solution)/shard_map/ppermute | solution.py:99
  65.6 1.0 copy.14
  66.6 1.1 copy.12
  68.6 0.8 copy-done.3
  69.4 3.6 %shard_map.69 = (f32[19,4,16,128]{3,2,1,0:T(8,128)}, f32[16,128]{1,0:T(8,128)}) custom-call(f32[19,4,16,128]{3,2,1,0:T(8,128)} %copy-done.3, bf16[2,19,4,16,128]{4,3,2,1,0:T(8,128)(2,1)} %f_ref.3, f32[4,16,128]{2,1,0:T(8,128)} %get-tuple-element.76.b_ref, f32[4,16,128]{2,1,0:T(8,128)} %get-tuple-element.75.l_ref), custom_call_target="tpu_custom_call" | custom-call | tf_op jit(solution)/shard_map/pallas_call | solution.py:231
  73.7 1.9 %collective-permute-start.8 = (f32[4,128]{1,0:T(4,128)S(1)}, f32[4,128]{1,0:T(4,128)S(1)}, u32[]{:S(2)}, u32[]{:S(2)}) collective-permute-start(f32[4,128]{1,0:T(4,128)S(1)} %get-tuple-element.82), channel_id=1, source_target_pairs={{0,32},{32,64},{64,96},{96,128},{128,160},{160,192},{192,224},{224... | collective-permute-start | bytes 6152 | tf_op jit(solution)/shard_map/ppermute | solution.py:99
  75.6 4.9 %collective-permute-start.9 = (f32[4,128]{1,0:T(4,128)S(1)}, f32[4,128]{1,0:T(4,128)S(1)}, u32[]{:S(2)}, u32[]{:S(2)}) collective-permute-start(f32[4,128]{1,0:T(4,128)S(1)} %get-tuple-element.83), channel_id=1, source_target_pairs={{32,0},{64,32},{96,64},{128,96},{160,128},{192,160},{224,192},{256... | collective-permute-start | bytes 6152 | tf_op jit(solution)/shard_map/ppermute | solution.py:100
  80.5 1.3 collective-permute-done.9
  81.9 1.9 %collective-permute-start.10 = (f32[24,4]{1,0:T(8,128)S(1)}, f32[24,4]{1,0:T(8,128)S(1)}, u32[]{:S(2)}, u32[]{:S(2)}) collective-permute-start(f32[24,4]{1,0:T(8,128)S(1)} %get-tuple-element.80), channel_id=1, source_target_pairs={{0,1},{1,2},{2,3},{3,4},{4,5},{5,6},{6,7},{7,8},{8,9},{9,10},{10,1... | collective-permute-start | bytes 1160 | tf_op jit(solution)/shard_map/ppermute | solution.py:99
  83.8 6.0 %collective-permute-start.11 = (f32[24,4]{1,0:T(8,128)S(1)}, f32[24,4]{1,0:T(8,128)S(1)}, u32[]{:S(2)}, u32[]{:S(2)}) collective-permute-start(f32[24,4]{1,0:T(8,128)S(1)} %get-tuple-element.81), channel_id=1, source_target_pairs={{1,0},{2,1},{3,2},{4,3},{5,4},{6,5},{7,6},{8,7},{9,8},{10,9},{11,1... | collective-permute-start | bytes 1160 | tf_op jit(solution)/shard_map/ppermute | solution.py:100
  89.9 1.3 collective-permute-done.11
  91.7 0.8 select_reduce_fusion.1
  92.4 2.6 %pad_maximum_fusion.18 = f32[4]{0:T(128)S(1)} fusion(f32[1]{0:T(128)} %bitcast.63, f32[1]{0:T(128)} %bitcast.62, f32[1]{0:T(128)} %bitcast.61, f32[1]{0:T(128)} %bitcast.60), kind=kLoop, calls=%fused_computation.179 | loop fusion | flops 12 | bytes 32 | tf_op jit(solution)/shard_map/stack | solution.py:278
  95.1 25.3 %psum.7 = f32[4]{0:T(128)S(1)} all-reduce(f32[4]{0:T(128)S(1)} %pad_maximum_fusion.18), channel_id=1, replica_groups=mesh['gx'=16,'gy'=32] {'gx'}, use_global_device_ids=true, to_apply=%region_4.5 | all-reduce | flops 4 | bytes 32 | tf_op jit(solution)/shard_map/psum | solution.py:106
  120.4 1.9 %collective-permute-start.12 = (f32[4]{0:T(128)S(1)}, f32[4]{0:T(128)S(1)}, u32[]{:S(2)}, u32[]{:S(2)}) collective-permute-start(f32[4]{0:T(128)S(1)} %psum.7), channel_id=1, source_target_pairs={{0,1},{1,0},{2,3},{3,2},{4,5},{5,4},{6,7},{7,6},{8,9},{9,8},{10,11... | collective-permute-start | bytes 56 | tf_op jit(solution)/shard_map/ppermute | solution.py:111
  122.3 3.5 %collective-permute-done.12 = f32[4]{0:T(128)S(1)} collective-permute-done((f32[4]{0:T(128)S(1)}, f32[4]{0:T(128)S(1)}, u32[]{:S(2)}, u32[]{:S(2)}) %collective-permute-start.12) | collective-permute-done | bytes 48 | tf_op jit(solution)/shard_map/ppermute | solution.py:111
  125.8 1.9 %collective-permute-start.13 = (f32[4]{0:T(128)S(1)}, f32[4]{0:T(128)S(1)}, u32[]{:S(2)}, u32[]{:S(2)}) collective-permute-start(f32[4]{0:T(128)S(1)} %add.116), channel_id=1, source_target_pairs={{0,2},{1,3},{2,0},{3,1},{4,6},{5,7},{6,4},{7,5},{8,10},{9,11},{10,... | collective-permute-start | bytes 56 | tf_op jit(solution)/shard_map/ppermute | solution.py:111
  127.8 4.4 %collective-permute-done.13 = f32[4]{0:T(128)S(1)} collective-permute-done((f32[4]{0:T(128)S(1)}, f32[4]{0:T(128)S(1)}, u32[]{:S(2)}, u32[]{:S(2)}) %collective-permute-start.13) | collective-permute-done | bytes 48 | tf_op jit(solution)/shard_map/ppermute | solution.py:111
  132.2 1.9 %collective-permute-start.14 = (f32[4]{0:T(128)S(1)}, f32[4]{0:T(128)S(1)}, u32[]{:S(2)}, u32[]{:S(2)}) collective-permute-start(f32[4]{0:T(128)S(1)} %add.117), channel_id=1, source_target_pairs={{0,4},{1,5},{2,6},{3,7},{4,0},{5,1},{6,2},{7,3},{8,12},{9,13},{10,... | collective-permute-start | bytes 56 | tf_op jit(solution)/shard_map/ppermute | solution.py:111
  134.1 7.4 %collective-permute-done.14 = f32[4]{0:T(128)S(1)} collective-permute-done((f32[4]{0:T(128)S(1)}, f32[4]{0:T(128)S(1)}, u32[]{:S(2)}, u32[]{:S(2)}) %collective-permute-start.14) | collective-permute-done | bytes 48 | tf_op jit(solution)/shard_map/ppermute | solution.py:111
  141.6 2.4 %collective-permute-start.15 = (f32[4]{0:T(128)S(1)}, f32[4]{0:T(128)S(1)}, u32[]{:S(2)}, u32[]{:S(2)}) collective-permute-start(f32[4]{0:T(128)S(1)} %add.118), channel_id=1, source_target_pairs={{0,8},{1,9},{2,10},{3,11},{4,12},{5,13},{6,14},{7,15},{8,0},{9,1},... | collective-permute-start | bytes 56 | tf_op jit(solution)/shard_map/ppermute | solution.py:111
  144.0 3.0 %collective-permute-done.15 = f32[4]{0:T(128)S(1)} collective-permute-done((f32[4]{0:T(128)S(1)}, f32[4]{0:T(128)S(1)}, u32[]{:S(2)}, u32[]{:S(2)}) %collective-permute-start.15) | collective-permute-done | bytes 48 | tf_op jit(solution)/shard_map/ppermute | solution.py:111
  147.0 3.0 %collective-permute-start.16 = (f32[4]{0:T(128)S(1)}, f32[4]{0:T(128)S(1)}, u32[]{:S(2)}, u32[]{:S(2)}) collective-permute-start(f32[4]{0:T(128)S(1)} %add.119), channel_id=1, source_target_pairs={{0,16},{1,17},{2,18},{3,19},{4,20},{5,21},{6,22},{7,23},{8,24},{9,... | collective-permute-start | bytes 56 | tf_op jit(solution)/shard_map/ppermute | solution.py:111
  150.0 3.9 %collective-permute-done.16 = f32[4]{0:T(128)S(1)} collective-permute-done((f32[4]{0:T(128)S(1)}, f32[4]{0:T(128)S(1)}, u32[]{:S(2)}, u32[]{:S(2)}) %collective-permute-start.16) | collective-permute-done | bytes 48 | tf_op jit(solution)/shard_map/ppermute | solution.py:111
  154.7 2.0 %select_add_fusion = f32[16,128]{1,0:T(8,128)} fusion(pred[16,128]{1,0:T(8,128)(4,1)S(1)} %get-tuple-element.16, f32[16,128]{1,0:T(8,128)S(1)} %get-tuple-element.15, pred[16,128]{1,0:T(8,128)(4,1)S(1)} %get-tuple-element.14, f32[]{:T(128)} %bitcast.65, f32[]{:T(128)} %bitcast.64), kind=kLoop, calls=%fused_computation.161 | loop fusion | flops 10240 | bytes 20488 | tf_op jit(solution)/shard_map/add | solution.py:288
  (97 shorter events, 7.7 us)
Async XLA Ops:
  1.8 12.4 %collective-permute-start.1 = (f32[19,4,1,128]{3,2,1,0:T(1,128)S(1)}, f32[19,4,1,128]{3,2,1,0:T(1,128)S(1)}, u32[]{:S(2)}, u32[]{:S(2)}) collective-permute-start(f32[19,4,1,128]{3,2,1,0:T(1,128)S(1)} %get-tuple-element.73), channel_id=1, source_target_pairs={{0,32},{32,64},{64,96},{96,128},{128,160},{160,192},{192,224},{224... | collective-permute-start | bytes 116744 | tf_op jit(solution)/shard_map/ppermute | solution.py:99
  3.7 8.2 %collective-permute-start = (f32[19,4,1,128]{3,2,1,0:T(1,128)S(1)}, f32[19,4,1,128]{3,2,1,0:T(1,128)S(1)}, u32[]{:S(2)}, u32[]{:S(2)}) collective-permute-start(f32[19,4,1,128]{3,2,1,0:T(1,128)S(1)} %get-tuple-element.74), channel_id=1, source_target_pairs={{32,0},{64,32},{96,64},{128,96},{160,128},{192,160},{224,192},{256... | collective-permute-start | bytes 116744 | tf_op jit(solution)/shard_map/ppermute | solution.py:100
  9.3 1.2 copy-start.4
  9.3 1.2 copy-start.7
  9.3 4.8 %copy-start = (f32[19,4,16,128]{3,2,1,0:T(8,128)S(1)}, f32[19,4,16,128]{3,2,1,0:T(8,128)}, u32[]{:S(2)}) copy-start(f32[19,4,16,128]{3,2,1,0:T(8,128)} %param.5) | copy-start | bytes 1867780
  10.5 0.8 copy-start.5
  15.8 20.2 %collective-permute-start.2 = (f32[19,4,18,1]{0,1,3,2:T(4,128)S(1)}, f32[19,4,18,1]{0,1,3,2:T(4,128)S(1)}, u32[]{:S(2)}, u32[]{:S(2)}) collective-permute-start(f32[19,4,18,1]{0,1,3,2:T(4,128)S(1)} %copy.7), channel_id=1, source_target_pairs={{1,0},{2,1},{3,2},{4,3},{5,4},{6,5},{7,6},{8,7},{9,8},{10,9},{11,1... | collective-permute-start | bytes 16424 | tf_op jit(solution)/shard_map/ppermute | solution.py:100
  27.1 8.0 %collective-permute-start.3 = (f32[19,4,18,1]{0,1,3,2:T(4,128)S(1)}, f32[19,4,18,1]{0,1,3,2:T(4,128)S(1)}, u32[]{:S(2)}, u32[]{:S(2)}) collective-permute-start(f32[19,4,18,1]{0,1,3,2:T(4,128)S(1)} %copy.9), channel_id=1, source_target_pairs={{0,1},{1,2},{2,3},{3,4},{4,5},{5,6},{6,7},{7,8},{8,9},{9,10},{10,1... | collective-permute-start | bytes 16424 | tf_op jit(solution)/shard_map/ppermute | solution.py:99
  38.0 0.8 copy-start.2
  44.3 9.7 %copy-start.1 = (f32[19,4,16,128]{3,2,1,0:T(8,128)S(1)}, f32[19,4,16,128]{3,2,1,0:T(8,128)}, u32[]{:S(2)}) copy-start(f32[19,4,16,128]{3,2,1,0:T(8,128)} %get-tuple-element.6) | copy-start | bytes 1867780
  44.3 5.6 %collective-permute-start.4 = (f32[19,4,1,128]{3,2,1,0:T(1,128)S(1)}, f32[19,4,1,128]{3,2,1,0:T(1,128)S(1)}, u32[]{:S(2)}, u32[]{:S(2)}) collective-permute-start(f32[19,4,1,128]{3,2,1,0:T(1,128)S(1)} %get-tuple-element.66), channel_id=1, source_target_pairs={{32,0},{64,32},{96,64},{128,96},{160,128},{192,160},{224,192},{256... | collective-permute-start | bytes 116744 | tf_op jit(solution)/shard_map/ppermute | solution.py:100
  47.5 6.5 %collective-permute-start.5 = (f32[19,4,1,128]{3,2,1,0:T(1,128)S(1)}, f32[19,4,1,128]{3,2,1,0:T(1,128)S(1)}, u32[]{:S(2)}, u32[]{:S(2)}) collective-permute-start(f32[19,4,1,128]{3,2,1,0:T(1,128)S(1)} %get-tuple-element.65), channel_id=1, source_target_pairs={{0,32},{32,64},{64,96},{96,128},{128,160},{160,192},{192,224},{224... | collective-permute-start | bytes 116744 | tf_op jit(solution)/shard_map/ppermute | solution.py:99
  55.7 10.9 %collective-permute-start.6 = (f32[19,4,18,1]{0,1,3,2:T(4,128)S(1)}, f32[19,4,18,1]{0,1,3,2:T(4,128)S(1)}, u32[]{:S(2)}, u32[]{:S(2)}) collective-permute-start(f32[19,4,18,1]{0,1,3,2:T(4,128)S(1)} %copy.11), channel_id=1, source_target_pairs={{1,0},{2,1},{3,2},{4,3},{5,4},{6,5},{7,6},{8,7},{9,8},{10,9},{11,1... | collective-permute-start | bytes 16424 | tf_op jit(solution)/shard_map/ppermute | solution.py:100
  57.6 8.0 %collective-permute-start.7 = (f32[19,4,18,1]{0,1,3,2:T(4,128)S(1)}, f32[19,4,18,1]{0,1,3,2:T(4,128)S(1)}, u32[]{:S(2)}, u32[]{:S(2)}) collective-permute-start(f32[19,4,18,1]{0,1,3,2:T(4,128)S(1)} %copy.13), channel_id=1, source_target_pairs={{0,1},{1,2},{2,3},{3,4},{4,5},{5,6},{6,7},{7,8},{8,9},{9,10},{10,1... | collective-permute-start | bytes 16424 | tf_op jit(solution)/shard_map/ppermute | solution.py:99
  68.6 0.8 copy-start.3
  69.4 3.6 %copy-start.6 = (f32[16,128]{1,0:T(8,128)S(1)}, f32[16,128]{1,0:T(8,128)}, u32[]{:S(2)}) copy-start(f32[16,128]{1,0:T(8,128)} %get-tuple-element.8) | copy-start | bytes 24580
  73.7 6.8 %collective-permute-start.8 = (f32[4,128]{1,0:T(4,128)S(1)}, f32[4,128]{1,0:T(4,128)S(1)}, u32[]{:S(2)}, u32[]{:S(2)}) collective-permute-start(f32[4,128]{1,0:T(4,128)S(1)} %get-tuple-element.82), channel_id=1, source_target_pairs={{0,32},{32,64},{64,96},{96,128},{128,160},{160,192},{192,224},{224... | collective-permute-start | bytes 6152 | tf_op jit(solution)/shard_map/ppermute | solution.py:99
  75.6 6.1 %collective-permute-start.9 = (f32[4,128]{1,0:T(4,128)S(1)}, f32[4,128]{1,0:T(4,128)S(1)}, u32[]{:S(2)}, u32[]{:S(2)}) collective-permute-start(f32[4,128]{1,0:T(4,128)S(1)} %get-tuple-element.83), channel_id=1, source_target_pairs={{32,0},{64,32},{96,64},{128,96},{160,128},{192,160},{224,192},{256... | collective-permute-start | bytes 6152 | tf_op jit(solution)/shard_map/ppermute | solution.py:100
  81.9 8.0 %collective-permute-start.10 = (f32[24,4]{1,0:T(8,128)S(1)}, f32[24,4]{1,0:T(8,128)S(1)}, u32[]{:S(2)}, u32[]{:S(2)}) collective-permute-start(f32[24,4]{1,0:T(8,128)S(1)} %get-tuple-element.80), channel_id=1, source_target_pairs={{0,1},{1,2},{2,3},{3,4},{4,5},{5,6},{6,7},{7,8},{8,9},{9,10},{10,1... | collective-permute-start | bytes 1160 | tf_op jit(solution)/shard_map/ppermute | solution.py:99
  83.8 7.4 %collective-permute-start.11 = (f32[24,4]{1,0:T(8,128)S(1)}, f32[24,4]{1,0:T(8,128)S(1)}, u32[]{:S(2)}, u32[]{:S(2)}) collective-permute-start(f32[24,4]{1,0:T(8,128)S(1)} %get-tuple-element.81), channel_id=1, source_target_pairs={{1,0},{2,1},{3,2},{4,3},{5,4},{6,5},{7,6},{8,7},{9,8},{10,9},{11,1... | collective-permute-start | bytes 1160 | tf_op jit(solution)/shard_map/ppermute | solution.py:100
  120.4 5.5 %collective-permute-start.12 = (f32[4]{0:T(128)S(1)}, f32[4]{0:T(128)S(1)}, u32[]{:S(2)}, u32[]{:S(2)}) collective-permute-start(f32[4]{0:T(128)S(1)} %psum.7), channel_id=1, source_target_pairs={{0,1},{1,0},{2,3},{3,2},{4,5},{5,4},{6,7},{7,6},{8,9},{9,8},{10,11... | collective-permute-start | bytes 56 | tf_op jit(solution)/shard_map/ppermute | solution.py:111
  125.8 6.3 %collective-permute-start.13 = (f32[4]{0:T(128)S(1)}, f32[4]{0:T(128)S(1)}, u32[]{:S(2)}, u32[]{:S(2)}) collective-permute-start(f32[4]{0:T(128)S(1)} %add.116), channel_id=1, source_target_pairs={{0,2},{1,3},{2,0},{3,1},{4,6},{5,7},{6,4},{7,5},{8,10},{9,11},{10,... | collective-permute-start | bytes 56 | tf_op jit(solution)/shard_map/ppermute | solution.py:111
  132.2 9.4 %collective-permute-start.14 = (f32[4]{0:T(128)S(1)}, f32[4]{0:T(128)S(1)}, u32[]{:S(2)}, u32[]{:S(2)}) collective-permute-start(f32[4]{0:T(128)S(1)} %add.117), channel_id=1, source_target_pairs={{0,4},{1,5},{2,6},{3,7},{4,0},{5,1},{6,2},{7,3},{8,12},{9,13},{10,... | collective-permute-start | bytes 56 | tf_op jit(solution)/shard_map/ppermute | solution.py:111
  141.6 5.5 %collective-permute-start.15 = (f32[4]{0:T(128)S(1)}, f32[4]{0:T(128)S(1)}, u32[]{:S(2)}, u32[]{:S(2)}) collective-permute-start(f32[4]{0:T(128)S(1)} %add.118), channel_id=1, source_target_pairs={{0,8},{1,9},{2,10},{3,11},{4,12},{5,13},{6,14},{7,15},{8,0},{9,1},... | collective-permute-start | bytes 56 | tf_op jit(solution)/shard_map/ppermute | solution.py:111
  147.0 7.0 %collective-permute-start.16 = (f32[4]{0:T(128)S(1)}, f32[4]{0:T(128)S(1)}, u32[]{:S(2)}, u32[]{:S(2)}) collective-permute-start(f32[4]{0:T(128)S(1)} %add.119), channel_id=1, source_target_pairs={{0,16},{1,17},{2,18},{3,19},{4,20},{5,21},{6,22},{7,23},{8,24},{9,... | collective-permute-start | bytes 56 | tf_op jit(solution)/shard_map/ppermute | solution.py:111

commit v4 on v3

--- a/solution.py
+++ b/solution.py
@@ -202,41 +202,45 @@
     return result, term
 
 
-def step_kernel(section, rows, g_ref, f_ref, b_ref, l_ref, res_ref, term_ref):
-    planes, width_x, _ = b_ref.shape
+def step_kernel(section, rows, a_ref, f_ref, b_ref, l_ref, res_ref, term_ref):
+    planes, width_x, width_y = b_ref.shape
     chunks = width_x // rows
 
-    def body(idx, acc):
-        z = idx // chunks
-        x0 = pl.multiple_of((idx % chunks) * rows, rows)
-        xs = pl.ds(x0, rows)
-        g = [g_ref[i, z, xs, :] for i in range(19)]
-        f = [f_ref[section, i, z, xs, :].astype(jnp.float32) for i in range(19)]
-        b = b_ref[z, xs, :]
-        lev = l_ref[z, xs, :]
-        result, term = cell_math(g, f, b, lev)
-        for j in range(19):
-            res_ref[j, z, xs, :] = result[j]
-        term_ref[xs, :] = term_ref[xs, :] + term
+    def body(z, acc):
+        for chunk in range(chunks):
+            x0 = chunk * rows
+            xs = pl.ds(x0, rows)
+            g = []
+            for i in range(19):
+                step_x, step_y, step_z = VELOCITIES[i]
+                zz = (z + step_z + planes) % planes
+                g.append(a_ref[i, zz, pl.ds(x0 + 1 + step_x, rows), pl.ds(1 + step_y, width_y)])
+            f = [f_ref[section, i, z, xs, :].astype(jnp.float32) for i in range(19)]
+            b = b_ref[z, xs, :]
+            lev = l_ref[z, xs, :]
+            result, term = cell_math(g, f, b, lev)
+            for j in range(19):
+                res_ref[j, z, xs, :] = result[j]
+            term_ref[xs, :] = term_ref[xs, :] + term
         return acc
 
     term_ref[...] = jnp.zeros_like(term_ref)
-    lax.fori_loop(0, planes * chunks, body, 0)
-
-
-def adjoint_step(section, pulled, forward_pops, blocking, lever):
-    _, planes, width_x, width_y = pulled.shape
+    lax.fori_loop(0, planes, body, 0)
+
+
+def adjoint_step(section, ext, forward_pops, blocking, lever):
+    planes, width_x, width_y = blocking.shape
     rows = 8 if width_x % 8 == 0 else width_x
     vmem = pl.BlockSpec(memory_space=pltpu.VMEM)
     return pl.pallas_call(
         functools.partial(step_kernel, section, rows),
         out_shape=(
-            jax.ShapeDtypeStruct(pulled.shape, jnp.float32),
+            jax.ShapeDtypeStruct((19, planes, width_x, width_y), jnp.float32),
             jax.ShapeDtypeStruct((width_x, width_y), jnp.float32),
         ),
         in_specs=[vmem] * 4,
         out_specs=(vmem, vmem),
-    )(pulled, forward_pops, blocking, lever)
+    )(ext, forward_pops, blocking, lever)
 
 
 def helmholtz(raw, w):
@@ -268,8 +272,7 @@
     adjoint = adjoint_in
     raw = jnp.zeros((width_x, width_y), jnp.float32)
     for section in (1, 0):
-        pulled = pull_back(halo(adjoint, 1), width_x, width_y)
-        adjoint, term = adjoint_step(section, pulled, forward_pops, blocking, lever)
+        adjoint, term = adjoint_step(section, halo(adjoint, 1), forward_pops, blocking, lever)
         raw = raw + term
     raw = SENSE_SCALE * raw
     smooth = helmholtz(raw, SWEEPS)

time: 158 us -> 173 us (1.095)
  Pallas kernels: 7.21 us -> 27.4 us
  local copies, waits for them, and re-layouts: 20.8 us -> 10.1 us
  other arithmetic: 9.23 us -> 15.2 us
  starting transfers between devices: 56.1 us -> 60.8 us
  waiting for transfers between devices: 36.8 us -> 32.4 us
    pallas_call x2, Pallas kernels: 7.21 us -> 27.4 us  [adjoint_step(): pl.pallas_call(functools.partial(step_kernel, section, rows), out_shape=(...]
    ppermute x6, waiting for transfers between devices: 11.8 us -> 4.36 us  [halo(): low = lax.ppermute(tail, axis, [(i, i + 1) for i in range(count - 1)])]
    ppermute x6, starting transfers between devices: 30.9 us -> 38.1 us  [halo(): high = lax.ppermute(head, axis, [(i + 1, i) for i in range(count - 1)])]
    concatenate x4 -> x6, other arithmetic: 0.39 us -> 7.37 us  [halo(): cells = jnp.concatenate([low, cells, high], axis=dim)]
    unnamed x22 -> x10, local copies, waits for them, and re-layouts: 6.22 us -> 0.03 us
    concatenate x2 -> x0, local copies, waits for them, and re-layouts: 4.33 us -> none  [halo(): cells = jnp.concatenate([low, cells, high], axis=dim)]
    ppermute x6, waiting for transfers between devices: 2.57 us -> 5.63 us  [halo(): high = lax.ppermute(head, axis, [(i + 1, i) for i in range(count - 1)])]
    ppermute x6, starting transfers between devices: 14 us -> 11.5 us  [halo(): low = lax.ppermute(tail, axis, [(i, i + 1) for i in range(count - 1)])]
  transfers between devices with their start and end apart: 17 -> 17, of which waited for: 10 -> 11; matrix products, arithmetic and copies ran while one was open for 7% -> 3% of each run, Pallas kernels for 0% -> 0%
where the time goes in v4:
time: 173 us; the launch traced here: 172 us
  starting transfers between devices  60.8 us (35%)
  waiting for transfers between devices  32.4 us (19%)
  Pallas kernels  27.4 us (16%)
  blocking collectives  25.6 us (15%)
  other arithmetic  15.2 us (9%)
  local copies, waits for them, and re-layouts  10.1 us (6%)
    ppermute x6, starting transfers between devices, halo(): high = lax.ppermute(head, axis, [(i + 1, i) for i in range(count - 1)])  38.1 us
    pallas_call x2, Pallas kernels, adjoint_step(): pl.pallas_call(functools.partial(step_kernel, section, rows), out_shape=(...  27.4 us
    psum x1, blocking collectives, global_sum(): values = lax.psum(values, 'gx')  25.6 us
    ppermute x5, waiting for transfers between devices, global_sum(): lax.ppermute(values, 'gy', [(i, i ^ 1 << k) for i in range(ny)])  22.4 us
    ppermute x6, starting transfers between devices, halo(): low = lax.ppermute(tail, axis, [(i, i + 1) for i in range(count - 1)])  11.5 us
    ppermute x5, starting transfers between devices, global_sum(): lax.ppermute(values, 'gy', [(i, i ^ 1 << k) for i in range(ny)])  11.2 us
    concatenate x6, other arithmetic, halo(): cells = jnp.concatenate([low, cells, high], axis=dim)  7.37 us
    ppermute x6, waiting for transfers between devices, halo(): high = lax.ppermute(head, axis, [(i + 1, i) for i in range(count - 1)])  5.63 us
  transfers between devices with their start and end apart: 17, of which 11 were waited for; matrix products, arithmetic and copies ran while one was open for 3% of the time, Pallas kernels for 0%

profile of v4, /device:TPU:38, one launch (start us, length us, event | category | flops | bytes accessed | tf_op | source)
XLA Modules:
  0.0 172.3 jit_solution(12014783172117330419)
XLA Ops:
  0.6 1.1 fusion.31
  1.8 1.9 %collective-permute-start = (f32[19,4,1,128]{3,2,1,0:T(1,128)S(1)}, f32[19,4,1,128]{3,2,1,0:T(1,128)S(1)}, u32[]{:S(2)}, u32[]{:S(2)}) collective-permute-start(f32[19,4,1,128]{3,2,1,0:T(1,128)S(1)} %get-tuple-element.25), channel_id=1, source_target_pairs={{0,32},{32,64},{64,96},{96,128},{128,160},{160,192},{192,224},{224... | collective-permute-start | bytes 116744 | tf_op jit(solution)/shard_map/ppermute | solution.py:99
  3.7 4.9 %collective-permute-start.1 = (f32[19,4,1,128]{3,2,1,0:T(1,128)S(1)}, f32[19,4,1,128]{3,2,1,0:T(1,128)S(1)}, u32[]{:S(2)}, u32[]{:S(2)}) collective-permute-start(f32[19,4,1,128]{3,2,1,0:T(1,128)S(1)} %get-tuple-element.26), channel_id=1, source_target_pairs={{32,0},{64,32},{96,64},{128,96},{160,128},{192,160},{224,192},{256... | collective-permute-start | bytes 116744 | tf_op jit(solution)/shard_map/ppermute | solution.py:100
  8.5 0.7 multiply_select_fusion
  9.3 0.9 collective-permute-done.1
  10.2 1.2 pad_maximum_fusion.2
  11.8 0.6 copy.8
  12.4 11.2 %collective-permute-start.3 = (f32[19,4,18,1]{0,1,3,2:T(4,128)S(1)}, f32[19,4,18,1]{0,1,3,2:T(4,128)S(1)}, u32[]{:S(2)}, u32[]{:S(2)}) collective-permute-start(f32[19,4,18,1]{0,1,3,2:T(4,128)S(1)} %copy.8), channel_id=1, source_target_pairs={{1,0},{2,1},{3,2},{4,3},{5,4},{6,5},{7,6},{8,7},{9,8},{10,9},{11,1... | collective-permute-start | bytes 16424 | tf_op jit(solution)/shard_map/ppermute | solution.py:100
  24.2 1.9 %collective-permute-start.2 = (f32[19,4,18,1]{0,1,3,2:T(4,128)S(1)}, f32[19,4,18,1]{0,1,3,2:T(4,128)S(1)}, u32[]{:S(2)}, u32[]{:S(2)}) collective-permute-start(f32[19,4,18,1]{0,1,3,2:T(4,128)S(1)} %copy.7), channel_id=1, source_target_pairs={{0,1},{1,2},{2,3},{3,4},{4,5},{5,6},{6,7},{7,8},{8,9},{9,10},{10,1... | collective-permute-start | bytes 16424 | tf_op jit(solution)/shard_map/ppermute | solution.py:99
  26.1 0.6 and_select_fusion
  26.7 1.0 copy.10
  27.8 4.4 %collective-permute-done.2 = f32[19,4,18,1]{0,1,3,2:T(4,128)S(1)} collective-permute-done((f32[19,4,18,1]{0,1,3,2:T(4,128)S(1)}, f32[19,4,18,1]{0,1,3,2:T(4,128)S(1)}, u32[]{:S(2)}, u32[]{:S(2)}) %collective-permute-start.2) | collective-permute-done | bytes 5504 | tf_op jit(solution)/shard_map/ppermute | solution.py:99
  32.1 1.0 copy.9
  33.1 2.4 %pad_maximum_fusion.a_ref = f32[19,4,18,130]{3,2,1,0:T(8,128)} fusion(f32[19,4,18,1]{3,2,1,0:T(8,128)S(1)} %copy.10, f32[19,4,1,128]{3,2,1,0:T(1,128)S(1)} %collective-permute-done.1, f32[19,4,16,128]{3,2,1,0:T(8,128)S(1)} %copy-done, f32[19,4,1,128]{3,2,1,0:T(1,128)S(1)} %collective-permute-done, f32[19,4,18,1]{3,2,1,0:T(8,128)S(1)} %copy.9), kind=kLoop, calls=%fused_computation | loop fusion | flops 711360 | bytes 1422720 | tf_op jit(solution)/shard_map/concatenate | solution.py:101
  35.6 13.7 %shard_map.68 = (f32[19,4,16,128]{3,2,1,0:T(8,128)}, f32[16,128]{1,0:T(8,128)}) custom-call(f32[19,4,18,130]{3,2,1,0:T(8,128)} %pad_maximum_fusion.a_ref, bf16[2,19,4,16,128]{4,3,2,1,0:T(8,128)(2,1)} %f_ref.3, f32[4,16,128]{2,1,0:T(8,128)} %get-tuple-element.28.b_ref, f32[4,16,128]{2,1,0:T(8,128)} %get-tuple-element.27.l_ref), custom_call_target="tpu_custom_call" | custom-call | tf_op jit(solution)/shard_map/pallas_call | solution.py:235
  49.2 1.1 fusion.30
  50.4 1.9 %collective-permute-start.4 = (f32[19,4,1,128]{3,2,1,0:T(1,128)S(1)}, f32[19,4,1,128]{3,2,1,0:T(1,128)S(1)}, u32[]{:S(2)}, u32[]{:S(2)}) collective-permute-start(f32[19,4,1,128]{3,2,1,0:T(1,128)S(1)} %get-tuple-element.23), channel_id=1, source_target_pairs={{0,32},{32,64},{64,96},{96,128},{128,160},{160,192},{192,224},{224... | collective-permute-start | bytes 116744 | tf_op jit(solution)/shard_map/ppermute | solution.py:99
  52.3 4.9 %collective-permute-start.5 = (f32[19,4,1,128]{3,2,1,0:T(1,128)S(1)}, f32[19,4,1,128]{3,2,1,0:T(1,128)S(1)}, u32[]{:S(2)}, u32[]{:S(2)}) collective-permute-start(f32[19,4,1,128]{3,2,1,0:T(1,128)S(1)} %get-tuple-element.24), channel_id=1, source_target_pairs={{32,0},{64,32},{96,64},{128,96},{160,128},{192,160},{224,192},{256... | collective-permute-start | bytes 116744 | tf_op jit(solution)/shard_map/ppermute | solution.py:100
  57.2 1.6 collective-permute-done.5
  58.8 1.2 pad_maximum_fusion.3
  61.0 1.9 %collective-permute-start.6 = (f32[19,4,18,1]{0,1,3,2:T(4,128)S(1)}, f32[19,4,18,1]{0,1,3,2:T(4,128)S(1)}, u32[]{:S(2)}, u32[]{:S(2)}) collective-permute-start(f32[19,4,18,1]{0,1,3,2:T(4,128)S(1)} %copy.11), channel_id=1, source_target_pairs={{0,1},{1,2},{2,3},{3,4},{4,5},{5,6},{6,7},{7,8},{8,9},{9,10},{10,1... | collective-permute-start | bytes 16424 | tf_op jit(solution)/shard_map/ppermute | solution.py:99
  63.5 6.0 %collective-permute-start.7 = (f32[19,4,18,1]{0,1,3,2:T(4,128)S(1)}, f32[19,4,18,1]{0,1,3,2:T(4,128)S(1)}, u32[]{:S(2)}, u32[]{:S(2)}) collective-permute-start(f32[19,4,18,1]{0,1,3,2:T(4,128)S(1)} %copy.12), channel_id=1, source_target_pairs={{1,0},{2,1},{3,2},{4,3},{5,4},{6,5},{7,6},{8,7},{9,8},{10,9},{11,1... | collective-permute-start | bytes 16424 | tf_op jit(solution)/shard_map/ppermute | solution.py:100
  69.5 1.0 copy.13
  71.1 1.0 copy.14
  72.1 2.4 %pad_maximum_fusion.1.a_ref = f32[19,4,18,130]{3,2,1,0:T(8,128)} fusion(f32[19,4,18,1]{3,2,1,0:T(8,128)S(1)} %copy.14, f32[19,4,1,128]{3,2,1,0:T(1,128)S(1)} %collective-permute-done.5, f32[19,4,16,128]{3,2,1,0:T(8,128)S(1)} %copy-done.1, f32[19,4,1,128]{3,2,1,0:T(1,128)S(1)} %collective-permute-done.4, f32[19,4,18,1]{3,2,1,0:T(8,128)S(1)} %copy.13), kind=kLoop, calls=%fused_computation.1 | loop fusion | flops 711360 | bytes 1422720 | tf_op jit(solution)/shard_map/concatenate | solution.py:101
  74.6 13.7 %shard_map.69 = (f32[19,4,16,128]{3,2,1,0:T(8,128)}, f32[16,128]{1,0:T(8,128)}) custom-call(f32[19,4,18,130]{3,2,1,0:T(8,128)} %pad_maximum_fusion.1.a_ref, bf16[2,19,4,16,128]{4,3,2,1,0:T(8,128)(2,1)} %f_ref.3, f32[4,16,128]{2,1,0:T(8,128)} %get-tuple-element.28.b_ref, f32[4,16,128]{2,1,0:T(8,128)} %get-tuple-element.27.l_ref), custom_call_target="tpu_custom_call" | custom-call | tf_op jit(solution)/shard_map/pallas_call | solution.py:235
  88.3 0.7 add_multiply_fusion
  89.0 1.9 %collective-permute-start.8 = (f32[4,128]{1,0:T(4,128)S(1)}, f32[4,128]{1,0:T(4,128)S(1)}, u32[]{:S(2)}, u32[]{:S(2)}) collective-permute-start(f32[4,128]{1,0:T(4,128)S(1)} %get-tuple-element.34), channel_id=1, source_target_pairs={{0,32},{32,64},{64,96},{96,128},{128,160},{160,192},{192,224},{224... | collective-permute-start | bytes 6152 | tf_op jit(solution)/shard_map/ppermute | solution.py:99
  90.9 4.9 %collective-permute-start.9 = (f32[4,128]{1,0:T(4,128)S(1)}, f32[4,128]{1,0:T(4,128)S(1)}, u32[]{:S(2)}, u32[]{:S(2)}) collective-permute-start(f32[4,128]{1,0:T(4,128)S(1)} %get-tuple-element.35), channel_id=1, source_target_pairs={{32,0},{64,32},{96,64},{128,96},{160,128},{192,160},{224,192},{256... | collective-permute-start | bytes 6152 | tf_op jit(solution)/shard_map/ppermute | solution.py:100
  95.8 1.3 collective-permute-done.9
  97.1 1.9 %collective-permute-start.10 = (f32[24,4]{1,0:T(8,128)S(1)}, f32[24,4]{1,0:T(8,128)S(1)}, u32[]{:S(2)}, u32[]{:S(2)}) collective-permute-start(f32[24,4]{1,0:T(8,128)S(1)} %get-tuple-element.32), channel_id=1, source_target_pairs={{0,1},{1,2},{2,3},{3,4},{4,5},{5,6},{6,7},{7,8},{8,9},{9,10},{10,1... | collective-permute-start | bytes 1160 | tf_op jit(solution)/shard_map/ppermute | solution.py:99
  99.0 6.3 %collective-permute-start.11 = (f32[24,4]{1,0:T(8,128)S(1)}, f32[24,4]{1,0:T(8,128)S(1)}, u32[]{:S(2)}, u32[]{:S(2)}) collective-permute-start(f32[24,4]{1,0:T(8,128)S(1)} %get-tuple-element.33), channel_id=1, source_target_pairs={{1,0},{2,1},{3,2},{4,3},{5,4},{6,5},{7,6},{8,7},{9,8},{10,9},{11,1... | collective-permute-start | bytes 1160 | tf_op jit(solution)/shard_map/ppermute | solution.py:100
  105.5 1.3 collective-permute-done.11
  107.3 0.8 select_reduce_fusion.1
  108.0 2.6 %pad_maximum_fusion.6 = f32[4]{0:T(128)S(1)} fusion(f32[1]{0:T(128)} %bitcast.3, f32[1]{0:T(128)} %bitcast.2, f32[1]{0:T(128)} %bitcast.1, f32[1]{0:T(128)} %bitcast), kind=kLoop, calls=%fused_computation.67 | loop fusion | flops 12 | bytes 32 | tf_op jit(solution)/shard_map/stack | solution.py:281
  110.6 25.6 %psum.7 = f32[4]{0:T(128)S(1)} all-reduce(f32[4]{0:T(128)S(1)} %pad_maximum_fusion.6), channel_id=1, replica_groups=mesh['gx'=16,'gy'=32] {'gx'}, use_global_device_ids=true, to_apply=%region_4.5 | all-reduce | flops 4 | bytes 32 | tf_op jit(solution)/shard_map/psum | solution.py:106
  136.2 1.9 %collective-permute-start.12 = (f32[4]{0:T(128)S(1)}, f32[4]{0:T(128)S(1)}, u32[]{:S(2)}, u32[]{:S(2)}) collective-permute-start(f32[4]{0:T(128)S(1)} %psum.7), channel_id=1, source_target_pairs={{0,1},{1,0},{2,3},{3,2},{4,5},{5,4},{6,7},{7,6},{8,9},{9,8},{10,11... | collective-permute-start | bytes 56 | tf_op jit(solution)/shard_map/ppermute | solution.py:111
  138.1 3.5 %collective-permute-done.12 = f32[4]{0:T(128)S(1)} collective-permute-done((f32[4]{0:T(128)S(1)}, f32[4]{0:T(128)S(1)}, u32[]{:S(2)}, u32[]{:S(2)}) %collective-permute-start.12) | collective-permute-done | bytes 48 | tf_op jit(solution)/shard_map/ppermute | solution.py:111
  141.7 1.9 %collective-permute-start.13 = (f32[4]{0:T(128)S(1)}, f32[4]{0:T(128)S(1)}, u32[]{:S(2)}, u32[]{:S(2)}) collective-permute-start(f32[4]{0:T(128)S(1)} %add.116), channel_id=1, source_target_pairs={{0,2},{1,3},{2,0},{3,1},{4,6},{5,7},{6,4},{7,5},{8,10},{9,11},{10,... | collective-permute-start | bytes 56 | tf_op jit(solution)/shard_map/ppermute | solution.py:111
  143.6 4.4 %collective-permute-done.13 = f32[4]{0:T(128)S(1)} collective-permute-done((f32[4]{0:T(128)S(1)}, f32[4]{0:T(128)S(1)}, u32[]{:S(2)}, u32[]{:S(2)}) %collective-permute-start.13) | collective-permute-done | bytes 48 | tf_op jit(solution)/shard_map/ppermute | solution.py:111
  148.0 1.9 %collective-permute-start.14 = (f32[4]{0:T(128)S(1)}, f32[4]{0:T(128)S(1)}, u32[]{:S(2)}, u32[]{:S(2)}) collective-permute-start(f32[4]{0:T(128)S(1)} %add.117), channel_id=1, source_target_pairs={{0,4},{1,5},{2,6},{3,7},{4,0},{5,1},{6,2},{7,3},{8,12},{9,13},{10,... | collective-permute-start | bytes 56 | tf_op jit(solution)/shard_map/ppermute | solution.py:111
  149.9 7.4 %collective-permute-done.14 = f32[4]{0:T(128)S(1)} collective-permute-done((f32[4]{0:T(128)S(1)}, f32[4]{0:T(128)S(1)}, u32[]{:S(2)}, u32[]{:S(2)}) %collective-permute-start.14) | collective-permute-done | bytes 48 | tf_op jit(solution)/shard_map/ppermute | solution.py:111
  157.4 2.4 %collective-permute-start.15 = (f32[4]{0:T(128)S(1)}, f32[4]{0:T(128)S(1)}, u32[]{:S(2)}, u32[]{:S(2)}) collective-permute-start(f32[4]{0:T(128)S(1)} %add.118), channel_id=1, source_target_pairs={{0,8},{1,9},{2,10},{3,11},{4,12},{5,13},{6,14},{7,15},{8,0},{9,1},... | collective-permute-start | bytes 56 | tf_op jit(solution)/shard_map/ppermute | solution.py:111
  159.8 3.0 %collective-permute-done.15 = f32[4]{0:T(128)S(1)} collective-permute-done((f32[4]{0:T(128)S(1)}, f32[4]{0:T(128)S(1)}, u32[]{:S(2)}, u32[]{:S(2)}) %collective-permute-start.15) | collective-permute-done | bytes 48 | tf_op jit(solution)/shard_map/ppermute | solution.py:111
  162.8 3.0 %collective-permute-start.16 = (f32[4]{0:T(128)S(1)}, f32[4]{0:T(128)S(1)}, u32[]{:S(2)}, u32[]{:S(2)}) collective-permute-start(f32[4]{0:T(128)S(1)} %add.119), channel_id=1, source_target_pairs={{0,16},{1,17},{2,18},{3,19},{4,20},{5,21},{6,22},{7,23},{8,24},{9,... | collective-permute-start | bytes 56 | tf_op jit(solution)/shard_map/ppermute | solution.py:111
  165.8 3.9 %collective-permute-done.16 = f32[4]{0:T(128)S(1)} collective-permute-done((f32[4]{0:T(128)S(1)}, f32[4]{0:T(128)S(1)}, u32[]{:S(2)}, u32[]{:S(2)}) %collective-permute-start.16) | collective-permute-done | bytes 48 | tf_op jit(solution)/shard_map/ppermute | solution.py:111
  169.9 0.6 fusion.34
  170.5 1.9 %select_add_fusion = f32[16,128]{1,0:T(8,128)} fusion(pred[16,128]{1,0:T(8,128)(4,1)S(1)} %get-tuple-element.16, f32[16,128]{1,0:T(8,128)S(1)} %get-tuple-element.15, pred[16,128]{1,0:T(8,128)(4,1)S(1)} %get-tuple-element.14, f32[]{:T(128)} %bitcast.5, f32[]{:T(128)} %bitcast.4), kind=kLoop, calls=%fused_computation.53 | loop fusion | flops 10240 | bytes 20488 | tf_op jit(solution)/shard_map/add | solution.py:291
  (39 shorter events, 3.7 us)
Async XLA Ops:
  1.8 7.5 %collective-permute-start = (f32[19,4,1,128]{3,2,1,0:T(1,128)S(1)}, f32[19,4,1,128]{3,2,1,0:T(1,128)S(1)}, u32[]{:S(2)}, u32[]{:S(2)}) collective-permute-start(f32[19,4,1,128]{3,2,1,0:T(1,128)S(1)} %get-tuple-element.25), channel_id=1, source_target_pairs={{0,32},{32,64},{64,96},{96,128},{128,160},{160,192},{192,224},{224... | collective-permute-start | bytes 116744 | tf_op jit(solution)/shard_map/ppermute | solution.py:99
  3.7 6.5 %collective-permute-start.1 = (f32[19,4,1,128]{3,2,1,0:T(1,128)S(1)}, f32[19,4,1,128]{3,2,1,0:T(1,128)S(1)}, u32[]{:S(2)}, u32[]{:S(2)}) collective-permute-start(f32[19,4,1,128]{3,2,1,0:T(1,128)S(1)} %get-tuple-element.26), channel_id=1, source_target_pairs={{32,0},{64,32},{96,64},{128,96},{160,128},{192,160},{224,192},{256... | collective-permute-start | bytes 116744 | tf_op jit(solution)/shard_map/ppermute | solution.py:100
  11.7 14.3 %copy-start.3 = (s32[4,16,128]{2,1,0:T(8,128)S(1)}, s32[4,16,128]{2,1,0:T(8,128)}, u32[]{:S(2)}) copy-start(s32[4,16,128]{2,1,0:T(8,128)} %param.7) | copy-start | bytes 98308
  11.7 21.4 %copy-start = (f32[19,4,16,128]{3,2,1,0:T(8,128)S(1)}, f32[19,4,16,128]{3,2,1,0:T(8,128)}, u32[]{:S(2)}) copy-start(f32[19,4,16,128]{3,2,1,0:T(8,128)} %param.5) | copy-start | bytes 1867780
  12.4 14.4 %collective-permute-start.3 = (f32[19,4,18,1]{0,1,3,2:T(4,128)S(1)}, f32[19,4,18,1]{0,1,3,2:T(4,128)S(1)}, u32[]{:S(2)}, u32[]{:S(2)}) collective-permute-start(f32[19,4,18,1]{0,1,3,2:T(4,128)S(1)} %copy.8), channel_id=1, source_target_pairs={{1,0},{2,1},{3,2},{4,3},{5,4},{6,5},{7,6},{8,7},{9,8},{10,9},{11,1... | collective-permute-start | bytes 16424 | tf_op jit(solution)/shard_map/ppermute | solution.py:100
  24.2 8.0 %collective-permute-start.2 = (f32[19,4,18,1]{0,1,3,2:T(4,128)S(1)}, f32[19,4,18,1]{0,1,3,2:T(4,128)S(1)}, u32[]{:S(2)}, u32[]{:S(2)}) collective-permute-start(f32[19,4,18,1]{0,1,3,2:T(4,128)S(1)} %copy.7), channel_id=1, source_target_pairs={{0,1},{1,2},{2,3},{3,4},{4,5},{5,6},{6,7},{7,8},{8,9},{9,10},{10,1... | collective-permute-start | bytes 16424 | tf_op jit(solution)/shard_map/ppermute | solution.py:99
  50.4 6.8 %collective-permute-start.4 = (f32[19,4,1,128]{3,2,1,0:T(1,128)S(1)}, f32[19,4,1,128]{3,2,1,0:T(1,128)S(1)}, u32[]{:S(2)}, u32[]{:S(2)}) collective-permute-start(f32[19,4,1,128]{3,2,1,0:T(1,128)S(1)} %get-tuple-element.23), channel_id=1, source_target_pairs={{0,32},{32,64},{64,96},{96,128},{128,160},{160,192},{192,224},{224... | collective-permute-start | bytes 116744 | tf_op jit(solution)/shard_map/ppermute | solution.py:99
  52.3 6.5 %collective-permute-start.5 = (f32[19,4,1,128]{3,2,1,0:T(1,128)S(1)}, f32[19,4,1,128]{3,2,1,0:T(1,128)S(1)}, u32[]{:S(2)}, u32[]{:S(2)}) collective-permute-start(f32[19,4,1,128]{3,2,1,0:T(1,128)S(1)} %get-tuple-element.24), channel_id=1, source_target_pairs={{32,0},{64,32},{96,64},{128,96},{160,128},{192,160},{224,192},{256... | collective-permute-start | bytes 116744 | tf_op jit(solution)/shard_map/ppermute | solution.py:100
  60.3 11.8 %copy-start.1 = (f32[19,4,16,128]{3,2,1,0:T(8,128)S(1)}, f32[19,4,16,128]{3,2,1,0:T(8,128)}, u32[]{:S(2)}) copy-start(f32[19,4,16,128]{3,2,1,0:T(8,128)} %get-tuple-element.6) | copy-start | bytes 1867780
  61.0 8.6 %collective-permute-start.6 = (f32[19,4,18,1]{0,1,3,2:T(4,128)S(1)}, f32[19,4,18,1]{0,1,3,2:T(4,128)S(1)}, u32[]{:S(2)}, u32[]{:S(2)}) collective-permute-start(f32[19,4,18,1]{0,1,3,2:T(4,128)S(1)} %copy.11), channel_id=1, source_target_pairs={{0,1},{1,2},{2,3},{3,4},{4,5},{5,6},{6,7},{7,8},{8,9},{9,10},{10,1... | collective-permute-start | bytes 16424 | tf_op jit(solution)/shard_map/ppermute | solution.py:99
  63.5 7.6 %collective-permute-start.7 = (f32[19,4,18,1]{0,1,3,2:T(4,128)S(1)}, f32[19,4,18,1]{0,1,3,2:T(4,128)S(1)}, u32[]{:S(2)}, u32[]{:S(2)}) collective-permute-start(f32[19,4,18,1]{0,1,3,2:T(4,128)S(1)} %copy.12), channel_id=1, source_target_pairs={{1,0},{2,1},{3,2},{4,3},{5,4},{6,5},{7,6},{8,7},{9,8},{10,9},{11,1... | collective-permute-start | bytes 16424 | tf_op jit(solution)/shard_map/ppermute | solution.py:100
  74.6 13.7 %copy-start.4 = (f32[16,128]{1,0:T(8,128)S(1)}, f32[16,128]{1,0:T(8,128)}, u32[]{:S(2)}) copy-start(f32[16,128]{1,0:T(8,128)} %get-tuple-element.8) | copy-start | bytes 24580
  74.6 32.7 %copy-start.2 = (s32[16,128]{1,0:T(8,128)S(1)}, s32[16,128]{1,0:T(8,128)}, u32[]{:S(2)}) copy-start(s32[16,128]{1,0:T(8,128)} %param.8) | copy-start | bytes 24580
  89.0 6.8 %collective-permute-start.8 = (f32[4,128]{1,0:T(4,128)S(1)}, f32[4,128]{1,0:T(4,128)S(1)}, u32[]{:S(2)}, u32[]{:S(2)}) collective-permute-start(f32[4,128]{1,0:T(4,128)S(1)} %get-tuple-element.34), channel_id=1, source_target_pairs={{0,32},{32,64},{64,96},{96,128},{128,160},{160,192},{192,224},{224... | collective-permute-start | bytes 6152 | tf_op jit(solution)/shard_map/ppermute | solution.py:99
  90.9 6.1 %collective-permute-start.9 = (f32[4,128]{1,0:T(4,128)S(1)}, f32[4,128]{1,0:T(4,128)S(1)}, u32[]{:S(2)}, u32[]{:S(2)}) collective-permute-start(f32[4,128]{1,0:T(4,128)S(1)} %get-tuple-element.35), channel_id=1, source_target_pairs={{32,0},{64,32},{96,64},{128,96},{160,128},{192,160},{224,192},{256... | collective-permute-start | bytes 6152 | tf_op jit(solution)/shard_map/ppermute | solution.py:100
  97.1 8.3 %collective-permute-start.10 = (f32[24,4]{1,0:T(8,128)S(1)}, f32[24,4]{1,0:T(8,128)S(1)}, u32[]{:S(2)}, u32[]{:S(2)}) collective-permute-start(f32[24,4]{1,0:T(8,128)S(1)} %get-tuple-element.32), channel_id=1, source_target_pairs={{0,1},{1,2},{2,3},{3,4},{4,5},{5,6},{6,7},{7,8},{8,9},{9,10},{10,1... | collective-permute-start | bytes 1160 | tf_op jit(solution)/shard_map/ppermute | solution.py:99
  99.0 7.7 %collective-permute-start.11 = (f32[24,4]{1,0:T(8,128)S(1)}, f32[24,4]{1,0:T(8,128)S(1)}, u32[]{:S(2)}, u32[]{:S(2)}) collective-permute-start(f32[24,4]{1,0:T(8,128)S(1)} %get-tuple-element.33), channel_id=1, source_target_pairs={{1,0},{2,1},{3,2},{4,3},{5,4},{6,5},{7,6},{8,7},{9,8},{10,9},{11,1... | collective-permute-start | bytes 1160 | tf_op jit(solution)/shard_map/ppermute | solution.py:100
  136.2 5.5 %collective-permute-start.12 = (f32[4]{0:T(128)S(1)}, f32[4]{0:T(128)S(1)}, u32[]{:S(2)}, u32[]{:S(2)}) collective-permute-start(f32[4]{0:T(128)S(1)} %psum.7), channel_id=1, source_target_pairs={{0,1},{1,0},{2,3},{3,2},{4,5},{5,4},{6,7},{7,6},{8,9},{9,8},{10,11... | collective-permute-start | bytes 56 | tf_op jit(solution)/shard_map/ppermute | solution.py:111
  141.7 6.3 %collective-permute-start.13 = (f32[4]{0:T(128)S(1)}, f32[4]{0:T(128)S(1)}, u32[]{:S(2)}, u32[]{:S(2)}) collective-permute-start(f32[4]{0:T(128)S(1)} %add.116), channel_id=1, source_target_pairs={{0,2},{1,3},{2,0},{3,1},{4,6},{5,7},{6,4},{7,5},{8,10},{9,11},{10,... | collective-permute-start | bytes 56 | tf_op jit(solution)/shard_map/ppermute | solution.py:111
  148.0 9.4 %collective-permute-start.14 = (f32[4]{0:T(128)S(1)}, f32[4]{0:T(128)S(1)}, u32[]{:S(2)}, u32[]{:S(2)}) collective-permute-start(f32[4]{0:T(128)S(1)} %add.117), channel_id=1, source_target_pairs={{0,4},{1,5},{2,6},{3,7},{4,0},{5,1},{6,2},{7,3},{8,12},{9,13},{10,... | collective-permute-start | bytes 56 | tf_op jit(solution)/shard_map/ppermute | solution.py:111
  157.4 5.5 %collective-permute-start.15 = (f32[4]{0:T(128)S(1)}, f32[4]{0:T(128)S(1)}, u32[]{:S(2)}, u32[]{:S(2)}) collective-permute-start(f32[4]{0:T(128)S(1)} %add.118), channel_id=1, source_target_pairs={{0,8},{1,9},{2,10},{3,11},{4,12},{5,13},{6,14},{7,15},{8,0},{9,1},... | collective-permute-start | bytes 56 | tf_op jit(solution)/shard_map/ppermute | solution.py:111
  162.8 7.0 %collective-permute-start.16 = (f32[4]{0:T(128)S(1)}, f32[4]{0:T(128)S(1)}, u32[]{:S(2)}, u32[]{:S(2)}) collective-permute-start(f32[4]{0:T(128)S(1)} %add.119), channel_id=1, source_target_pairs={{0,16},{1,17},{2,18},{3,19},{4,20},{5,21},{6,22},{7,23},{8,24},{9,... | collective-permute-start | bytes 56 | tf_op jit(solution)/shard_map/ppermute | solution.py:111

commit v5 on v3

--- a/solution.py
+++ b/solution.py
@@ -91,15 +91,33 @@
 
 
 def halo(cells, w):
+    return halo_many([cells], [w])[0]
+
+
+def halo_many(arrays, widths):
     for axis, dim in (("gx", -2), ("gy", -1)):
         count = lax.axis_size(axis)
-        size = cells.shape[dim]
-        head = lax.slice_in_dim(cells, 0, w, axis=cells.ndim + dim)
-        tail = lax.slice_in_dim(cells, size - w, size, axis=cells.ndim + dim)
-        low = lax.ppermute(tail, axis, [(i, i + 1) for i in range(count - 1)])
-        high = lax.ppermute(head, axis, [(i + 1, i) for i in range(count - 1)])
-        cells = jnp.concatenate([low, cells, high], axis=dim)
-    return cells
+        heads, tails = [], []
+        for a, w in zip(arrays, widths):
+            size = a.shape[dim]
+            heads.append(lax.slice_in_dim(a, 0, w, axis=a.ndim + dim))
+            tails.append(lax.slice_in_dim(a, size - w, size, axis=a.ndim + dim))
+
+        def send(pieces, pairs):
+            if len(pieces) == 1:
+                return [lax.ppermute(pieces[0], axis, pairs)]
+            flat = jnp.concatenate([p.reshape(-1) for p in pieces])
+            got = lax.ppermute(flat, axis, pairs)
+            out, at = [], 0
+            for p in pieces:
+                out.append(got[at : at + p.size].reshape(p.shape))
+                at += p.size
+            return out
+
+        lows = send(tails, [(i, i + 1) for i in range(count - 1)])
+        highs = send(heads, [(i + 1, i) for i in range(count - 1)])
+        arrays = [jnp.concatenate([lo, a, hi], axis=dim) for lo, a, hi in zip(lows, arrays, highs)]
+    return arrays
 
 
 def global_sum(values):
@@ -225,13 +243,13 @@
 
 
 def adjoint_step(section, pulled, forward_pops, blocking, lever):
-    _, planes, width_x, width_y = pulled.shape
+    planes, width_x, width_y = blocking.shape
     rows = 8 if width_x % 8 == 0 else width_x
     vmem = pl.BlockSpec(memory_space=pltpu.VMEM)
     return pl.pallas_call(
         functools.partial(step_kernel, section, rows),
         out_shape=(
-            jax.ShapeDtypeStruct(pulled.shape, jnp.float32),
+            jax.ShapeDtypeStruct((19, planes, width_x, width_y), jnp.float32),
             jax.ShapeDtypeStruct((width_x, width_y), jnp.float32),
         ),
         in_specs=[vmem] * 4,
@@ -258,6 +276,11 @@
     return smooth[w:-w, w:-w]
 
 
+def pad_to(a, rows, cols):
+    pad = [(0, 0)] * (a.ndim - 2) + [(0, rows - a.shape[-2]), (0, cols - a.shape[-1])]
+    return jnp.pad(a, pad)
+
+
 def per_device(adjoint_in, forward_pops, solid_mask, region_label, design):
     planes, width_x, width_y = solid_mask.shape
     inside = region_label > 0
@@ -265,13 +288,31 @@
         solid_mask == 1, 1.0, jnp.where(inside[None], BLOCK_LIMIT * design[None], 0.0)
     ).astype(jnp.float32)
     lever = jnp.where((solid_mask == 0) & inside[None], BLOCK_LIMIT, 0.0).astype(jnp.float32)
-    adjoint = adjoint_in
-    raw = jnp.zeros((width_x, width_y), jnp.float32)
-    for section in (1, 0):
-        pulled = pull_back(halo(adjoint, 1), width_x, width_y)
-        adjoint, term = adjoint_step(section, pulled, forward_pops, blocking, lever)
-        raw = raw + term
-    raw = SENSE_SCALE * raw
+    saved_one = forward_pops[1].astype(jnp.float32)
+    adj_ext, saved_ext, block_ext = halo_many([adjoint_in, saved_one, blocking], [2, 1, 1])
+    ext_x, ext_y = width_x + 2, width_y + 2
+    rows = -(-ext_x // 8) * 8
+    cols = -(-ext_y // 128) * 128
+    pulled = pad_to(pull_back(adj_ext, ext_x, ext_y), rows, cols)
+    first, term_ext = adjoint_step(
+        0,
+        pulled,
+        pad_to(saved_ext, rows, cols)[None],
+        pad_to(block_ext, rows, cols),
+        pad_to(jnp.pad(lever, ((0, 0), (1, 1), (1, 1))), rows, cols),
+    )
+    gxi = lax.axis_index("gx")
+    gyi = lax.axis_index("gy")
+    nx = lax.axis_size("gx")
+    ny = lax.axis_size("gy")
+    xs = gxi * width_x - 1 + lax.broadcasted_iota(jnp.int32, (ext_x, ext_y), 0)
+    ys = gyi * width_y - 1 + lax.broadcasted_iota(jnp.int32, (ext_x, ext_y), 1)
+    in_grid = (xs >= 0) & (xs < nx * width_x) & (ys >= 0) & (ys < ny * width_y)
+    first = jnp.where(in_grid, first[:, :, :ext_x, :ext_y], 0.0)
+    term_one = term_ext[1 : 1 + width_x, 1 : 1 + width_y]
+    pulled = pull_back(first, width_x, width_y)
+    adjoint, term_two = adjoint_step(0, pulled, forward_pops, blocking, lever)
+    raw = SENSE_SCALE * (term_one + term_two)
     smooth = helmholtz(raw, SWEEPS)
     region_one = (region_label == 1).astype(jnp.float32)
     region_two = (region_label == 2).astype(jnp.float32)

time: 158 us -> 141 us (0.89)
  waiting for transfers between devices: 36.8 us -> 23.3 us
  local copies, waits for them, and re-layouts: 20.8 us -> 12.3 us
  other arithmetic: 9.23 us -> 16.3 us
  starting transfers between devices: 56.1 us -> 50.3 us
  Pallas kernels: 7.21 us -> 11.2 us
    ppermute x12 -> x8, starting transfers between devices: 44.9 us -> 34.9 us  [the longest x4 19.9 us: send(): got = lax.ppermute(flat, axis, pairs)]
    ppermute x12 -> x8, waiting for transfers between devices: 14.4 us -> 5.24 us  [the longest x4 2.67 us: send(): got = lax.ppermute(flat, axis, pairs)]
    unnamed x22 -> x21, local copies, waits for them, and re-layouts: 6.22 us -> 1.95 us
    ppermute x5, starting transfers between devices: 11.2 us -> 15.4 us  [global_sum(): lax.ppermute(values, 'gy', [(i, i ^ 1 << k) for i in range(ny)])]
    ppermute x5, waiting for transfers between devices: 22.4 us -> 18.1 us  [global_sum(): lax.ppermute(values, 'gy', [(i, i ^ 1 << k) for i in range(ny)])]
    ppermute x4 -> x0, local copies, waits for them, and re-layouts: 4.18 us -> none  [the longest x2 2.1 us: halo(): high = lax.ppermute(head, axis, [(i + 1, i) for i in range(count - 1)])]
    concatenate x2, local copies, waits for them, and re-layouts: 4.33 us -> 0.15 us  [send(): flat = jnp.concatenate([p.reshape(-1) for p in pieces])]
    pallas_call x2, Pallas kernels: 7.21 us -> 11.2 us  [adjoint_step(): pl.pallas_call(functools.partial(step_kernel, section, rows), out_shape=(...]
  transfers between devices with their start and end apart: 17 -> 13, of which waited for: 10 -> 10; matrix products, arithmetic and copies ran while one was open for 7% -> 1% of each run, Pallas kernels for 0% -> 0%
where the time goes in v5:
time: 141 us; the launch traced here: 140 us
  starting transfers between devices  50.3 us (36%)
  blocking collectives  25.6 us (18%)
  waiting for transfers between devices  23.3 us (17%)
  other arithmetic  16.3 us (12%)
  local copies, waits for them, and re-layouts  12.3 us (9%)
  Pallas kernels  11.2 us (8%)
    psum x1, blocking collectives, global_sum(): values = lax.psum(values, 'gx')  25.6 us
    ppermute x4, starting transfers between devices, send(): got = lax.ppermute(flat, axis, pairs)  19.9 us
    ppermute x5, waiting for transfers between devices, global_sum(): lax.ppermute(values, 'gy', [(i, i ^ 1 << k) for i in range(ny)])  18.1 us
    ppermute x5, starting transfers between devices, global_sum(): lax.ppermute(values, 'gy', [(i, i ^ 1 << k) for i in range(ny)])  15.4 us
    ppermute x4, starting transfers between devices, send(): return [lax.ppermute(pieces[0], axis, pairs)]  15 us
    pallas_call x2, Pallas kernels, adjoint_step(): pl.pallas_call(functools.partial(step_kernel, section, rows), out_shape=(...  11.2 us
  transfers between devices with their start and end apart: 13, of which 10 were waited for; matrix products, arithmetic and copies ran while one was open for 1% of the time, Pallas kernels for 0%

profile of v5, /device:TPU:38, one launch (start us, length us, event | category | flops | bytes accessed | tf_op | source)
XLA Modules:
  0.0 140.3 jit_solution(14235743265480219936)
XLA Ops:
  0.6 0.8 multiply_select_fusion
  1.4 0.8 and_select_fusion
  2.2 1.0 bitcast_convert_fusion
  3.5 1.1 fusion.63
  4.7 1.9 %collective-permute-start = (f32[29696]{0:T(1024)S(1)}, f32[29696]{0:T(1024)S(1)}, u32[]{:S(2)}, u32[]{:S(2)}) collective-permute-start(f32[29696]{0:T(1024)S(1)} %pad_maximum_fusion.2), channel_id=1, source_target_pairs={{0,32},{32,64},{64,96},{96,128},{128,160},{160,192},{192,224},{224... | collective-permute-start | bytes 356360 | tf_op jit(solution)/shard_map/ppermute | solution.py:110
  6.6 4.9 %collective-permute-start.1 = (f32[29696]{0:T(1024)S(1)}, f32[29696]{0:T(1024)S(1)}, u32[]{:S(2)}, u32[]{:S(2)}) collective-permute-start(f32[29696]{0:T(1024)S(1)} %pad_maximum_fusion.3), channel_id=1, source_target_pairs={{32,0},{64,32},{96,64},{128,96},{160,128},{192,160},{224,192},{256... | collective-permute-start | bytes 356360 | tf_op jit(solution)/shard_map/ppermute | solution.py:110
  11.6 0.4 collective-permute-done
  12.0 1.8 %collective-permute-done.1 = f32[29696]{0:T(1024)S(1)} collective-permute-done((f32[29696]{0:T(1024)S(1)}, f32[29696]{0:T(1024)S(1)}, u32[]{:S(2)}, u32[]{:S(2)}) %collective-permute-start.1) | collective-permute-done | bytes 118816 | tf_op jit(solution)/shard_map/ppermute | solution.py:110
  13.9 0.6 copy-done.4
  14.7 0.3 fusion.62
  15.3 0.7 slice.771
  16.3 0.8 slice.768
  17.3 0.9 slice_reduce_fusion.1
  18.4 4.3 %collective-permute-start.2 = (f32[4480]{0:T(1024)S(1)}, f32[4480]{0:T(1024)S(1)}, u32[]{:S(2)}, u32[]{:S(2)}) collective-permute-start(f32[4480]{0:T(1024)S(1)} %concatenate.119), channel_id=1, source_target_pairs={{0,1},{1,2},{2,3},{3,4},{4,5},{5,6},{6,7},{7,8},{8,9},{9,10},{10,1... | collective-permute-start | bytes 53768 | tf_op jit(solution)/shard_map/ppermute | solution.py:110
  23.3 8.8 %collective-permute-start.3 = (f32[4480]{0:T(1024)S(1)}, f32[4480]{0:T(1024)S(1)}, u32[]{:S(2)}, u32[]{:S(2)}) collective-permute-start(f32[4480]{0:T(1024)S(1)} %concatenate.120), channel_id=1, source_target_pairs={{1,0},{2,1},{3,2},{4,3},{5,4},{6,5},{7,6},{8,7},{9,8},{10,9},{11,1... | collective-permute-start | bytes 53768 | tf_op jit(solution)/shard_map/ppermute | solution.py:110
  32.2 0.7 pad.271.l_ref
  33.2 0.4 collective-permute-done.3
  35.8 1.4 %pad.31.g_ref = f32[19,4,24,256]{3,2,1,0:T(8,128)} pad(f32[19,4,18,130]{3,2,1,0:T(8,128)S(1)} %fusion.28, f32[]{:T(128)} %constant.55.clone.1), padding=0_0x0_0x0_6x0_126 | pad | bytes 2579140 | tf_op jit(solution)/shard_map/jit(_pad)/pad | solution.py:281
  37.3 0.3 reshape.193
  37.7 0.3 reshape.194
  38.5 2.4 %fusion.f_ref = f32[1,19,4,24,256]{4,3,2,1,0:T(8,128)} fusion(f32[19,4,18,1]{3,2,1,0:T(8,128)S(1)} %reshape.194, f32[19,4,18,1]{3,2,1,0:T(8,128)S(1)} %reshape.193, f32[19,4,1,128]{3,2,1,0:T(1,128)S(1)} %slice.619, f32[19,4,16,128]{3,2,1,0:T(8,128)S(1)} %bitcast_convert_fusion, f32[19,4,1,128]{3,2,1,0:T(1,128)S(1)} %slice.617), kind=kLoop, calls=%fused_computation.1 | loop fusion | flops 7938048 | bytes 2579136 | tf_op jit(solution)/shard_map/broadcast_in_dim | solution.py:300
  40.9 0.8 select_maximum_fusion.2.b_ref
  41.7 7.6 %shard_map.68 = (f32[19,4,24,256]{3,2,1,0:T(8,128)}, f32[24,256]{1,0:T(8,128)}) custom-call(f32[19,4,24,256]{3,2,1,0:T(8,128)} %pad.31.g_ref, f32[1,19,4,24,256]{4,3,2,1,0:T(8,128)} %fusion.f_ref, f32[4,24,256]{2,1,0:T(8,128)} %select_maximum_fusion.2.b_ref, f32[4,24,256]{2,1,0:T(8,128)} %pad.271.l_ref), custom_call_target="tpu_custom_call" | custom-call | tf_op jit(solution)/shard_map/pallas_call | solution.py:249
  49.3 1.7 %slice_select_fusion = f32[19,4,18,130]{3,2,1,0:T(8,128)S(1)} fusion(f32[19,4,24,256]{3,2,1,0:T(8,128)} %get-tuple-element.6, pred[18,130]{1,0:T(8,128)(4,1)S(1)} %and_and_fusion.1), kind=kLoop, calls=%fused_computation.14 | loop fusion | flops 177840 | bytes 1425060 | tf_op jit(solution)/shard_map/jit(_where)/select_n | solution.py:311
  51.8 0.8 copy-done.1
  52.6 3.6 %shard_map.69 = (f32[19,4,16,128]{3,2,1,0:T(8,128)}, f32[16,128]{1,0:T(8,128)}) custom-call(f32[19,4,16,128]{3,2,1,0:T(8,128)} %copy-done.1, bf16[2,19,4,16,128]{4,3,2,1,0:T(8,128)(2,1)} %f_ref.1, f32[4,16,128]{2,1,0:T(8,128)} %copy-done.2, f32[4,16,128]{2,1,0:T(8,128)} %copy-done.3), custom_call_target="tpu_custom_call" | custom-call | tf_op jit(solution)/shard_map/pallas_call | solution.py:249
  56.2 0.8 add_multiply_fusion
  57.1 1.9 %collective-permute-start.4 = (f32[4,128]{1,0:T(4,128)S(1)}, f32[4,128]{1,0:T(4,128)S(1)}, u32[]{:S(2)}, u32[]{:S(2)}) collective-permute-start(f32[4,128]{1,0:T(4,128)S(1)} %get-tuple-element.82), channel_id=1, source_target_pairs={{0,32},{32,64},{64,96},{96,128},{128,160},{160,192},{192,224},{224... | collective-permute-start | bytes 6152 | tf_op jit(solution)/shard_map/ppermute | solution.py:108
  59.0 4.9 %collective-permute-start.5 = (f32[4,128]{1,0:T(4,128)S(1)}, f32[4,128]{1,0:T(4,128)S(1)}, u32[]{:S(2)}, u32[]{:S(2)}) collective-permute-start(f32[4,128]{1,0:T(4,128)S(1)} %get-tuple-element.83), channel_id=1, source_target_pairs={{32,0},{64,32},{96,64},{128,96},{160,128},{192,160},{224,192},{256... | collective-permute-start | bytes 6152 | tf_op jit(solution)/shard_map/ppermute | solution.py:108
  63.9 1.3 collective-permute-done.5
  65.2 1.9 %collective-permute-start.6 = (f32[24,4]{1,0:T(8,128)S(1)}, f32[24,4]{1,0:T(8,128)S(1)}, u32[]{:S(2)}, u32[]{:S(2)}) collective-permute-start(f32[24,4]{1,0:T(8,128)S(1)} %get-tuple-element.80), channel_id=1, source_target_pairs={{0,1},{1,2},{2,3},{3,4},{4,5},{5,6},{6,7},{7,8},{8,9},{9,10},{10,1... | collective-permute-start | bytes 1160 | tf_op jit(solution)/shard_map/ppermute | solution.py:108
  67.1 6.3 %collective-permute-start.7 = (f32[24,4]{1,0:T(8,128)S(1)}, f32[24,4]{1,0:T(8,128)S(1)}, u32[]{:S(2)}, u32[]{:S(2)}) collective-permute-start(f32[24,4]{1,0:T(8,128)S(1)} %get-tuple-element.81), channel_id=1, source_target_pairs={{1,0},{2,1},{3,2},{4,3},{5,4},{6,5},{7,6},{8,7},{9,8},{10,9},{11,1... | collective-permute-start | bytes 1160 | tf_op jit(solution)/shard_map/ppermute | solution.py:108
  73.5 1.3 collective-permute-done.7
  75.3 0.8 select_reduce_fusion.1
  76.1 2.5 %pad_maximum_fusion.17 = f32[4]{0:T(128)S(1)} fusion(f32[1]{0:T(128)} %bitcast.74, f32[1]{0:T(128)} %bitcast.73, f32[1]{0:T(128)} %bitcast.72, f32[1]{0:T(128)} %bitcast.71), kind=kLoop, calls=%fused_computation.216 | loop fusion | flops 12 | bytes 32 | tf_op jit(solution)/shard_map/stack | solution.py:319
  78.6 25.6 %psum.7 = f32[4]{0:T(128)S(1)} all-reduce(f32[4]{0:T(128)S(1)} %pad_maximum_fusion.17), channel_id=1, replica_groups=mesh['gx'=16,'gy'=32] {'gx'}, use_global_device_ids=true, to_apply=%region_4.5 | all-reduce | flops 4 | bytes 32 | tf_op jit(solution)/shard_map/psum | solution.py:124
  104.2 2.3 %collective-permute-start.8 = (f32[4]{0:T(128)S(1)}, f32[4]{0:T(128)S(1)}, u32[]{:S(2)}, u32[]{:S(2)}) collective-permute-start(f32[4]{0:T(128)S(1)} %psum.7), channel_id=1, source_target_pairs={{0,1},{1,0},{2,3},{3,2},{4,5},{5,4},{6,7},{7,6},{8,9},{9,8},{10,11... | collective-permute-start | bytes 56 | tf_op jit(solution)/shard_map/ppermute | solution.py:129
  106.6 3.1 %collective-permute-done.8 = f32[4]{0:T(128)S(1)} collective-permute-done((f32[4]{0:T(128)S(1)}, f32[4]{0:T(128)S(1)}, u32[]{:S(2)}, u32[]{:S(2)}) %collective-permute-start.8) | collective-permute-done | bytes 48 | tf_op jit(solution)/shard_map/ppermute | solution.py:129
  109.7 3.5 %collective-permute-start.9 = (f32[4]{0:T(128)S(1)}, f32[4]{0:T(128)S(1)}, u32[]{:S(2)}, u32[]{:S(2)}) collective-permute-start(f32[4]{0:T(128)S(1)} %add.146), channel_id=1, source_target_pairs={{0,2},{1,3},{2,0},{3,1},{4,6},{5,7},{6,4},{7,5},{8,10},{9,11},{10,... | collective-permute-start | bytes 56 | tf_op jit(solution)/shard_map/ppermute | solution.py:129
  113.2 2.8 %collective-permute-done.9 = f32[4]{0:T(128)S(1)} collective-permute-done((f32[4]{0:T(128)S(1)}, f32[4]{0:T(128)S(1)}, u32[]{:S(2)}, u32[]{:S(2)}) %collective-permute-start.9) | collective-permute-done | bytes 48 | tf_op jit(solution)/shard_map/ppermute | solution.py:129
  116.0 4.1 %collective-permute-start.10 = (f32[4]{0:T(128)S(1)}, f32[4]{0:T(128)S(1)}, u32[]{:S(2)}, u32[]{:S(2)}) collective-permute-start(f32[4]{0:T(128)S(1)} %add.147), channel_id=1, source_target_pairs={{0,4},{1,5},{2,6},{3,7},{4,0},{5,1},{6,2},{7,3},{8,12},{9,13},{10,... | collective-permute-start | bytes 56 | tf_op jit(solution)/shard_map/ppermute | solution.py:129
  120.2 5.2 %collective-permute-done.10 = f32[4]{0:T(128)S(1)} collective-permute-done((f32[4]{0:T(128)S(1)}, f32[4]{0:T(128)S(1)}, u32[]{:S(2)}, u32[]{:S(2)}) %collective-permute-start.10) | collective-permute-done | bytes 48 | tf_op jit(solution)/shard_map/ppermute | solution.py:129
  125.4 2.4 %collective-permute-start.11 = (f32[4]{0:T(128)S(1)}, f32[4]{0:T(128)S(1)}, u32[]{:S(2)}, u32[]{:S(2)}) collective-permute-start(f32[4]{0:T(128)S(1)} %add.148), channel_id=1, source_target_pairs={{0,8},{1,9},{2,10},{3,11},{4,12},{5,13},{6,14},{7,15},{8,0},{9,1},... | collective-permute-start | bytes 56 | tf_op jit(solution)/shard_map/ppermute | solution.py:129
  127.8 3.0 %collective-permute-done.11 = f32[4]{0:T(128)S(1)} collective-permute-done((f32[4]{0:T(128)S(1)}, f32[4]{0:T(128)S(1)}, u32[]{:S(2)}, u32[]{:S(2)}) %collective-permute-start.11) | collective-permute-done | bytes 48 | tf_op jit(solution)/shard_map/ppermute | solution.py:129
  130.8 3.0 %collective-permute-start.12 = (f32[4]{0:T(128)S(1)}, f32[4]{0:T(128)S(1)}, u32[]{:S(2)}, u32[]{:S(2)}) collective-permute-start(f32[4]{0:T(128)S(1)} %add.149), channel_id=1, source_target_pairs={{0,16},{1,17},{2,18},{3,19},{4,20},{5,21},{6,22},{7,23},{8,24},{9,... | collective-permute-start | bytes 56 | tf_op jit(solution)/shard_map/ppermute | solution.py:129
  133.9 3.9 %collective-permute-done.12 = f32[4]{0:T(128)S(1)} collective-permute-done((f32[4]{0:T(128)S(1)}, f32[4]{0:T(128)S(1)}, u32[]{:S(2)}, u32[]{:S(2)}) %collective-permute-start.12) | collective-permute-done | bytes 48 | tf_op jit(solution)/shard_map/ppermute | solution.py:129
  137.9 0.6 fusion.67
  138.5 1.9 %select_add_fusion = f32[16,128]{1,0:T(8,128)} fusion(pred[16,128]{1,0:T(8,128)(4,1)S(1)} %get-tuple-element.22, f32[16,128]{1,0:T(8,128)S(1)} %get-tuple-element.21, pred[16,128]{1,0:T(8,128)(4,1)S(1)} %get-tuple-element.20, f32[]{:T(128)} %bitcast.76, f32[]{:T(128)} %bitcast.75), kind=kLoop, calls=%fused_computation.198 | loop fusion | flops 10240 | bytes 20488 | tf_op jit(solution)/shard_map/add | solution.py:329
  (113 shorter events, 6.5 us)
Async XLA Ops:
  0.6 13.9 %copy-start = (f32[19,4,16,128]{3,2,1,0:T(8,128)S(1)}, f32[19,4,16,128]{3,2,1,0:T(8,128)}, u32[]{:S(2)}) copy-start(f32[19,4,16,128]{3,2,1,0:T(8,128)} %param.5) | copy-start | bytes 1867780
  2.2 30.0 %copy-start.3 = (f32[4,16,128]{2,1,0:T(8,128)}, f32[4,16,128]{2,1,0:T(8,128)S(1)}, u32[]{:S(2)}) copy-start(f32[4,16,128]{2,1,0:T(8,128)S(1)} %get-tuple-element.73.l_ref) | copy-start | bytes 98308
  2.2 38.7 %copy-start.2 = (f32[4,16,128]{2,1,0:T(8,128)}, f32[4,16,128]{2,1,0:T(8,128)S(1)}, u32[]{:S(2)}) copy-start(f32[4,16,128]{2,1,0:T(8,128)S(1)} %get-tuple-element.74.b_ref) | copy-start | bytes 98308
  4.7 7.4 %collective-permute-start = (f32[29696]{0:T(1024)S(1)}, f32[29696]{0:T(1024)S(1)}, u32[]{:S(2)}, u32[]{:S(2)}) collective-permute-start(f32[29696]{0:T(1024)S(1)} %pad_maximum_fusion.2), channel_id=1, source_target_pairs={{0,32},{32,64},{64,96},{96,128},{128,160},{160,192},{192,224},{224... | collective-permute-start | bytes 356360 | tf_op jit(solution)/shard_map/ppermute | solution.py:110
  6.6 7.2 %collective-permute-start.1 = (f32[29696]{0:T(1024)S(1)}, f32[29696]{0:T(1024)S(1)}, u32[]{:S(2)}, u32[]{:S(2)}) collective-permute-start(f32[29696]{0:T(1024)S(1)} %pad_maximum_fusion.3), channel_id=1, source_target_pairs={{32,0},{64,32},{96,64},{128,96},{160,128},{192,160},{224,192},{256... | collective-permute-start | bytes 356360 | tf_op jit(solution)/shard_map/ppermute | solution.py:110
  13.9 0.6 copy-start.4
  18.4 14.5 %collective-permute-start.2 = (f32[4480]{0:T(1024)S(1)}, f32[4480]{0:T(1024)S(1)}, u32[]{:S(2)}, u32[]{:S(2)}) collective-permute-start(f32[4480]{0:T(1024)S(1)} %concatenate.119), channel_id=1, source_target_pairs={{0,1},{1,2},{2,3},{3,4},{4,5},{5,6},{6,7},{7,8},{8,9},{9,10},{10,1... | collective-permute-start | bytes 53768 | tf_op jit(solution)/shard_map/ppermute | solution.py:110
  23.3 10.3 %collective-permute-start.3 = (f32[4480]{0:T(1024)S(1)}, f32[4480]{0:T(1024)S(1)}, u32[]{:S(2)}, u32[]{:S(2)}) collective-permute-start(f32[4480]{0:T(1024)S(1)} %concatenate.120), channel_id=1, source_target_pairs={{1,0},{2,1},{3,2},{4,3},{5,4},{6,5},{7,6},{8,7},{9,8},{10,9},{11,1... | collective-permute-start | bytes 53768 | tf_op jit(solution)/shard_map/ppermute | solution.py:110
  51.1 24.3 %copy-start.5 = (s32[16,128]{1,0:T(8,128)S(1)}, s32[16,128]{1,0:T(8,128)}, u32[]{:S(2)}) copy-start(s32[16,128]{1,0:T(8,128)} %param.8) | copy-start | bytes 24580
  51.8 0.8 copy-start.1
  57.1 6.8 %collective-permute-start.4 = (f32[4,128]{1,0:T(4,128)S(1)}, f32[4,128]{1,0:T(4,128)S(1)}, u32[]{:S(2)}, u32[]{:S(2)}) collective-permute-start(f32[4,128]{1,0:T(4,128)S(1)} %get-tuple-element.82), channel_id=1, source_target_pairs={{0,32},{32,64},{64,96},{96,128},{128,160},{160,192},{192,224},{224... | collective-permute-start | bytes 6152 | tf_op jit(solution)/shard_map/ppermute | solution.py:108
  59.0 6.1 %collective-permute-start.5 = (f32[4,128]{1,0:T(4,128)S(1)}, f32[4,128]{1,0:T(4,128)S(1)}, u32[]{:S(2)}, u32[]{:S(2)}) collective-permute-start(f32[4,128]{1,0:T(4,128)S(1)} %get-tuple-element.83), channel_id=1, source_target_pairs={{32,0},{64,32},{96,64},{128,96},{160,128},{192,160},{224,192},{256... | collective-permute-start | bytes 6152 | tf_op jit(solution)/shard_map/ppermute | solution.py:108
  65.2 8.3 %collective-permute-start.6 = (f32[24,4]{1,0:T(8,128)S(1)}, f32[24,4]{1,0:T(8,128)S(1)}, u32[]{:S(2)}, u32[]{:S(2)}) collective-permute-start(f32[24,4]{1,0:T(8,128)S(1)} %get-tuple-element.80), channel_id=1, source_target_pairs={{0,1},{1,2},{2,3},{3,4},{4,5},{5,6},{6,7},{7,8},{8,9},{9,10},{10,1... | collective-permute-start | bytes 1160 | tf_op jit(solution)/shard_map/ppermute | solution.py:108
  67.1 7.7 %collective-permute-start.7 = (f32[24,4]{1,0:T(8,128)S(1)}, f32[24,4]{1,0:T(8,128)S(1)}, u32[]{:S(2)}, u32[]{:S(2)}) collective-permute-start(f32[24,4]{1,0:T(8,128)S(1)} %get-tuple-element.81), channel_id=1, source_target_pairs={{1,0},{2,1},{3,2},{4,3},{5,4},{6,5},{7,6},{8,7},{9,8},{10,9},{11,1... | collective-permute-start | bytes 1160 | tf_op jit(solution)/shard_map/ppermute | solution.py:108
  104.2 5.5 %collective-permute-start.8 = (f32[4]{0:T(128)S(1)}, f32[4]{0:T(128)S(1)}, u32[]{:S(2)}, u32[]{:S(2)}) collective-permute-start(f32[4]{0:T(128)S(1)} %psum.7), channel_id=1, source_target_pairs={{0,1},{1,0},{2,3},{3,2},{4,5},{5,4},{6,7},{7,6},{8,9},{9,8},{10,11... | collective-permute-start | bytes 56 | tf_op jit(solution)/shard_map/ppermute | solution.py:129
  109.7 6.3 %collective-permute-start.9 = (f32[4]{0:T(128)S(1)}, f32[4]{0:T(128)S(1)}, u32[]{:S(2)}, u32[]{:S(2)}) collective-permute-start(f32[4]{0:T(128)S(1)} %add.146), channel_id=1, source_target_pairs={{0,2},{1,3},{2,0},{3,1},{4,6},{5,7},{6,4},{7,5},{8,10},{9,11},{10,... | collective-permute-start | bytes 56 | tf_op jit(solution)/shard_map/ppermute | solution.py:129
  116.0 9.4 %collective-permute-start.10 = (f32[4]{0:T(128)S(1)}, f32[4]{0:T(128)S(1)}, u32[]{:S(2)}, u32[]{:S(2)}) collective-permute-start(f32[4]{0:T(128)S(1)} %add.147), channel_id=1, source_target_pairs={{0,4},{1,5},{2,6},{3,7},{4,0},{5,1},{6,2},{7,3},{8,12},{9,13},{10,... | collective-permute-start | bytes 56 | tf_op jit(solution)/shard_map/ppermute | solution.py:129
  125.4 5.5 %collective-permute-start.11 = (f32[4]{0:T(128)S(1)}, f32[4]{0:T(128)S(1)}, u32[]{:S(2)}, u32[]{:S(2)}) collective-permute-start(f32[4]{0:T(128)S(1)} %add.148), channel_id=1, source_target_pairs={{0,8},{1,9},{2,10},{3,11},{4,12},{5,13},{6,14},{7,15},{8,0},{9,1},... | collective-permute-start | bytes 56 | tf_op jit(solution)/shard_map/ppermute | solution.py:129
  130.8 7.0 %collective-permute-start.12 = (f32[4]{0:T(128)S(1)}, f32[4]{0:T(128)S(1)}, u32[]{:S(2)}, u32[]{:S(2)}) collective-permute-start(f32[4]{0:T(128)S(1)} %add.149), channel_id=1, source_target_pairs={{0,16},{1,17},{2,18},{3,19},{4,20},{5,21},{6,22},{7,23},{8,24},{9,... | collective-permute-start | bytes 56 | tf_op jit(solution)/shard_map/ppermute | solution.py:129

commit v6 on v5

--- a/solution.py
+++ b/solution.py
@@ -257,23 +257,28 @@
     )(pulled, forward_pops, blocking, lever)
 
 
-def helmholtz(raw, w):
-    scale_den = 1.0 + 4.0 * FILTER_WEIGHT
-    width_x, width_y = raw.shape
+def in_grid_mask(shape, w, width_x, width_y):
     nx = lax.axis_size("gx")
     ny = lax.axis_size("gy")
-    gxi = lax.axis_index("gx")
-    gyi = lax.axis_index("gy")
-    raw_ext = halo(raw, w)
-    xs = gxi * width_x - w + lax.broadcasted_iota(jnp.int32, raw_ext.shape, 0)
-    ys = gyi * width_y - w + lax.broadcasted_iota(jnp.int32, raw_ext.shape, 1)
-    valid = (xs >= 0) & (xs < nx * width_x) & (ys >= 0) & (ys < ny * width_y)
+    xs = lax.axis_index("gx") * width_x - w + lax.broadcasted_iota(jnp.int32, shape, 0)
+    ys = lax.axis_index("gy") * width_y - w + lax.broadcasted_iota(jnp.int32, shape, 1)
+    return (xs >= 0) & (xs < nx * width_x) & (ys >= 0) & (ys < ny * width_y)
+
+
+def sweeps(raw_ext, valid, w):
+    scale_den = 1.0 + 4.0 * FILTER_WEIGHT
     smooth = raw_ext
     for sweep in range(SWEEPS):
         framed = jnp.pad(smooth, 1)
         beside_all = framed[:-2, 1:-1] + framed[2:, 1:-1] + framed[1:-1, :-2] + framed[1:-1, 2:]
         smooth = jnp.where(valid, (raw_ext + FILTER_WEIGHT * beside_all) / scale_den, 0.0)
     return smooth[w:-w, w:-w]
+
+
+def helmholtz(raw, w):
+    width_x, width_y = raw.shape
+    raw_ext = halo(raw, w)
+    return sweeps(raw_ext, in_grid_mask(raw_ext.shape, w, width_x, width_y), w)
 
 
 def pad_to(a, rows, cols):
@@ -289,7 +294,14 @@
     ).astype(jnp.float32)
     lever = jnp.where((solid_mask == 0) & inside[None], BLOCK_LIMIT, 0.0).astype(jnp.float32)
     saved_one = forward_pops[1].astype(jnp.float32)
-    adj_ext, saved_ext, block_ext = halo_many([adjoint_in, saved_one, blocking], [2, 1, 1])
+    region_one = (region_label == 1).astype(jnp.float32)
+    region_two = (region_label == 2).astype(jnp.float32)
+    adj_ext, saved_ext, block_ext, one_ext, two_ext = halo_many(
+        [adjoint_in, saved_one, blocking, region_one, region_two], [2, 1, 1, SWEEPS, SWEEPS]
+    )
+    valid = in_grid_mask(one_ext.shape, SWEEPS, width_x, width_y)
+    weight_one = sweeps(one_ext, valid, SWEEPS)
+    weight_two = sweeps(two_ext, valid, SWEEPS)
     ext_x, ext_y = width_x + 2, width_y + 2
     rows = -(-ext_x // 8) * 8
     cols = -(-ext_y // 128) * 128
@@ -301,30 +313,22 @@
         pad_to(block_ext, rows, cols),
         pad_to(jnp.pad(lever, ((0, 0), (1, 1), (1, 1))), rows, cols),
     )
-    gxi = lax.axis_index("gx")
-    gyi = lax.axis_index("gy")
-    nx = lax.axis_size("gx")
-    ny = lax.axis_size("gy")
-    xs = gxi * width_x - 1 + lax.broadcasted_iota(jnp.int32, (ext_x, ext_y), 0)
-    ys = gyi * width_y - 1 + lax.broadcasted_iota(jnp.int32, (ext_x, ext_y), 1)
-    in_grid = (xs >= 0) & (xs < nx * width_x) & (ys >= 0) & (ys < ny * width_y)
+    in_grid = in_grid_mask((ext_x, ext_y), 1, width_x, width_y)
     first = jnp.where(in_grid, first[:, :, :ext_x, :ext_y], 0.0)
     term_one = term_ext[1 : 1 + width_x, 1 : 1 + width_y]
     pulled = pull_back(first, width_x, width_y)
     adjoint, term_two = adjoint_step(0, pulled, forward_pops, blocking, lever)
     raw = SENSE_SCALE * (term_one + term_two)
-    smooth = helmholtz(raw, SWEEPS)
-    region_one = (region_label == 1).astype(jnp.float32)
-    region_two = (region_label == 2).astype(jnp.float32)
     stats = jnp.stack(
         [
-            jnp.sum(smooth * region_one),
-            jnp.sum(smooth * region_two),
+            jnp.sum(weight_one * raw),
+            jnp.sum(weight_two * raw),
             jnp.sum(region_one),
             jnp.sum(region_two),
         ]
     )
     stats = global_sum(stats)
+    smooth = helmholtz(raw, SWEEPS)
     means = stats[:2] / jnp.maximum(stats[2:], 1.0)
     sensitivity = region_one * (smooth - means[0]) + region_two * (smooth - means[1])
     return (adjoint, sensitivity)

time: 141 us -> 145 us (1.028)
  starting transfers between devices: 50.3 us -> 38.8 us
  waiting for transfers between devices: 23.3 us -> 33.5 us
  other arithmetic: 16.3 us -> 19.4 us
  local copies, waits for them, and re-layouts: 12.3 us -> 14.1 us
    ppermute x4, waiting for transfers between devices: 2.67 us -> 7.94 us  [send(): got = lax.ppermute(flat, axis, pairs)]
    ppermute x4, starting transfers between devices: 15 us -> 10.1 us  [send(): return [lax.ppermute(pieces[0], axis, pairs)]]
    ppermute x5, waiting for transfers between devices: 18.1 us -> 22.4 us  [global_sum(): lax.ppermute(values, 'gy', [(i, i ^ 1 << k) for i in range(ny)])]
    ppermute x5, starting transfers between devices: 15.4 us -> 11.2 us  [global_sum(): lax.ppermute(values, 'gy', [(i, i ^ 1 << k) for i in range(ny)])]
    ppermute x4, starting transfers between devices: 19.9 us -> 17.5 us  [send(): got = lax.ppermute(flat, axis, pairs)]
    reduce_sum x1 -> x2, other arithmetic: 0.75 us -> 2.94 us  [the longest x1 1.54 us: per_device(): jnp.sum(weight_one * raw)]
    slice x8 -> x10, local copies, waits for them, and re-layouts: 2.82 us -> 3.02 us  [halo_many(): tails.append(lax.slice_in_dim(a, size - w, size, axis=a.ndim + dim))]
  transfers between devices with their start and end apart: 13 -> 13, of which waited for: 10 -> 8; matrix products, arithmetic and copies ran while one was open for 1% -> 5% of each run, Pallas kernels for 0% -> 0%
where the time goes in v6:
time: 145 us
  starting transfers between devices  38.8 us (27%)
  waiting for transfers between devices  33.5 us (23%)
  blocking collectives  26 us (18%)
  other arithmetic  19.4 us (13%)
  local copies, waits for them, and re-layouts  14.1 us (10%)
  Pallas kernels  11.3 us (8%)
  between operations  1.6 us (1%)
    psum x1, blocking collectives, global_sum(): values = lax.psum(values, 'gx')  26 us
    ppermute x5, waiting for transfers between devices, global_sum(): lax.ppermute(values, 'gy', [(i, i ^ 1 << k) for i in range(ny)])  22.4 us
    ppermute x4, starting transfers between devices, send(): got = lax.ppermute(flat, axis, pairs)  17.5 us
    pallas_call x2, Pallas kernels, adjoint_step(): pl.pallas_call(functools.partial(step_kernel, section, rows), out_shape=(...  11.3 us
    ppermute x5, starting transfers between devices, global_sum(): lax.ppermute(values, 'gy', [(i, i ^ 1 << k) for i in range(ny)])  11.2 us
    ppermute x4, starting transfers between devices, send(): return [lax.ppermute(pieces[0], axis, pairs)]  10.1 us
    ppermute x4, waiting for transfers between devices, send(): got = lax.ppermute(flat, axis, pairs)  7.94 us
    ppermute x4, waiting for transfers between devices, send(): return [lax.ppermute(pieces[0], axis, pairs)]  3.18 us
  transfers between devices with their start and end apart: 13, of which 8 were waited for; matrix products, arithmetic and copies ran while one was open for 5% of the time, Pallas kernels for 0%

profile of v6, /device:TPU:38, one launch (start us, length us, event | category | flops | bytes accessed | tf_op | source)
XLA Modules:
  0.0 144.6 jit_solution(4356873258493490782)
XLA Ops:
  0.6 1.2 fusion.116
  1.8 1.0 bitcast_convert_fusion
  3.1 1.4 convert_reduce_fusion
  4.5 0.8 and_select_fusion
  5.5 1.9 %collective-permute-start.1 = (f32[30720]{0:T(1024)S(1)}, f32[30720]{0:T(1024)S(1)}, u32[]{:S(2)}, u32[]{:S(2)}) collective-permute-start(f32[30720]{0:T(1024)S(1)} %get-tuple-element.105), channel_id=1, source_target_pairs={{32,0},{64,32},{96,64},{128,96},{160,128},{192,160},{224,192},{256... | collective-permute-start | bytes 368648 | tf_op jit(solution)/shard_map/ppermute | solution.py:110
  7.4 2.4 %collective-permute-start = (f32[30720]{0:T(1024)S(1)}, f32[30720]{0:T(1024)S(1)}, u32[]{:S(2)}, u32[]{:S(2)}) collective-permute-start(f32[30720]{0:T(1024)S(1)} %get-tuple-element.104), channel_id=1, source_target_pairs={{0,32},{32,64},{64,96},{96,128},{128,160},{160,192},{192,224},{224... | collective-permute-start | bytes 368648 | tf_op jit(solution)/shard_map/ppermute | solution.py:110
  9.9 0.7 and_and_fusion.1
  10.5 0.5 compare_and_fusion
  11.0 0.5 fusion.111
  11.6 3.2 %collective-permute-done = f32[30720]{0:T(1024)S(1)} collective-permute-done((f32[30720]{0:T(1024)S(1)}, f32[30720]{0:T(1024)S(1)}, u32[]{:S(2)}, u32[]{:S(2)}) %collective-permute-start) | collective-permute-done | bytes 122912 | tf_op jit(solution)/shard_map/ppermute | solution.py:110
  14.8 0.6 copy-done.4
  16.0 0.9 reshape.278
  16.9 0.8 slice.1031
  17.9 0.9 slice_reduce_fusion.1
  19.0 0.8 slice_bitcast_fusion.21
  20.5 11.2 %collective-permute-start.3 = (f32[4672]{0:T(1024)S(1)}, f32[4672]{0:T(1024)S(1)}, u32[]{:S(2)}, u32[]{:S(2)}) collective-permute-start(f32[4672]{0:T(1024)S(1)} %concatenate.134), channel_id=1, source_target_pairs={{1,0},{2,1},{3,2},{4,3},{5,4},{6,5},{7,6},{8,7},{9,8},{10,9},{11,1... | collective-permute-start | bytes 56072 | tf_op jit(solution)/shard_map/ppermute | solution.py:110
  32.4 1.9 %collective-permute-start.2 = (f32[4672]{0:T(1024)S(1)}, f32[4672]{0:T(1024)S(1)}, u32[]{:S(2)}, u32[]{:S(2)}) collective-permute-start(f32[4672]{0:T(1024)S(1)} %concatenate.133), channel_id=1, source_target_pairs={{0,1},{1,2},{2,3},{3,4},{4,5},{5,6},{6,7},{7,8},{8,9},{9,10},{10,1... | collective-permute-start | bytes 56072 | tf_op jit(solution)/shard_map/ppermute | solution.py:110
  34.5 0.7 pad.313.l_ref
  35.5 4.7 %collective-permute-done.2 = f32[4672]{0:T(1024)S(1)} collective-permute-done((f32[4672]{0:T(1024)S(1)}, f32[4672]{0:T(1024)S(1)}, u32[]{:S(2)}, u32[]{:S(2)}) %collective-permute-start.2) | collective-permute-done | bytes 18720 | tf_op jit(solution)/shard_map/ppermute | solution.py:110
  42.5 1.4 pad.55.g_ref
  44.0 0.3 reshape.294
  44.4 0.3 reshape.293
  45.2 2.4 %fusion.f_ref = f32[1,19,4,24,256]{4,3,2,1,0:T(8,128)} fusion(f32[19,4,18,1]{3,2,1,0:T(8,128)S(1)} %reshape.294, f32[19,4,18,1]{3,2,1,0:T(8,128)S(1)} %reshape.293, f32[19,4,1,128]{3,2,1,0:T(1,128)S(1)} %slice.829, f32[19,4,16,128]{3,2,1,0:T(8,128)S(1)} %bitcast_convert_fusion, f32[19,4,1,128]{3,2,1,0:T(1,128)S(1)} %slice.827), kind=kLoop, calls=%fused_computation.1 | loop fusion | flops 7938048 | bytes 2579136 | tf_op jit(solution)/shard_map/broadcast_in_dim | solution.py:312
  47.5 0.8 select_maximum_fusion.2.b_ref
  48.3 7.7 %shard_map.68 = (f32[19,4,24,256]{3,2,1,0:T(8,128)}, f32[24,256]{1,0:T(8,128)}) custom-call(f32[19,4,24,256]{3,2,1,0:T(8,128)} %pad.55.g_ref, f32[1,19,4,24,256]{4,3,2,1,0:T(8,128)} %fusion.f_ref, f32[4,24,256]{2,1,0:T(8,128)} %select_maximum_fusion.2.b_ref, f32[4,24,256]{2,1,0:T(8,128)} %pad.313.l_ref), custom_call_target="tpu_custom_call" | custom-call | tf_op jit(solution)/shard_map/pallas_call | solution.py:249
  56.0 1.7 %slice_select_fusion = f32[19,4,18,130]{3,2,1,0:T(8,128)S(1)} fusion(f32[19,4,24,256]{3,2,1,0:T(8,128)} %get-tuple-element.6, pred[18,130]{1,0:T(8,128)(4,1)S(1)} %copy-done.9), kind=kLoop, calls=%fused_computation.14 | loop fusion | flops 177840 | bytes 1425060 | tf_op jit(solution)/shard_map/jit(_where)/select_n | solution.py:317
  58.5 0.8 copy-done.1
  59.3 3.6 %shard_map.69 = (f32[19,4,16,128]{3,2,1,0:T(8,128)}, f32[16,128]{1,0:T(8,128)}) custom-call(f32[19,4,16,128]{3,2,1,0:T(8,128)} %copy-done.1, bf16[2,19,4,16,128]{4,3,2,1,0:T(8,128)(2,1)} %f_ref.1, f32[4,16,128]{2,1,0:T(8,128)} %copy-done.2, f32[4,16,128]{2,1,0:T(8,128)} %copy-done.3), custom_call_target="tpu_custom_call" | custom-call | tf_op jit(solution)/shard_map/pallas_call | solution.py:249
  64.4 1.5 %fusion.106 = (f32[]{:T(128)}, f32[]{:T(128)}, f32[16,128]{1,0:T(8,128)S(1)}) fusion(f32[24,136]{1,0:T(8,128)S(1)} %pad_maximum_fusion.14, f32[24,136]{1,0:T(8,128)S(1)} %get-tuple-element.91, f32[24,136]{1,0:T(8,128)S(1)} %get-tuple-element.90, f32[24,136]{1,0:T(8,128)S(1)} %get-tuple-element.89, pred[24,136]{1,0:T(8,128)(4,1)S(1)} %and_and_fusion, ...), kind=kLoop, calls=%fused_computation.274 | loop fusion | flops 36862 | bytes 92168 | tf_op jit(solution)/shard_map/reduce_sum | solution.py:324
  65.9 1.9 %collective-permute-start.5 = (f32[4,128]{1,0:T(4,128)S(1)}, f32[4,128]{1,0:T(4,128)S(1)}, u32[]{:S(2)}, u32[]{:S(2)}) collective-permute-start(f32[4,128]{1,0:T(4,128)S(1)} %get-tuple-element.103), channel_id=1, source_target_pairs={{32,0},{64,32},{96,64},{128,96},{160,128},{192,160},{224,192},{256... | collective-permute-start | bytes 6152 | tf_op jit(solution)/shard_map/ppermute | solution.py:108
  67.8 2.6 %pad_maximum_fusion.19 = f32[4]{0:T(128)S(1)} fusion(f32[1]{0:T(128)} %bitcast.82, f32[1]{0:T(128)} %bitcast.81, f32[1]{0:T(128)} %bitcast.80, f32[1]{0:T(128)} %bitcast.79), kind=kLoop, calls=%fused_computation.326 | loop fusion | flops 12 | bytes 32 | tf_op jit(solution)/shard_map/stack | solution.py:322
  70.4 2.4 %collective-permute-start.4 = (f32[4,128]{1,0:T(4,128)S(1)}, f32[4,128]{1,0:T(4,128)S(1)}, u32[]{:S(2)}, u32[]{:S(2)}) collective-permute-start(f32[4,128]{1,0:T(4,128)S(1)} %get-tuple-element.102), channel_id=1, source_target_pairs={{0,32},{32,64},{64,96},{96,128},{128,160},{160,192},{192,224},{224... | collective-permute-start | bytes 6152 | tf_op jit(solution)/shard_map/ppermute | solution.py:108
  72.8 26.0 %psum.7 = f32[4]{0:T(128)S(1)} all-reduce(f32[4]{0:T(128)S(1)} %pad_maximum_fusion.19), channel_id=1, replica_groups=mesh['gx'=16,'gy'=32] {'gx'}, use_global_device_ids=true, to_apply=%region_4.5 | all-reduce | flops 4 | bytes 32 | tf_op jit(solution)/shard_map/psum | solution.py:124
  98.8 1.9 %collective-permute-start.8 = (f32[4]{0:T(128)S(1)}, f32[4]{0:T(128)S(1)}, u32[]{:S(2)}, u32[]{:S(2)}) collective-permute-start(f32[4]{0:T(128)S(1)} %psum.7), channel_id=1, source_target_pairs={{0,1},{1,0},{2,3},{3,2},{4,5},{5,4},{6,7},{7,6},{8,9},{9,8},{10,11... | collective-permute-start | bytes 56 | tf_op jit(solution)/shard_map/ppermute | solution.py:129
  100.7 3.5 %collective-permute-done.8 = f32[4]{0:T(128)S(1)} collective-permute-done((f32[4]{0:T(128)S(1)}, f32[4]{0:T(128)S(1)}, u32[]{:S(2)}, u32[]{:S(2)}) %collective-permute-start.8) | collective-permute-done | bytes 48 | tf_op jit(solution)/shard_map/ppermute | solution.py:129
  104.3 1.9 %collective-permute-start.9 = (f32[4]{0:T(128)S(1)}, f32[4]{0:T(128)S(1)}, u32[]{:S(2)}, u32[]{:S(2)}) collective-permute-start(f32[4]{0:T(128)S(1)} %add.294), channel_id=1, source_target_pairs={{0,2},{1,3},{2,0},{3,1},{4,6},{5,7},{6,4},{7,5},{8,10},{9,11},{10,... | collective-permute-start | bytes 56 | tf_op jit(solution)/shard_map/ppermute | solution.py:129
  106.2 4.4 %collective-permute-done.9 = f32[4]{0:T(128)S(1)} collective-permute-done((f32[4]{0:T(128)S(1)}, f32[4]{0:T(128)S(1)}, u32[]{:S(2)}, u32[]{:S(2)}) %collective-permute-start.9) | collective-permute-done | bytes 48 | tf_op jit(solution)/shard_map/ppermute | solution.py:129
  110.6 1.9 %collective-permute-start.10 = (f32[4]{0:T(128)S(1)}, f32[4]{0:T(128)S(1)}, u32[]{:S(2)}, u32[]{:S(2)}) collective-permute-start(f32[4]{0:T(128)S(1)} %add.295), channel_id=1, source_target_pairs={{0,4},{1,5},{2,6},{3,7},{4,0},{5,1},{6,2},{7,3},{8,12},{9,13},{10,... | collective-permute-start | bytes 56 | tf_op jit(solution)/shard_map/ppermute | solution.py:129
  112.5 7.4 %collective-permute-done.10 = f32[4]{0:T(128)S(1)} collective-permute-done((f32[4]{0:T(128)S(1)}, f32[4]{0:T(128)S(1)}, u32[]{:S(2)}, u32[]{:S(2)}) %collective-permute-start.10) | collective-permute-done | bytes 48 | tf_op jit(solution)/shard_map/ppermute | solution.py:129
  120.0 2.4 %collective-permute-start.11 = (f32[4]{0:T(128)S(1)}, f32[4]{0:T(128)S(1)}, u32[]{:S(2)}, u32[]{:S(2)}) collective-permute-start(f32[4]{0:T(128)S(1)} %add.296), channel_id=1, source_target_pairs={{0,8},{1,9},{2,10},{3,11},{4,12},{5,13},{6,14},{7,15},{8,0},{9,1},... | collective-permute-start | bytes 56 | tf_op jit(solution)/shard_map/ppermute | solution.py:129
  122.4 3.0 %collective-permute-done.11 = f32[4]{0:T(128)S(1)} collective-permute-done((f32[4]{0:T(128)S(1)}, f32[4]{0:T(128)S(1)}, u32[]{:S(2)}, u32[]{:S(2)}) %collective-permute-start.11) | collective-permute-done | bytes 48 | tf_op jit(solution)/shard_map/ppermute | solution.py:129
  125.4 3.0 %collective-permute-start.12 = (f32[4]{0:T(128)S(1)}, f32[4]{0:T(128)S(1)}, u32[]{:S(2)}, u32[]{:S(2)}) collective-permute-start(f32[4]{0:T(128)S(1)} %add.297), channel_id=1, source_target_pairs={{0,16},{1,17},{2,18},{3,19},{4,20},{5,21},{6,22},{7,23},{8,24},{9,... | collective-permute-start | bytes 56 | tf_op jit(solution)/shard_map/ppermute | solution.py:129
  128.4 3.9 %collective-permute-done.12 = f32[4]{0:T(128)S(1)} collective-permute-done((f32[4]{0:T(128)S(1)}, f32[4]{0:T(128)S(1)}, u32[]{:S(2)}, u32[]{:S(2)}) %collective-permute-start.12) | collective-permute-done | bytes 48 | tf_op jit(solution)/shard_map/ppermute | solution.py:129
  132.6 1.9 %collective-permute-start.7 = (f32[24,4]{1,0:T(8,128)S(1)}, f32[24,4]{1,0:T(8,128)S(1)}, u32[]{:S(2)}, u32[]{:S(2)}) collective-permute-start(f32[24,4]{1,0:T(8,128)S(1)} %get-tuple-element.97), channel_id=1, source_target_pairs={{1,0},{2,1},{3,2},{4,3},{5,4},{6,5},{7,6},{8,7},{9,8},{10,9},{11,1... | collective-permute-start | bytes 1160 | tf_op jit(solution)/shard_map/ppermute | solution.py:108
  134.5 3.9 %collective-permute-start.6 = (f32[24,4]{1,0:T(8,128)S(1)}, f32[24,4]{1,0:T(8,128)S(1)}, u32[]{:S(2)}, u32[]{:S(2)}) collective-permute-start(f32[24,4]{1,0:T(8,128)S(1)} %get-tuple-element.96), channel_id=1, source_target_pairs={{0,1},{1,2},{2,3},{3,4},{4,5},{5,6},{6,7},{7,8},{8,9},{9,10},{10,1... | collective-permute-start | bytes 1160 | tf_op jit(solution)/shard_map/ppermute | solution.py:108
  138.4 0.6 fusion.124
  139.0 3.2 %collective-permute-done.6 = f32[24,4]{1,0:T(8,128)S(1)} collective-permute-done((f32[24,4]{1,0:T(8,128)S(1)}, f32[24,4]{1,0:T(8,128)S(1)}, u32[]{:S(2)}, u32[]{:S(2)}) %collective-permute-start.6) | collective-permute-done | bytes 416 | tf_op jit(solution)/shard_map/ppermute | solution.py:108
  142.7 1.9 %select_add_fusion = f32[16,128]{1,0:T(8,128)} fusion(pred[16,128]{1,0:T(8,128)(4,1)S(1)} %copy-done.11, pred[16,128]{1,0:T(8,128)(4,1)S(1)} %copy-done.13, f32[24,136]{1,0:T(8,128)S(1)} %get-tuple-element.85, f32[24,136]{1,0:T(8,128)S(1)} %get-tuple-element.84, f32[24,136]{1,0:T(8,128)S(1)} %get-tuple-element.83, f32[24,136]{1,0:T(8,128)S(1)} %pad_maximum_fusion.13, ...), kind=kLoop, calls=%fused_computation.294 | loop fusion | flops 22528 | bytes 47112 | tf_op jit(solution)/shard_map/add | solution.py:333
  (158 shorter events, 8.4 us)
Async XLA Ops:
  0.6 14.8 %copy-start = (f32[19,4,16,128]{3,2,1,0:T(8,128)S(1)}, f32[19,4,16,128]{3,2,1,0:T(8,128)}, u32[]{:S(2)}) copy-start(f32[19,4,16,128]{3,2,1,0:T(8,128)} %param.5) | copy-start | bytes 1867780
  4.5 0.9 copy-start.12
  4.5 11.4 %copy-start.10 = (pred[16,128]{1,0:T(8,128)(4,1)}, pred[16,128]{1,0:T(8,128)(4,1)S(1)}, u32[]{:S(2)}) copy-start(pred[16,128]{1,0:T(8,128)(4,1)S(1)} %get-tuple-element.22) | copy-start | bytes 6148
  5.3 29.2 %copy-start.3 = (f32[4,16,128]{2,1,0:T(8,128)}, f32[4,16,128]{2,1,0:T(8,128)S(1)}, u32[]{:S(2)}) copy-start(f32[4,16,128]{2,1,0:T(8,128)S(1)} %get-tuple-element.79.l_ref) | copy-start | bytes 98308
  5.3 42.2 %copy-start.2 = (f32[4,16,128]{2,1,0:T(8,128)}, f32[4,16,128]{2,1,0:T(8,128)S(1)}, u32[]{:S(2)}) copy-start(f32[4,16,128]{2,1,0:T(8,128)S(1)} %get-tuple-element.80.b_ref) | copy-start | bytes 98308
  5.5 6.1 %collective-permute-start.1 = (f32[30720]{0:T(1024)S(1)}, f32[30720]{0:T(1024)S(1)}, u32[]{:S(2)}, u32[]{:S(2)}) collective-permute-start(f32[30720]{0:T(1024)S(1)} %get-tuple-element.105), channel_id=1, source_target_pairs={{32,0},{64,32},{96,64},{128,96},{160,128},{192,160},{224,192},{256... | collective-permute-start | bytes 368648 | tf_op jit(solution)/shard_map/ppermute | solution.py:110
  7.4 7.4 %collective-permute-start = (f32[30720]{0:T(1024)S(1)}, f32[30720]{0:T(1024)S(1)}, u32[]{:S(2)}, u32[]{:S(2)}) collective-permute-start(f32[30720]{0:T(1024)S(1)} %get-tuple-element.104), channel_id=1, source_target_pairs={{0,32},{32,64},{64,96},{96,128},{128,160},{160,192},{192,224},{224... | collective-permute-start | bytes 368648 | tf_op jit(solution)/shard_map/ppermute | solution.py:110
  14.8 0.6 copy-start.4
  17.7 2.7 %copy-start.5 = (f32[3040]{0:T(1024)S(1)}, f32[3040]{0:T(1024)}, u32[]{:S(2)}) copy-start(f32[3040]{0:T(1024)} %reshape.278) | copy-start | bytes 36484
  17.9 16.5 %copy-start.6 = (pred[24]{0:T(512)(128)(4,1)S(1)}, pred[24]{0:T(512)(128)(4,1)}, u32[]{:S(2)}) copy-start(pred[24]{0:T(512)(128)(4,1)} %compare_and_fusion) | copy-start | bytes 76
  17.9 16.5 %copy-start.7 = (pred[136]{0:T(512)(128)(4,1)S(1)}, pred[136]{0:T(512)(128)(4,1)}, u32[]{:S(2)}) copy-start(pred[136]{0:T(512)(128)(4,1)} %get-tuple-element.120) | copy-start | bytes 412
  17.9 16.5 %copy-start.8 = (pred[136]{0:T(512)(128)(4,1)S(1)}, pred[136]{0:T(512)(128)(4,1)}, u32[]{:S(2)}) copy-start(pred[136]{0:T(512)(128)(4,1)} %get-tuple-element.121) | copy-start | bytes 412
  20.5 14.8 %collective-permute-start.3 = (f32[4672]{0:T(1024)S(1)}, f32[4672]{0:T(1024)S(1)}, u32[]{:S(2)}, u32[]{:S(2)}) collective-permute-start(f32[4672]{0:T(1024)S(1)} %concatenate.134), channel_id=1, source_target_pairs={{1,0},{2,1},{3,2},{4,3},{5,4},{6,5},{7,6},{8,7},{9,8},{10,9},{11,1... | collective-permute-start | bytes 56072 | tf_op jit(solution)/shard_map/ppermute | solution.py:110
  32.4 7.8 %collective-permute-start.2 = (f32[4672]{0:T(1024)S(1)}, f32[4672]{0:T(1024)S(1)}, u32[]{:S(2)}, u32[]{:S(2)}) collective-permute-start(f32[4672]{0:T(1024)S(1)} %concatenate.133), channel_id=1, source_target_pairs={{0,1},{1,2},{2,3},{3,4},{4,5},{5,6},{6,7},{7,8},{8,9},{9,10},{10,1... | collective-permute-start | bytes 56072 | tf_op jit(solution)/shard_map/ppermute | solution.py:110
  48.3 7.7 %copy-start.9 = (pred[18,130]{1,0:T(8,128)(4,1)S(1)}, pred[18,130]{1,0:T(8,128)(4,1)}, u32[]{:S(2)}) copy-start(pred[18,130]{1,0:T(8,128)(4,1)} %and_and_fusion.1) | copy-start | bytes 7024
  58.2 84.5 %copy-start.11 = (pred[16,128]{1,0:T(8,128)(4,1)S(1)}, pred[16,128]{1,0:T(8,128)(4,1)}, u32[]{:S(2)}) copy-start(pred[16,128]{1,0:T(8,128)(4,1)} %copy-done.10) | copy-start | bytes 6148
  58.2 84.5 %copy-start.13 = (pred[16,128]{1,0:T(8,128)(4,1)S(1)}, pred[16,128]{1,0:T(8,128)(4,1)}, u32[]{:S(2)}) copy-start(pred[16,128]{1,0:T(8,128)(4,1)} %copy-done.12) | copy-start | bytes 6148
  58.5 0.8 copy-start.1
  65.9 66.6 %collective-permute-start.5 = (f32[4,128]{1,0:T(4,128)S(1)}, f32[4,128]{1,0:T(4,128)S(1)}, u32[]{:S(2)}, u32[]{:S(2)}) collective-permute-start(f32[4,128]{1,0:T(4,128)S(1)} %get-tuple-element.103), channel_id=1, source_target_pairs={{32,0},{64,32},{96,64},{128,96},{160,128},{192,160},{224,192},{256... | collective-permute-start | bytes 6152 | tf_op jit(solution)/shard_map/ppermute | solution.py:108
  70.4 62.1 %collective-permute-start.4 = (f32[4,128]{1,0:T(4,128)S(1)}, f32[4,128]{1,0:T(4,128)S(1)}, u32[]{:S(2)}, u32[]{:S(2)}) collective-permute-start(f32[4,128]{1,0:T(4,128)S(1)} %get-tuple-element.102), channel_id=1, source_target_pairs={{0,32},{32,64},{64,96},{96,128},{128,160},{160,192},{192,224},{224... | collective-permute-start | bytes 6152 | tf_op jit(solution)/shard_map/ppermute | solution.py:108
  98.8 5.5 %collective-permute-start.8 = (f32[4]{0:T(128)S(1)}, f32[4]{0:T(128)S(1)}, u32[]{:S(2)}, u32[]{:S(2)}) collective-permute-start(f32[4]{0:T(128)S(1)} %psum.7), channel_id=1, source_target_pairs={{0,1},{1,0},{2,3},{3,2},{4,5},{5,4},{6,7},{7,6},{8,9},{9,8},{10,11... | collective-permute-start | bytes 56 | tf_op jit(solution)/shard_map/ppermute | solution.py:129
  104.3 6.3 %collective-permute-start.9 = (f32[4]{0:T(128)S(1)}, f32[4]{0:T(128)S(1)}, u32[]{:S(2)}, u32[]{:S(2)}) collective-permute-start(f32[4]{0:T(128)S(1)} %add.294), channel_id=1, source_target_pairs={{0,2},{1,3},{2,0},{3,1},{4,6},{5,7},{6,4},{7,5},{8,10},{9,11},{10,... | collective-permute-start | bytes 56 | tf_op jit(solution)/shard_map/ppermute | solution.py:129
  110.6 9.4 %collective-permute-start.10 = (f32[4]{0:T(128)S(1)}, f32[4]{0:T(128)S(1)}, u32[]{:S(2)}, u32[]{:S(2)}) collective-permute-start(f32[4]{0:T(128)S(1)} %add.295), channel_id=1, source_target_pairs={{0,4},{1,5},{2,6},{3,7},{4,0},{5,1},{6,2},{7,3},{8,12},{9,13},{10,... | collective-permute-start | bytes 56 | tf_op jit(solution)/shard_map/ppermute | solution.py:129
  120.0 5.5 %collective-permute-start.11 = (f32[4]{0:T(128)S(1)}, f32[4]{0:T(128)S(1)}, u32[]{:S(2)}, u32[]{:S(2)}) collective-permute-start(f32[4]{0:T(128)S(1)} %add.296), channel_id=1, source_target_pairs={{0,8},{1,9},{2,10},{3,11},{4,12},{5,13},{6,14},{7,15},{8,0},{9,1},... | collective-permute-start | bytes 56 | tf_op jit(solution)/shard_map/ppermute | solution.py:129
  125.4 7.0 %collective-permute-start.12 = (f32[4]{0:T(128)S(1)}, f32[4]{0:T(128)S(1)}, u32[]{:S(2)}, u32[]{:S(2)}) collective-permute-start(f32[4]{0:T(128)S(1)} %add.297), channel_id=1, source_target_pairs={{0,16},{1,17},{2,18},{3,19},{4,20},{5,21},{6,22},{7,23},{8,24},{9,... | collective-permute-start | bytes 56 | tf_op jit(solution)/shard_map/ppermute | solution.py:129
  132.6 6.5 %collective-permute-start.7 = (f32[24,4]{1,0:T(8,128)S(1)}, f32[24,4]{1,0:T(8,128)S(1)}, u32[]{:S(2)}, u32[]{:S(2)}) collective-permute-start(f32[24,4]{1,0:T(8,128)S(1)} %get-tuple-element.97), channel_id=1, source_target_pairs={{1,0},{2,1},{3,2},{4,3},{5,4},{6,5},{7,6},{8,7},{9,8},{10,9},{11,1... | collective-permute-start | bytes 1160 | tf_op jit(solution)/shard_map/ppermute | solution.py:108
  134.5 7.7 %collective-permute-start.6 = (f32[24,4]{1,0:T(8,128)S(1)}, f32[24,4]{1,0:T(8,128)S(1)}, u32[]{:S(2)}, u32[]{:S(2)}) collective-permute-start(f32[24,4]{1,0:T(8,128)S(1)} %get-tuple-element.96), channel_id=1, source_target_pairs={{0,1},{1,2},{2,3},{3,4},{4,5},{5,6},{6,7},{7,8},{8,9},{9,10},{10,1... | collective-permute-start | bytes 1160 | tf_op jit(solution)/shard_map/ppermute | solution.py:108

commit v7 on v5

--- a/solution.py
+++ b/solution.py
@@ -121,13 +121,12 @@
 
 
 def global_sum(values):
-    values = lax.psum(values, "gx")
     ny = lax.axis_size("gy")
     bits = ny.bit_length() - 1
     assert 1 << bits == ny
     for k in range(bits):
         values = values + lax.ppermute(values, "gy", [(i, i ^ (1 << k)) for i in range(ny)])
-    return values
+    return lax.psum(values, "gx")
 
 
 def pull_back(ext, width_x, width_y):

time: 141 us -> 144 us (1.021)
  the two profiles are of different devices: /device:TPU:38 before, /device:TPU:1 now
where the time goes in v7:
time: 144 us; the launch traced here: 142 us
  starting transfers between devices  49.2 us (34%)
  blocking collectives  28.8 us (20%)
  other arithmetic  21.3 us (15%)
  waiting for transfers between devices  17.6 us (12%)
  local copies, waits for them, and re-layouts  12.3 us (9%)
  Pallas kernels  11.2 us (8%)
    psum x1, blocking collectives, global_sum(): return lax.psum(values, 'gx')  28.8 us
    ppermute x5, starting transfers between devices, global_sum(): lax.ppermute(values, 'gy', [(i, i ^ 1 << k) for i in range(ny)])  24 us
    ppermute x4, starting transfers between devices, send(): got = lax.ppermute(flat, axis, pairs)  15.1 us
    pallas_call x2, Pallas kernels, adjoint_step(): pl.pallas_call(functools.partial(step_kernel, section, rows), out_shape=(...  11.2 us
    ppermute x4, starting transfers between devices, send(): return [lax.ppermute(pieces[0], axis, pairs)]  10.1 us
    ppermute x4, waiting for transfers between devices, send(): return [lax.ppermute(pieces[0], axis, pairs)]  7.87 us
    ppermute x5, waiting for transfers between devices, global_sum(): lax.ppermute(values, 'gy', [(i, i ^ 1 << k) for i in range(ny)])  6.05 us
    add x5, other arithmetic, global_sum(): values + lax.ppermute(values, 'gy', [(i, i ^ 1 << k) for i in range(ny)])  5.09 us
  transfers between devices with their start and end apart: 13, of which 9 were waited for; matrix products, arithmetic and copies ran while one was open for 1% of the time, Pallas kernels for 0%

profile of v7, /device:TPU:1, one launch (start us, length us, event | category | flops | bytes accessed | tf_op | source)
XLA Modules:
  0.0 141.7 jit_solution(5212346344614051662)
XLA Ops:
  0.6 0.8 multiply_select_fusion
  1.4 0.8 and_select_fusion
  2.2 1.0 bitcast_convert_fusion
  3.5 1.1 fusion.63
  4.7 4.6 %collective-permute-start = (f32[29696]{0:T(1024)S(1)}, f32[29696]{0:T(1024)S(1)}, u32[]{:S(2)}, u32[]{:S(2)}) collective-permute-start(f32[29696]{0:T(1024)S(1)} %pad_maximum_fusion.2), channel_id=1, source_target_pairs={{0,32},{32,64},{64,96},{96,128},{128,160},{160,192},{192,224},{224... | collective-permute-start | bytes 356360 | tf_op jit(solution)/shard_map/ppermute | solution.py:110
  9.3 5.5 %collective-permute-start.1 = (f32[29696]{0:T(1024)S(1)}, f32[29696]{0:T(1024)S(1)}, u32[]{:S(2)}, u32[]{:S(2)}) collective-permute-start(f32[29696]{0:T(1024)S(1)} %pad_maximum_fusion.3), channel_id=1, source_target_pairs={{32,0},{64,32},{96,64},{128,96},{160,128},{192,160},{224,192},{256... | collective-permute-start | bytes 356360 | tf_op jit(solution)/shard_map/ppermute | solution.py:110
  14.9 0.8 collective-permute-done.1
  15.7 0.6 copy-done.4
  17.1 0.7 slice.771
  18.1 0.8 slice.768
  19.1 0.9 slice_reduce_fusion.1
  20.2 3.7 %collective-permute-start.2 = (f32[4480]{0:T(1024)S(1)}, f32[4480]{0:T(1024)S(1)}, u32[]{:S(2)}, u32[]{:S(2)}) collective-permute-start(f32[4480]{0:T(1024)S(1)} %concatenate.119), channel_id=1, source_target_pairs={{0,1},{1,2},{2,3},{3,4},{4,5},{5,6},{6,7},{7,8},{8,9},{9,10},{10,1... | collective-permute-start | bytes 53768 | tf_op jit(solution)/shard_map/ppermute | solution.py:110
  24.6 1.3 collective-permute-start.3
  25.9 0.7 pad.271.l_ref
  26.9 2.8 %collective-permute-done.3 = f32[4480]{0:T(1024)S(1)} collective-permute-done((f32[4480]{0:T(1024)S(1)}, f32[4480]{0:T(1024)S(1)}, u32[]{:S(2)}, u32[]{:S(2)}) %collective-permute-start.3) | collective-permute-done | bytes 17952 | tf_op jit(solution)/shard_map/ppermute | solution.py:110
  32.0 1.4 %pad.31.g_ref = f32[19,4,24,256]{3,2,1,0:T(8,128)} pad(f32[19,4,18,130]{3,2,1,0:T(8,128)S(1)} %fusion.28, f32[]{:T(128)} %constant.55.clone.1), padding=0_0x0_0x0_6x0_126 | pad | bytes 2579140 | tf_op jit(solution)/shard_map/jit(_pad)/pad | solution.py:280
  33.4 0.3 reshape.193
  33.9 0.3 reshape.194
  34.7 2.4 %fusion.f_ref = f32[1,19,4,24,256]{4,3,2,1,0:T(8,128)} fusion(f32[19,4,18,1]{3,2,1,0:T(8,128)S(1)} %reshape.194, f32[19,4,18,1]{3,2,1,0:T(8,128)S(1)} %reshape.193, f32[19,4,1,128]{3,2,1,0:T(1,128)S(1)} %slice.619, f32[19,4,16,128]{3,2,1,0:T(8,128)S(1)} %bitcast_convert_fusion, f32[19,4,1,128]{3,2,1,0:T(1,128)S(1)} %slice.617), kind=kLoop, calls=%fused_computation.1 | loop fusion | flops 7938048 | bytes 2579136 | tf_op jit(solution)/shard_map/broadcast_in_dim | solution.py:299
  37.0 0.8 select_maximum_fusion.2.b_ref
  37.8 7.6 %shard_map.68 = (f32[19,4,24,256]{3,2,1,0:T(8,128)}, f32[24,256]{1,0:T(8,128)}) custom-call(f32[19,4,24,256]{3,2,1,0:T(8,128)} %pad.31.g_ref, f32[1,19,4,24,256]{4,3,2,1,0:T(8,128)} %fusion.f_ref, f32[4,24,256]{2,1,0:T(8,128)} %select_maximum_fusion.2.b_ref, f32[4,24,256]{2,1,0:T(8,128)} %pad.271.l_ref), custom_call_target="tpu_custom_call" | custom-call | tf_op jit(solution)/shard_map/pallas_call | solution.py:248
  45.4 1.7 %slice_select_fusion = f32[19,4,18,130]{3,2,1,0:T(8,128)S(1)} fusion(f32[19,4,24,256]{3,2,1,0:T(8,128)} %get-tuple-element.6, pred[18,130]{1,0:T(8,128)(4,1)S(1)} %and_and_fusion.1), kind=kLoop, calls=%fused_computation.14 | loop fusion | flops 177840 | bytes 1425060 | tf_op jit(solution)/shard_map/jit(_where)/select_n | solution.py:310
  48.0 0.8 copy-done.1
  48.8 3.6 %shard_map.69 = (f32[19,4,16,128]{3,2,1,0:T(8,128)}, f32[16,128]{1,0:T(8,128)}) custom-call(f32[19,4,16,128]{3,2,1,0:T(8,128)} %copy-done.1, bf16[2,19,4,16,128]{4,3,2,1,0:T(8,128)(2,1)} %f_ref.1, f32[4,16,128]{2,1,0:T(8,128)} %copy-done.2, f32[4,16,128]{2,1,0:T(8,128)} %copy-done.3), custom_call_target="tpu_custom_call" | custom-call | tf_op jit(solution)/shard_map/pallas_call | solution.py:248
  52.4 0.8 add_multiply_fusion
  53.2 2.9 %collective-permute-start.4 = (f32[4,128]{1,0:T(4,128)S(1)}, f32[4,128]{1,0:T(4,128)S(1)}, u32[]{:S(2)}, u32[]{:S(2)}) collective-permute-start(f32[4,128]{1,0:T(4,128)S(1)} %get-tuple-element.82), channel_id=1, source_target_pairs={{0,32},{32,64},{64,96},{96,128},{128,160},{160,192},{192,224},{224... | collective-permute-start | bytes 6152 | tf_op jit(solution)/shard_map/ppermute | solution.py:108
  56.2 1.9 %collective-permute-start.5 = (f32[4,128]{1,0:T(4,128)S(1)}, f32[4,128]{1,0:T(4,128)S(1)}, u32[]{:S(2)}, u32[]{:S(2)}) collective-permute-start(f32[4,128]{1,0:T(4,128)S(1)} %get-tuple-element.83), channel_id=1, source_target_pairs={{32,0},{64,32},{96,64},{128,96},{160,128},{192,160},{224,192},{256... | collective-permute-start | bytes 6152 | tf_op jit(solution)/shard_map/ppermute | solution.py:108
  58.1 3.0 %collective-permute-done.5 = f32[4,128]{1,0:T(4,128)S(1)} collective-permute-done((f32[4,128]{1,0:T(4,128)S(1)}, f32[4,128]{1,0:T(4,128)S(1)}, u32[]{:S(2)}, u32[]{:S(2)}) %collective-permute-start.5) | collective-permute-done | bytes 2080 | tf_op jit(solution)/shard_map/ppermute | solution.py:108
  61.1 4.0 %collective-permute-start.6 = (f32[24,4]{1,0:T(8,128)S(1)}, f32[24,4]{1,0:T(8,128)S(1)}, u32[]{:S(2)}, u32[]{:S(2)}) collective-permute-start(f32[24,4]{1,0:T(8,128)S(1)} %get-tuple-element.80), channel_id=1, source_target_pairs={{0,1},{1,2},{2,3},{3,4},{4,5},{5,6},{6,7},{7,8},{8,9},{9,10},{10,1... | collective-permute-start | bytes 1160 | tf_op jit(solution)/shard_map/ppermute | solution.py:108
  65.1 1.3 collective-permute-start.7
  66.5 4.9 %collective-permute-done.7 = f32[24,4]{1,0:T(8,128)S(1)} collective-permute-done((f32[24,4]{1,0:T(8,128)S(1)}, f32[24,4]{1,0:T(8,128)S(1)}, u32[]{:S(2)}, u32[]{:S(2)}) %collective-permute-start.7) | collective-permute-done | bytes 416 | tf_op jit(solution)/shard_map/ppermute | solution.py:108
  71.9 0.8 select_reduce_fusion.1
  72.7 2.5 %pad_maximum_fusion.17 = f32[4]{0:T(128)S(1)} fusion(f32[1]{0:T(128)} %bitcast.74, f32[1]{0:T(128)} %bitcast.73, f32[1]{0:T(128)} %bitcast.72, f32[1]{0:T(128)} %bitcast.71), kind=kLoop, calls=%fused_computation.216 | loop fusion | flops 12 | bytes 32 | tf_op jit(solution)/shard_map/stack | solution.py:318
  75.2 4.8 %collective-permute-start.8 = (f32[4]{0:T(128)S(1)}, f32[4]{0:T(128)S(1)}, u32[]{:S(2)}, u32[]{:S(2)}) collective-permute-start(f32[4]{0:T(128)S(1)} %pad_maximum_fusion.17), channel_id=1, source_target_pairs={{0,1},{1,0},{2,3},{3,2},{4,5},{5,4},{6,7},{7,6},{8,9},{9,8},{10,11... | collective-permute-start | bytes 56 | tf_op jit(solution)/shard_map/ppermute | solution.py:128
  80.1 0.9 collective-permute-done.8
  81.0 2.5 %fusion.68 = f32[4]{0:T(128)S(1)} fusion(f32[4]{0:T(128)S(1)} %collective-permute-done.8, f32[1]{0:T(128)} %bitcast.74, f32[1]{0:T(128)} %bitcast.73, f32[1]{0:T(128)} %bitcast.72, f32[1]{0:T(128)} %bitcast.71), kind=kLoop, calls=%fused_computation.224 | loop fusion | flops 16 | bytes 48 | tf_op jit(solution)/shard_map/add | solution.py:128
  83.5 4.5 %collective-permute-start.9 = (f32[4]{0:T(128)S(1)}, f32[4]{0:T(128)S(1)}, u32[]{:S(2)}, u32[]{:S(2)}) collective-permute-start(f32[4]{0:T(128)S(1)} %fusion.68), channel_id=1, source_target_pairs={{0,2},{1,3},{2,0},{3,1},{4,6},{5,7},{6,4},{7,5},{8,10},{9,11},{10,... | collective-permute-start | bytes 56 | tf_op jit(solution)/shard_map/ppermute | solution.py:128
  88.1 0.9 collective-permute-done.9
  89.0 2.5 %fusion.69 = f32[4]{0:T(128)S(1)} fusion(f32[4]{0:T(128)S(1)} %collective-permute-done.9, f32[4]{0:T(128)S(1)} %collective-permute-done.8, f32[1]{0:T(128)} %bitcast.74, f32[1]{0:T(128)} %bitcast.73, f32[1]{0:T(128)} %bitcast.72, f32[1]{0:T(128)} %bitcast.71), kind=kLoop, calls=%fused_computation.225 | loop fusion | flops 20 | bytes 64 | tf_op jit(solution)/shard_map/add | solution.py:128
  91.6 5.9 %collective-permute-start.10 = (f32[4]{0:T(128)S(1)}, f32[4]{0:T(128)S(1)}, u32[]{:S(2)}, u32[]{:S(2)}) collective-permute-start(f32[4]{0:T(128)S(1)} %fusion.69), channel_id=1, source_target_pairs={{0,4},{1,5},{2,6},{3,7},{4,0},{5,1},{6,2},{7,3},{8,12},{9,13},{10,... | collective-permute-start | bytes 56 | tf_op jit(solution)/shard_map/ppermute | solution.py:128
  97.5 2.3 %collective-permute-done.10 = f32[4]{0:T(128)S(1)} collective-permute-done((f32[4]{0:T(128)S(1)}, f32[4]{0:T(128)S(1)}, u32[]{:S(2)}, u32[]{:S(2)}) %collective-permute-start.10) | collective-permute-done | bytes 48 | tf_op jit(solution)/shard_map/ppermute | solution.py:128
  99.8 3.8 %collective-permute-start.11 = (f32[4]{0:T(128)S(1)}, f32[4]{0:T(128)S(1)}, u32[]{:S(2)}, u32[]{:S(2)}) collective-permute-start(f32[4]{0:T(128)S(1)} %add.148), channel_id=1, source_target_pairs={{0,8},{1,9},{2,10},{3,11},{4,12},{5,13},{6,14},{7,15},{8,0},{9,1},... | collective-permute-start | bytes 56 | tf_op jit(solution)/shard_map/ppermute | solution.py:128
  103.6 0.9 collective-permute-done.11
  104.6 4.9 %collective-permute-start.12 = (f32[4]{0:T(128)S(1)}, f32[4]{0:T(128)S(1)}, u32[]{:S(2)}, u32[]{:S(2)}) collective-permute-start(f32[4]{0:T(128)S(1)} %add.149), channel_id=1, source_target_pairs={{0,16},{1,17},{2,18},{3,19},{4,20},{5,21},{6,22},{7,23},{8,24},{9,... | collective-permute-start | bytes 56 | tf_op jit(solution)/shard_map/ppermute | solution.py:128
  109.4 0.9 collective-permute-done.12
  110.4 28.8 %psum.7 = f32[4]{0:T(128)S(1)} all-reduce(f32[4]{0:T(128)S(1)} %add.150), channel_id=1, replica_groups=mesh['gx'=16,'gy'=32] {'gx'}, use_global_device_ids=true, to_apply=%region_4.5 | all-reduce | flops 4 | bytes 32 | tf_op jit(solution)/shard_map/psum | solution.py:129
  139.2 0.6 fusion.67
  139.9 1.9 %select_add_fusion = f32[16,128]{1,0:T(8,128)} fusion(pred[16,128]{1,0:T(8,128)(4,1)S(1)} %get-tuple-element.22, f32[16,128]{1,0:T(8,128)S(1)} %get-tuple-element.21, pred[16,128]{1,0:T(8,128)(4,1)S(1)} %get-tuple-element.20, f32[]{:T(128)} %bitcast.76, f32[]{:T(128)} %bitcast.75), kind=kLoop, calls=%fused_computation.198 | loop fusion | flops 10240 | bytes 20488 | tf_op jit(solution)/shard_map/add | solution.py:328
  (113 shorter events, 6.8 us)
Async XLA Ops:
  0.6 15.7 %copy-start = (f32[19,4,16,128]{3,2,1,0:T(8,128)S(1)}, f32[19,4,16,128]{3,2,1,0:T(8,128)}, u32[]{:S(2)}) copy-start(f32[19,4,16,128]{3,2,1,0:T(8,128)} %param.5) | copy-start | bytes 1867780
  2.2 23.7 %copy-start.3 = (f32[4,16,128]{2,1,0:T(8,128)}, f32[4,16,128]{2,1,0:T(8,128)S(1)}, u32[]{:S(2)}) copy-start(f32[4,16,128]{2,1,0:T(8,128)S(1)} %get-tuple-element.73.l_ref) | copy-start | bytes 98308
  2.2 34.8 %copy-start.2 = (f32[4,16,128]{2,1,0:T(8,128)}, f32[4,16,128]{2,1,0:T(8,128)S(1)}, u32[]{:S(2)}) copy-start(f32[4,16,128]{2,1,0:T(8,128)S(1)} %get-tuple-element.74.b_ref) | copy-start | bytes 98308
  4.7 10.2 %collective-permute-start = (f32[29696]{0:T(1024)S(1)}, f32[29696]{0:T(1024)S(1)}, u32[]{:S(2)}, u32[]{:S(2)}) collective-permute-start(f32[29696]{0:T(1024)S(1)} %pad_maximum_fusion.2), channel_id=1, source_target_pairs={{0,32},{32,64},{64,96},{96,128},{128,160},{160,192},{192,224},{224... | collective-permute-start | bytes 356360 | tf_op jit(solution)/shard_map/ppermute | solution.py:110
  9.3 6.4 %collective-permute-start.1 = (f32[29696]{0:T(1024)S(1)}, f32[29696]{0:T(1024)S(1)}, u32[]{:S(2)}, u32[]{:S(2)}) collective-permute-start(f32[29696]{0:T(1024)S(1)} %pad_maximum_fusion.3), channel_id=1, source_target_pairs={{32,0},{64,32},{96,64},{128,96},{160,128},{192,160},{224,192},{256... | collective-permute-start | bytes 356360 | tf_op jit(solution)/shard_map/ppermute | solution.py:110
  15.7 0.6 copy-start.4
  20.2 6.4 %collective-permute-start.2 = (f32[4480]{0:T(1024)S(1)}, f32[4480]{0:T(1024)S(1)}, u32[]{:S(2)}, u32[]{:S(2)}) collective-permute-start(f32[4480]{0:T(1024)S(1)} %concatenate.119), channel_id=1, source_target_pairs={{0,1},{1,2},{2,3},{3,4},{4,5},{5,6},{6,7},{7,8},{8,9},{9,10},{10,1... | collective-permute-start | bytes 53768 | tf_op jit(solution)/shard_map/ppermute | solution.py:110
  24.6 5.2 %collective-permute-start.3 = (f32[4480]{0:T(1024)S(1)}, f32[4480]{0:T(1024)S(1)}, u32[]{:S(2)}, u32[]{:S(2)}) collective-permute-start(f32[4480]{0:T(1024)S(1)} %concatenate.120), channel_id=1, source_target_pairs={{1,0},{2,1},{3,2},{4,3},{5,4},{6,5},{7,6},{8,7},{9,8},{10,9},{11,1... | collective-permute-start | bytes 53768 | tf_op jit(solution)/shard_map/ppermute | solution.py:110
  47.2 24.7 %copy-start.5 = (s32[16,128]{1,0:T(8,128)S(1)}, s32[16,128]{1,0:T(8,128)}, u32[]{:S(2)}) copy-start(s32[16,128]{1,0:T(8,128)} %param.8) | copy-start | bytes 24580
  47.9 0.8 copy-start.1
  53.2 4.9 %collective-permute-start.4 = (f32[4,128]{1,0:T(4,128)S(1)}, f32[4,128]{1,0:T(4,128)S(1)}, u32[]{:S(2)}, u32[]{:S(2)}) collective-permute-start(f32[4,128]{1,0:T(4,128)S(1)} %get-tuple-element.82), channel_id=1, source_target_pairs={{0,32},{32,64},{64,96},{96,128},{128,160},{160,192},{192,224},{224... | collective-permute-start | bytes 6152 | tf_op jit(solution)/shard_map/ppermute | solution.py:108
  56.2 4.9 %collective-permute-start.5 = (f32[4,128]{1,0:T(4,128)S(1)}, f32[4,128]{1,0:T(4,128)S(1)}, u32[]{:S(2)}, u32[]{:S(2)}) collective-permute-start(f32[4,128]{1,0:T(4,128)S(1)} %get-tuple-element.83), channel_id=1, source_target_pairs={{32,0},{64,32},{96,64},{128,96},{160,128},{192,160},{224,192},{256... | collective-permute-start | bytes 6152 | tf_op jit(solution)/shard_map/ppermute | solution.py:108
  61.1 5.4 %collective-permute-start.6 = (f32[24,4]{1,0:T(8,128)S(1)}, f32[24,4]{1,0:T(8,128)S(1)}, u32[]{:S(2)}, u32[]{:S(2)}) collective-permute-start(f32[24,4]{1,0:T(8,128)S(1)} %get-tuple-element.80), channel_id=1, source_target_pairs={{0,1},{1,2},{2,3},{3,4},{4,5},{5,6},{6,7},{7,8},{8,9},{9,10},{10,1... | collective-permute-start | bytes 1160 | tf_op jit(solution)/shard_map/ppermute | solution.py:108
  65.1 6.3 %collective-permute-start.7 = (f32[24,4]{1,0:T(8,128)S(1)}, f32[24,4]{1,0:T(8,128)S(1)}, u32[]{:S(2)}, u32[]{:S(2)}) collective-permute-start(f32[24,4]{1,0:T(8,128)S(1)} %get-tuple-element.81), channel_id=1, source_target_pairs={{1,0},{2,1},{3,2},{4,3},{5,4},{6,5},{7,6},{8,7},{9,8},{10,9},{11,1... | collective-permute-start | bytes 1160 | tf_op jit(solution)/shard_map/ppermute | solution.py:108
  75.2 5.8 %collective-permute-start.8 = (f32[4]{0:T(128)S(1)}, f32[4]{0:T(128)S(1)}, u32[]{:S(2)}, u32[]{:S(2)}) collective-permute-start(f32[4]{0:T(128)S(1)} %pad_maximum_fusion.17), channel_id=1, source_target_pairs={{0,1},{1,0},{2,3},{3,2},{4,5},{5,4},{6,7},{7,6},{8,9},{9,8},{10,11... | collective-permute-start | bytes 56 | tf_op jit(solution)/shard_map/ppermute | solution.py:128
  83.5 5.5 %collective-permute-start.9 = (f32[4]{0:T(128)S(1)}, f32[4]{0:T(128)S(1)}, u32[]{:S(2)}, u32[]{:S(2)}) collective-permute-start(f32[4]{0:T(128)S(1)} %fusion.68), channel_id=1, source_target_pairs={{0,2},{1,3},{2,0},{3,1},{4,6},{5,7},{6,4},{7,5},{8,10},{9,11},{10,... | collective-permute-start | bytes 56 | tf_op jit(solution)/shard_map/ppermute | solution.py:128
  91.6 8.2 %collective-permute-start.10 = (f32[4]{0:T(128)S(1)}, f32[4]{0:T(128)S(1)}, u32[]{:S(2)}, u32[]{:S(2)}) collective-permute-start(f32[4]{0:T(128)S(1)} %fusion.69), channel_id=1, source_target_pairs={{0,4},{1,5},{2,6},{3,7},{4,0},{5,1},{6,2},{7,3},{8,12},{9,13},{10,... | collective-permute-start | bytes 56 | tf_op jit(solution)/shard_map/ppermute | solution.py:128
  99.8 4.8 %collective-permute-start.11 = (f32[4]{0:T(128)S(1)}, f32[4]{0:T(128)S(1)}, u32[]{:S(2)}, u32[]{:S(2)}) collective-permute-start(f32[4]{0:T(128)S(1)} %add.148), channel_id=1, source_target_pairs={{0,8},{1,9},{2,10},{3,11},{4,12},{5,13},{6,14},{7,15},{8,0},{9,1},... | collective-permute-start | bytes 56 | tf_op jit(solution)/shard_map/ppermute | solution.py:128
  104.6 5.8 %collective-permute-start.12 = (f32[4]{0:T(128)S(1)}, f32[4]{0:T(128)S(1)}, u32[]{:S(2)}, u32[]{:S(2)}) collective-permute-start(f32[4]{0:T(128)S(1)} %add.149), channel_id=1, source_target_pairs={{0,16},{1,17},{2,18},{3,19},{4,20},{5,21},{6,22},{7,23},{8,24},{9,... | collective-permute-start | bytes 56 | tf_op jit(solution)/shard_map/ppermute | solution.py:128

commit v8 on v7

--- a/solution.py
+++ b/solution.py
@@ -121,12 +121,10 @@
 
 
 def global_sum(values):
-    ny = lax.axis_size("gy")
-    bits = ny.bit_length() - 1
-    assert 1 << bits == ny
-    for k in range(bits):
-        values = values + lax.ppermute(values, "gy", [(i, i ^ (1 << k)) for i in range(ny)])
-    return lax.psum(values, "gx")
+    axes = ("gx", "gy")
+    count = lax.axis_size("gx") * lax.axis_size("gy")
+    rows = jnp.broadcast_to(values[None, :], (count,) + values.shape)
+    return jnp.sum(lax.all_to_all(rows, axes, 0, 0, tiled=True), axis=0)
 
 
 def pull_back(ext, width_x, width_y):

time: 144 us -> 117 us (0.81)
  starting transfers between devices: 49.2 us -> 25.2 us
  blocking collectives: 28.8 us -> 37.3 us
  waiting for transfers between devices: 17.6 us -> 11.5 us
  other arithmetic: 21.3 us -> 16.9 us
    all_to_all x0 -> x1, blocking collectives: none -> 37.3 us  [global_sum(): return jnp.sum(lax.all_to_all(rows, axes, 0, 0, tiled=True), axis=0)]
    psum x1 -> x0, blocking collectives: 28.8 us -> none  [global_sum(): return lax.psum(values, 'gx')]
    ppermute x5 -> x0, starting transfers between devices: 24 us -> none  [global_sum(): lax.ppermute(values, 'gy', [(i, i ^ 1 << k) for i in range(ny)])]
    ppermute x5 -> x0, waiting for transfers between devices: 6.05 us -> none  [global_sum(): lax.ppermute(values, 'gy', [(i, i ^ 1 << k) for i in range(ny)])]
    add x5 -> x0, other arithmetic: 5.09 us -> none  [global_sum(): values + lax.ppermute(values, 'gy', [(i, i ^ 1 << k) for i in range(ny)])]
  transfers between devices with their start and end apart: 13 -> 8, of which waited for: 9 -> 4; matrix products, arithmetic and copies ran while one was open for 1% -> 2% of each run, Pallas kernels for 0% -> 0%
where the time goes in v8:
time: 117 us; the launch traced here: 116 us
  blocking collectives  37.3 us (32%)
  starting transfers between devices  25.2 us (22%)
  other arithmetic  16.9 us (14%)
  local copies, waits for them, and re-layouts  12.4 us (11%)
  waiting for transfers between devices  11.5 us (10%)
  Pallas kernels  11.2 us (10%)
  between operations  1.3 us (1%)
    all_to_all x1, blocking collectives, global_sum(): return jnp.sum(lax.all_to_all(rows, axes, 0, 0, tiled=True), axis=0)  37.3 us
    ppermute x4, starting transfers between devices, send(): got = lax.ppermute(flat, axis, pairs)  15.1 us
    pallas_call x2, Pallas kernels, adjoint_step(): pl.pallas_call(functools.partial(step_kernel, section, rows), out_shape=(...  11.2 us
    ppermute x4, starting transfers between devices, send(): return [lax.ppermute(pieces[0], axis, pairs)]  10.1 us
    ppermute x4, waiting for transfers between devices, send(): return [lax.ppermute(pieces[0], axis, pairs)]  7.87 us
    ppermute x4, waiting for transfers between devices, send(): got = lax.ppermute(flat, axis, pairs)  3.63 us
    slice x8, local copies, waits for them, and re-layouts, halo_many(): tails.append(lax.slice_in_dim(a, size - w, size, axis=a.ndim + dim))  2.82 us
    another operation x1, other arithmetic, per_device(): jnp.stack([jnp.sum(smooth * region_one), jnp.sum(smooth * region_two), jn...  2.65 us
  transfers between devices with their start and end apart: 8, of which 4 were waited for; matrix products, arithmetic and copies ran while one was open for 2% of the time, Pallas kernels for 0%

profile of v8, /device:TPU:1, one launch (start us, length us, event | category | flops | bytes accessed | tf_op | source)
XLA Modules:
  0.0 115.8 jit_solution(1377678232457325536)
XLA Ops:
  0.6 0.8 multiply_select_fusion
  1.4 0.8 and_select_fusion
  2.2 1.0 bitcast_convert_fusion
  3.3 0.2 slice_reduce_fusion.5
  3.5 1.1 fusion.63
  4.7 4.6 %collective-permute-start = (f32[29696]{0:T(1024)S(1)}, f32[29696]{0:T(1024)S(1)}, u32[]{:S(2)}, u32[]{:S(2)}) collective-permute-start(f32[29696]{0:T(1024)S(1)} %pad_maximum_fusion.2), channel_id=1, source_target_pairs={{0,32},{32,64},{64,96},{96,128},{128,160},{160,192},{192,224},{224... | collective-permute-start | bytes 356360 | tf_op jit(solution)/shard_map/ppermute | solution.py:110
  9.3 5.5 %collective-permute-start.1 = (f32[29696]{0:T(1024)S(1)}, f32[29696]{0:T(1024)S(1)}, u32[]{:S(2)}, u32[]{:S(2)}) collective-permute-start(f32[29696]{0:T(1024)S(1)} %pad_maximum_fusion.3), channel_id=1, source_target_pairs={{32,0},{64,32},{96,64},{128,96},{160,128},{192,160},{224,192},{256... | collective-permute-start | bytes 356360 | tf_op jit(solution)/shard_map/ppermute | solution.py:110
  14.9 0.8 collective-permute-done.1
  15.7 0.6 copy-done.4
  16.4 0.1 pad_maximum_fusion
  16.5 0.3 fusion.62
  16.8 0.3 reshape.186
  17.1 0.7 slice.771
  17.8 0.2 slice_reduce_fusion.3
  18.1 0.8 slice.768
  19.0 0.2 pad_maximum_fusion.1
  19.1 0.9 slice_reduce_fusion.1
  20.2 3.7 %collective-permute-start.2 = (f32[4480]{0:T(1024)S(1)}, f32[4480]{0:T(1024)S(1)}, u32[]{:S(2)}, u32[]{:S(2)}) collective-permute-start(f32[4480]{0:T(1024)S(1)} %concatenate.119), channel_id=1, source_target_pairs={{0,1},{1,2},{2,3},{3,4},{4,5},{5,6},{6,7},{7,8},{8,9},{9,10},{10,1... | collective-permute-start | bytes 53768 | tf_op jit(solution)/shard_map/ppermute | solution.py:110
  24.0 0.3 reshape.190
  24.6 1.3 %collective-permute-start.3 = (f32[4480]{0:T(1024)S(1)}, f32[4480]{0:T(1024)S(1)}, u32[]{:S(2)}, u32[]{:S(2)}) collective-permute-start(f32[4480]{0:T(1024)S(1)} %concatenate.120), channel_id=1, source_target_pairs={{1,0},{2,1},{3,2},{4,3},{5,4},{6,5},{7,6},{8,7},{9,8},{10,9},{11,1... | collective-permute-start | bytes 53768 | tf_op jit(solution)/shard_map/ppermute | solution.py:110
  25.9 0.7 pad.271.l_ref
  26.6 0.3 reshape.189
  26.9 2.8 %collective-permute-done.3 = f32[4480]{0:T(1024)S(1)} collective-permute-done((f32[4480]{0:T(1024)S(1)}, f32[4480]{0:T(1024)S(1)}, u32[]{:S(2)}, u32[]{:S(2)}) %collective-permute-start.3) | collective-permute-done | bytes 17952 | tf_op jit(solution)/shard_map/ppermute | solution.py:110
  29.7 0.3 reshape.193
  30.0 0.2 maximum_bitcast_fusion.16
  30.5 0.2 maximum_bitcast_fusion.13
  32.0 1.4 %pad.31.g_ref = f32[19,4,24,256]{3,2,1,0:T(8,128)} pad(f32[19,4,18,130]{3,2,1,0:T(8,128)S(1)} %fusion.28, f32[]{:T(128)} %constant.55.clone.1), padding=0_0x0_0x0_6x0_126 | pad | bytes 2579140 | tf_op jit(solution)/shard_map/jit(_pad)/pad | solution.py:278
  33.4 0.3 reshape.199
  33.8 0.3 reshape.200
  34.6 2.4 %fusion.f_ref = f32[1,19,4,24,256]{4,3,2,1,0:T(8,128)} fusion(f32[19,4,18,1]{3,2,1,0:T(8,128)S(1)} %reshape.200, f32[19,4,18,1]{3,2,1,0:T(8,128)S(1)} %reshape.199, f32[19,4,1,128]{3,2,1,0:T(1,128)S(1)} %slice.619, f32[19,4,16,128]{3,2,1,0:T(8,128)S(1)} %bitcast_convert_fusion, f32[19,4,1,128]{3,2,1,0:T(1,128)S(1)} %slice.617), kind=kLoop, calls=%fused_computation.1 | loop fusion | flops 7938048 | bytes 2579136 | tf_op jit(solution)/shard_map/broadcast_in_dim | solution.py:297
  37.0 0.8 select_maximum_fusion.2.b_ref
  37.8 7.6 %shard_map.68 = (f32[19,4,24,256]{3,2,1,0:T(8,128)}, f32[24,256]{1,0:T(8,128)}) custom-call(f32[19,4,24,256]{3,2,1,0:T(8,128)} %pad.31.g_ref, f32[1,19,4,24,256]{4,3,2,1,0:T(8,128)} %fusion.f_ref, f32[4,24,256]{2,1,0:T(8,128)} %select_maximum_fusion.2.b_ref, f32[4,24,256]{2,1,0:T(8,128)} %pad.271.l_ref), custom_call_target="tpu_custom_call" | custom-call | tf_op jit(solution)/shard_map/pallas_call | solution.py:246
  45.4 1.7 %slice_select_fusion = f32[19,4,18,130]{3,2,1,0:T(8,128)S(1)} fusion(f32[19,4,24,256]{3,2,1,0:T(8,128)} %get-tuple-element.6, pred[18,130]{1,0:T(8,128)(4,1)S(1)} %and_and_fusion.1), kind=kLoop, calls=%fused_computation.14 | loop fusion | flops 177840 | bytes 1425060 | tf_op jit(solution)/shard_map/jit(_where)/select_n | solution.py:308
  47.9 0.8 copy-done.1
  48.8 3.6 %shard_map.69 = (f32[19,4,16,128]{3,2,1,0:T(8,128)}, f32[16,128]{1,0:T(8,128)}) custom-call(f32[19,4,16,128]{3,2,1,0:T(8,128)} %copy-done.1, bf16[2,19,4,16,128]{4,3,2,1,0:T(8,128)(2,1)} %f_ref.1, f32[4,16,128]{2,1,0:T(8,128)} %copy-done.2, f32[4,16,128]{2,1,0:T(8,128)} %copy-done.3), custom_call_target="tpu_custom_call" | custom-call | tf_op jit(solution)/shard_map/pallas_call | solution.py:246
  52.4 0.8 add_multiply_fusion
  53.2 2.9 %collective-permute-start.4 = (f32[4,128]{1,0:T(4,128)S(1)}, f32[4,128]{1,0:T(4,128)S(1)}, u32[]{:S(2)}, u32[]{:S(2)}) collective-permute-start(f32[4,128]{1,0:T(4,128)S(1)} %get-tuple-element.82), channel_id=1, source_target_pairs={{0,32},{32,64},{64,96},{96,128},{128,160},{160,192},{192,224},{224... | collective-permute-start | bytes 6152 | tf_op jit(solution)/shard_map/ppermute | solution.py:108
  56.1 1.9 %collective-permute-start.5 = (f32[4,128]{1,0:T(4,128)S(1)}, f32[4,128]{1,0:T(4,128)S(1)}, u32[]{:S(2)}, u32[]{:S(2)}) collective-permute-start(f32[4,128]{1,0:T(4,128)S(1)} %get-tuple-element.83), channel_id=1, source_target_pairs={{32,0},{64,32},{96,64},{128,96},{160,128},{192,160},{224,192},{256... | collective-permute-start | bytes 6152 | tf_op jit(solution)/shard_map/ppermute | solution.py:108
  58.1 3.0 %collective-permute-done.5 = f32[4,128]{1,0:T(4,128)S(1)} collective-permute-done((f32[4,128]{1,0:T(4,128)S(1)}, f32[4,128]{1,0:T(4,128)S(1)}, u32[]{:S(2)}, u32[]{:S(2)}) %collective-permute-start.5) | collective-permute-done | bytes 2080 | tf_op jit(solution)/shard_map/ppermute | solution.py:108
  61.1 4.0 %collective-permute-start.6 = (f32[24,4]{1,0:T(8,128)S(1)}, f32[24,4]{1,0:T(8,128)S(1)}, u32[]{:S(2)}, u32[]{:S(2)}) collective-permute-start(f32[24,4]{1,0:T(8,128)S(1)} %get-tuple-element.80), channel_id=1, source_target_pairs={{0,1},{1,2},{2,3},{3,4},{4,5},{5,6},{6,7},{7,8},{8,9},{9,10},{10,1... | collective-permute-start | bytes 1160 | tf_op jit(solution)/shard_map/ppermute | solution.py:108
  65.1 1.3 %collective-permute-start.7 = (f32[24,4]{1,0:T(8,128)S(1)}, f32[24,4]{1,0:T(8,128)S(1)}, u32[]{:S(2)}, u32[]{:S(2)}) collective-permute-start(f32[24,4]{1,0:T(8,128)S(1)} %get-tuple-element.81), channel_id=1, source_target_pairs={{1,0},{2,1},{3,2},{4,3},{5,4},{6,5},{7,6},{8,7},{9,8},{10,9},{11,1... | collective-permute-start | bytes 1160 | tf_op jit(solution)/shard_map/ppermute | solution.py:108
  66.5 4.9 %collective-permute-done.7 = f32[24,4]{1,0:T(8,128)S(1)} collective-permute-done((f32[24,4]{1,0:T(8,128)S(1)}, f32[24,4]{1,0:T(8,128)S(1)}, u32[]{:S(2)}, u32[]{:S(2)}) %collective-permute-start.7) | collective-permute-done | bytes 416 | tf_op jit(solution)/shard_map/ppermute | solution.py:108
  71.9 0.8 select_reduce_fusion.1
  72.7 2.6 %pad_maximum_fusion.17 = f32[4]{0:T(128)S(1)} fusion(f32[1]{0:T(128)} %bitcast.74, f32[1]{0:T(128)} %bitcast.73, f32[1]{0:T(128)} %bitcast.72, f32[1]{0:T(128)} %bitcast.71), kind=kLoop, calls=%fused_computation.216 | loop fusion | flops 12 | bytes 32 | tf_op jit(solution)/shard_map/stack | solution.py:316
  75.5 37.3 %all_to_all.6 = f32[512,1,4]{2,1,0:T(1,128)S(1)} all-to-all(f32[512,1,4]{2,1,0:T(1,128)S(1)} %broadcast_in_dim.60), channel_id=1, replica_groups=mesh['gx'=16,'gy'=32] {'gx','gy'}, dimensions={0} | all-to-all | bytes 16384 | tf_op jit(solution)/shard_map/all_to_all | solution.py:127
  112.8 0.6 reduce_sum.49
  113.4 0.6 fusion.67
  114.0 1.9 %select_add_fusion = f32[16,128]{1,0:T(8,128)} fusion(pred[16,128]{1,0:T(8,128)(4,1)S(1)} %get-tuple-element.22, f32[16,128]{1,0:T(8,128)S(1)} %get-tuple-element.21, pred[16,128]{1,0:T(8,128)(4,1)S(1)} %get-tuple-element.20, f32[]{:T(128)} %bitcast.76, f32[]{:T(128)} %bitcast.75), kind=kLoop, calls=%fused_computation.198 | loop fusion | flops 10240 | bytes 20488 | tf_op jit(solution)/shard_map/add | solution.py:326
  (100 shorter events, 4.4 us)
Async XLA Ops:
  0.6 15.7 %copy-start = (f32[19,4,16,128]{3,2,1,0:T(8,128)S(1)}, f32[19,4,16,128]{3,2,1,0:T(8,128)}, u32[]{:S(2)}) copy-start(f32[19,4,16,128]{3,2,1,0:T(8,128)} %param.5) | copy-start | bytes 1867780
  2.2 23.7 %copy-start.3 = (f32[4,16,128]{2,1,0:T(8,128)}, f32[4,16,128]{2,1,0:T(8,128)S(1)}, u32[]{:S(2)}) copy-start(f32[4,16,128]{2,1,0:T(8,128)S(1)} %get-tuple-element.73.l_ref) | copy-start | bytes 98308
  2.2 34.8 %copy-start.2 = (f32[4,16,128]{2,1,0:T(8,128)}, f32[4,16,128]{2,1,0:T(8,128)S(1)}, u32[]{:S(2)}) copy-start(f32[4,16,128]{2,1,0:T(8,128)S(1)} %get-tuple-element.74.b_ref) | copy-start | bytes 98308
  4.7 10.2 %collective-permute-start = (f32[29696]{0:T(1024)S(1)}, f32[29696]{0:T(1024)S(1)}, u32[]{:S(2)}, u32[]{:S(2)}) collective-permute-start(f32[29696]{0:T(1024)S(1)} %pad_maximum_fusion.2), channel_id=1, source_target_pairs={{0,32},{32,64},{64,96},{96,128},{128,160},{160,192},{192,224},{224... | collective-permute-start | bytes 356360 | tf_op jit(solution)/shard_map/ppermute | solution.py:110
  9.3 6.4 %collective-permute-start.1 = (f32[29696]{0:T(1024)S(1)}, f32[29696]{0:T(1024)S(1)}, u32[]{:S(2)}, u32[]{:S(2)}) collective-permute-start(f32[29696]{0:T(1024)S(1)} %pad_maximum_fusion.3), channel_id=1, source_target_pairs={{32,0},{64,32},{96,64},{128,96},{160,128},{192,160},{224,192},{256... | collective-permute-start | bytes 356360 | tf_op jit(solution)/shard_map/ppermute | solution.py:110
  15.7 0.6 copy-start.4
  20.2 6.4 %collective-permute-start.2 = (f32[4480]{0:T(1024)S(1)}, f32[4480]{0:T(1024)S(1)}, u32[]{:S(2)}, u32[]{:S(2)}) collective-permute-start(f32[4480]{0:T(1024)S(1)} %concatenate.119), channel_id=1, source_target_pairs={{0,1},{1,2},{2,3},{3,4},{4,5},{5,6},{6,7},{7,8},{8,9},{9,10},{10,1... | collective-permute-start | bytes 53768 | tf_op jit(solution)/shard_map/ppermute | solution.py:110
  24.6 5.2 %collective-permute-start.3 = (f32[4480]{0:T(1024)S(1)}, f32[4480]{0:T(1024)S(1)}, u32[]{:S(2)}, u32[]{:S(2)}) collective-permute-start(f32[4480]{0:T(1024)S(1)} %concatenate.120), channel_id=1, source_target_pairs={{1,0},{2,1},{3,2},{4,3},{5,4},{6,5},{7,6},{8,7},{9,8},{10,9},{11,1... | collective-permute-start | bytes 53768 | tf_op jit(solution)/shard_map/ppermute | solution.py:110
  47.2 24.7 %copy-start.5 = (s32[16,128]{1,0:T(8,128)S(1)}, s32[16,128]{1,0:T(8,128)}, u32[]{:S(2)}) copy-start(s32[16,128]{1,0:T(8,128)} %param.8) | copy-start | bytes 24580
  47.9 0.8 copy-start.1
  53.2 4.9 %collective-permute-start.4 = (f32[4,128]{1,0:T(4,128)S(1)}, f32[4,128]{1,0:T(4,128)S(1)}, u32[]{:S(2)}, u32[]{:S(2)}) collective-permute-start(f32[4,128]{1,0:T(4,128)S(1)} %get-tuple-element.82), channel_id=1, source_target_pairs={{0,32},{32,64},{64,96},{96,128},{128,160},{160,192},{192,224},{224... | collective-permute-start | bytes 6152 | tf_op jit(solution)/shard_map/ppermute | solution.py:108
  56.1 4.9 %collective-permute-start.5 = (f32[4,128]{1,0:T(4,128)S(1)}, f32[4,128]{1,0:T(4,128)S(1)}, u32[]{:S(2)}, u32[]{:S(2)}) collective-permute-start(f32[4,128]{1,0:T(4,128)S(1)} %get-tuple-element.83), channel_id=1, source_target_pairs={{32,0},{64,32},{96,64},{128,96},{160,128},{192,160},{224,192},{256... | collective-permute-start | bytes 6152 | tf_op jit(solution)/shard_map/ppermute | solution.py:108
  61.1 5.4 %collective-permute-start.6 = (f32[24,4]{1,0:T(8,128)S(1)}, f32[24,4]{1,0:T(8,128)S(1)}, u32[]{:S(2)}, u32[]{:S(2)}) collective-permute-start(f32[24,4]{1,0:T(8,128)S(1)} %get-tuple-element.80), channel_id=1, source_target_pairs={{0,1},{1,2},{2,3},{3,4},{4,5},{5,6},{6,7},{7,8},{8,9},{9,10},{10,1... | collective-permute-start | bytes 1160 | tf_op jit(solution)/shard_map/ppermute | solution.py:108
  65.1 6.3 %collective-permute-start.7 = (f32[24,4]{1,0:T(8,128)S(1)}, f32[24,4]{1,0:T(8,128)S(1)}, u32[]{:S(2)}, u32[]{:S(2)}) collective-permute-start(f32[24,4]{1,0:T(8,128)S(1)} %get-tuple-element.81), channel_id=1, source_target_pairs={{1,0},{2,1},{3,2},{4,3},{5,4},{6,5},{7,6},{8,7},{9,8},{10,9},{11,1... | collective-permute-start | bytes 1160 | tf_op jit(solution)/shard_map/ppermute | solution.py:108

commit v9 on v8

--- a/solution.py
+++ b/solution.py
@@ -90,6 +90,24 @@
 RELAX = moment_table()
 
 
+def relax_groups():
+    rows = []
+    for line in RELAX:
+        groups = []
+        for l, value in enumerate(line):
+            for group in groups:
+                if abs(group[0] - value) <= 1e-12 * max(1.0, abs(value)):
+                    group[1].append(l)
+                    break
+            else:
+                groups.append((value, [l]))
+        rows.append(groups)
+    return rows
+
+
+RELAX_GROUPS = relax_groups()
+
+
 def halo(cells, w):
     return halo_many([cells], [w])[0]
 
@@ -155,8 +173,11 @@
     q = []
     for j in range(19):
         acc = None
-        for l in range(19):
-            t = RELAX[j][l] * g[l]
+        for value, members in RELAX_GROUPS[j]:
+            part = g[members[0]]
+            for l in members[1:]:
+                part = part + g[l]
+            t = value * part
             acc = t if acc is None else acc + t
         q.append(acc)
     tsum = None
@@ -294,7 +315,7 @@
     first, term_ext = adjoint_step(
         0,
         pulled,
-        pad_to(saved_ext, rows, cols)[None],
+        pad_to(saved_ext, rows, cols).astype(jnp.bfloat16)[None],
         pad_to(block_ext, rows, cols),
         pad_to(jnp.pad(lever, ((0, 0), (1, 1), (1, 1))), rows, cols),
     )

time: 117 us -> 115 us (0.983)
  Pallas kernels: 11.2 us -> 9.93 us
    pallas_call x2, Pallas kernels: 11.2 us -> 9.93 us  [adjoint_step(): pl.pallas_call(functools.partial(step_kernel, section, rows), out_shape=(...]
where the time goes in v9:
time: 115 us; the launch traced here: 114 us
  blocking collectives  37.3 us (32%)
  starting transfers between devices  25.2 us (22%)
  other arithmetic  17 us (15%)
  local copies, waits for them, and re-layouts  12.5 us (11%)
  waiting for transfers between devices  10.6 us (9%)
  Pallas kernels  9.93 us (9%)
  between operations  1.32 us (1%)
    all_to_all x1, blocking collectives, global_sum(): return jnp.sum(lax.all_to_all(rows, axes, 0, 0, tiled=True), axis=0)  37.3 us
    ppermute x4, starting transfers between devices, send(): got = lax.ppermute(flat, axis, pairs)  15.1 us
    ppermute x4, starting transfers between devices, send(): return [lax.ppermute(pieces[0], axis, pairs)]  10.1 us
    pallas_call x2, Pallas kernels, adjoint_step(): pl.pallas_call(functools.partial(step_kernel, section, rows), out_shape=(...  9.93 us
    ppermute x4, waiting for transfers between devices, send(): return [lax.ppermute(pieces[0], axis, pairs)]  7.87 us
    slice x8, local copies, waits for them, and re-layouts, halo_many(): tails.append(lax.slice_in_dim(a, size - w, size, axis=a.ndim + dim))  2.82 us
    ppermute x4, waiting for transfers between devices, send(): got = lax.ppermute(flat, axis, pairs)  2.71 us
    another operation x1, other arithmetic, per_device(): jnp.stack([jnp.sum(smooth * region_one), jnp.sum(smooth * region_two), jn...  2.58 us
  transfers between devices with their start and end apart: 8, of which 4 were waited for; matrix products, arithmetic and copies ran while one was open for 2% of the time, Pallas kernels for 0%

profile of v9, /device:TPU:1, one launch (start us, length us, event | category | flops | bytes accessed | tf_op | source)
XLA Modules:
  0.0 113.9 jit_solution(3450157955834494060)
XLA Ops:
  0.6 0.8 multiply_select_fusion
  1.4 0.8 and_select_fusion
  2.2 1.0 bitcast_convert_fusion
  3.3 0.2 slice_reduce_fusion.5
  3.5 1.1 fusion.64
  4.7 4.6 %collective-permute-start = (f32[29696]{0:T(1024)S(1)}, f32[29696]{0:T(1024)S(1)}, u32[]{:S(2)}, u32[]{:S(2)}) collective-permute-start(f32[29696]{0:T(1024)S(1)} %pad_maximum_fusion.2), channel_id=1, source_target_pairs={{0,32},{32,64},{64,96},{96,128},{128,160},{160,192},{192,224},{224... | collective-permute-start | bytes 356360 | tf_op jit(solution)/shard_map/ppermute | solution.py:128
  9.3 5.5 %collective-permute-start.1 = (f32[29696]{0:T(1024)S(1)}, f32[29696]{0:T(1024)S(1)}, u32[]{:S(2)}, u32[]{:S(2)}) collective-permute-start(f32[29696]{0:T(1024)S(1)} %pad_maximum_fusion.3), channel_id=1, source_target_pairs={{32,0},{64,32},{96,64},{128,96},{160,128},{192,160},{224,192},{256... | collective-permute-start | bytes 356360 | tf_op jit(solution)/shard_map/ppermute | solution.py:128
  14.9 0.7 pad.268.l_ref
  15.7 0.6 copy-done.5
  16.4 0.1 pad_maximum_fusion
  16.5 0.3 fusion.63
  16.8 0.3 reshape.188
  17.1 0.7 slice.773
  17.8 0.2 slice_reduce_fusion.3
  18.1 0.8 slice.770
  19.0 0.2 pad_maximum_fusion.1
  19.1 0.9 slice_reduce_fusion.1
  20.3 3.7 %collective-permute-start.2 = (f32[4480]{0:T(1024)S(1)}, f32[4480]{0:T(1024)S(1)}, u32[]{:S(2)}, u32[]{:S(2)}) collective-permute-start(f32[4480]{0:T(1024)S(1)} %concatenate.120), channel_id=1, source_target_pairs={{0,1},{1,2},{2,3},{3,4},{4,5},{5,6},{6,7},{7,8},{8,9},{9,10},{10,1... | collective-permute-start | bytes 53768 | tf_op jit(solution)/shard_map/ppermute | solution.py:128
  24.0 0.3 reshape.192
  24.6 1.3 %collective-permute-start.3 = (f32[4480]{0:T(1024)S(1)}, f32[4480]{0:T(1024)S(1)}, u32[]{:S(2)}, u32[]{:S(2)}) collective-permute-start(f32[4480]{0:T(1024)S(1)} %concatenate.121), channel_id=1, source_target_pairs={{1,0},{2,1},{3,2},{4,3},{5,4},{6,5},{7,6},{8,7},{9,8},{10,9},{11,1... | collective-permute-start | bytes 53768 | tf_op jit(solution)/shard_map/ppermute | solution.py:128
  25.9 0.9 fusion.61
  26.8 0.3 reshape.191
  27.1 2.6 %collective-permute-done.3 = f32[4480]{0:T(1024)S(1)} collective-permute-done((f32[4480]{0:T(1024)S(1)}, f32[4480]{0:T(1024)S(1)}, u32[]{:S(2)}, u32[]{:S(2)}) %collective-permute-start.3) | collective-permute-done | bytes 17952 | tf_op jit(solution)/shard_map/ppermute | solution.py:128
  29.7 0.3 reshape.195
  30.0 0.2 maximum_bitcast_fusion.16
  30.5 0.2 maximum_bitcast_fusion.13
  32.0 1.4 %pad.32.g_ref = f32[19,4,24,256]{3,2,1,0:T(8,128)} pad(f32[19,4,18,130]{3,2,1,0:T(8,128)S(1)} %fusion.28, f32[]{:T(128)} %constant.56.clone.1), padding=0_0x0_0x0_6x0_126 | pad | bytes 2579140 | tf_op jit(solution)/shard_map/jit(_pad)/pad | solution.py:299
  33.5 0.4 reshape.201
  33.9 0.4 reshape.202
  34.8 0.8 select_maximum_fusion.b_ref
  35.5 1.6 %fusion.9.f_ref = bf16[1,19,4,24,256]{4,3,2,1,0:T(8,128)(2,1)} fusion(bf16[19,4,18,1]{3,2,1,0:T(8,128)(2,1)S(1)} %reshape.202, bf16[19,4,18,128]{3,2,1,0:T(8,128)(2,1)S(1)} %copy-done.1, bf16[19,4,18,1]{3,2,1,0:T(8,128)(2,1)S(1)} %reshape.201), kind=kLoop, calls=%fused_computation.12 | loop fusion | flops 7004160 | bytes 1289568 | tf_op jit(solution)/shard_map/broadcast_in_dim | solution.py:318
  37.2 6.6 %shard_map.68 = (f32[19,4,24,256]{3,2,1,0:T(8,128)}, f32[24,256]{1,0:T(8,128)}) custom-call(f32[19,4,24,256]{3,2,1,0:T(8,128)} %pad.32.g_ref, bf16[1,19,4,24,256]{4,3,2,1,0:T(8,128)(2,1)} %fusion.9.f_ref, f32[4,24,256]{2,1,0:T(8,128)} %select_maximum_fusion.b_ref, f32[4,24,256]{2,1,0:T(8,128)} %pad.268.l_ref), custom_call_target="tpu_custom_call" | custom-call | tf_op jit(solution)/shard_map/pallas_call | solution.py:267
  43.7 1.7 %slice_select_fusion = f32[19,4,18,130]{3,2,1,0:T(8,128)S(1)} fusion(f32[19,4,24,256]{3,2,1,0:T(8,128)} %get-tuple-element.6, pred[18,130]{1,0:T(8,128)(4,1)S(1)} %and_and_fusion.1), kind=kLoop, calls=%fused_computation.6 | loop fusion | flops 177840 | bytes 1425060 | tf_op jit(solution)/shard_map/jit(_where)/select_n | solution.py:329
  46.3 0.8 copy-done.2
  47.1 3.3 %shard_map.69 = (f32[19,4,16,128]{3,2,1,0:T(8,128)}, f32[16,128]{1,0:T(8,128)}) custom-call(f32[19,4,16,128]{3,2,1,0:T(8,128)} %copy-done.2, bf16[2,19,4,16,128]{4,3,2,1,0:T(8,128)(2,1)} %f_ref.1, f32[4,16,128]{2,1,0:T(8,128)} %copy-done.3, f32[4,16,128]{2,1,0:T(8,128)} %copy-done.4), custom_call_target="tpu_custom_call" | custom-call | tf_op jit(solution)/shard_map/pallas_call | solution.py:267
  50.4 0.8 add_multiply_fusion
  51.2 2.9 %collective-permute-start.4 = (f32[4,128]{1,0:T(4,128)S(1)}, f32[4,128]{1,0:T(4,128)S(1)}, u32[]{:S(2)}, u32[]{:S(2)}) collective-permute-start(f32[4,128]{1,0:T(4,128)S(1)} %get-tuple-element.82), channel_id=1, source_target_pairs={{0,32},{32,64},{64,96},{96,128},{128,160},{160,192},{192,224},{224... | collective-permute-start | bytes 6152 | tf_op jit(solution)/shard_map/ppermute | solution.py:126
  54.2 1.9 %collective-permute-start.5 = (f32[4,128]{1,0:T(4,128)S(1)}, f32[4,128]{1,0:T(4,128)S(1)}, u32[]{:S(2)}, u32[]{:S(2)}) collective-permute-start(f32[4,128]{1,0:T(4,128)S(1)} %get-tuple-element.83), channel_id=1, source_target_pairs={{32,0},{64,32},{96,64},{128,96},{160,128},{192,160},{224,192},{256... | collective-permute-start | bytes 6152 | tf_op jit(solution)/shard_map/ppermute | solution.py:126
  56.1 3.0 %collective-permute-done.5 = f32[4,128]{1,0:T(4,128)S(1)} collective-permute-done((f32[4,128]{1,0:T(4,128)S(1)}, f32[4,128]{1,0:T(4,128)S(1)}, u32[]{:S(2)}, u32[]{:S(2)}) %collective-permute-start.5) | collective-permute-done | bytes 2080 | tf_op jit(solution)/shard_map/ppermute | solution.py:126
  59.2 4.0 %collective-permute-start.6 = (f32[24,4]{1,0:T(8,128)S(1)}, f32[24,4]{1,0:T(8,128)S(1)}, u32[]{:S(2)}, u32[]{:S(2)}) collective-permute-start(f32[24,4]{1,0:T(8,128)S(1)} %get-tuple-element.80), channel_id=1, source_target_pairs={{0,1},{1,2},{2,3},{3,4},{4,5},{5,6},{6,7},{7,8},{8,9},{9,10},{10,1... | collective-permute-start | bytes 1160 | tf_op jit(solution)/shard_map/ppermute | solution.py:126
  63.2 1.3 %collective-permute-start.7 = (f32[24,4]{1,0:T(8,128)S(1)}, f32[24,4]{1,0:T(8,128)S(1)}, u32[]{:S(2)}, u32[]{:S(2)}) collective-permute-start(f32[24,4]{1,0:T(8,128)S(1)} %get-tuple-element.81), channel_id=1, source_target_pairs={{1,0},{2,1},{3,2},{4,3},{5,4},{6,5},{7,6},{8,7},{9,8},{10,9},{11,1... | collective-permute-start | bytes 1160 | tf_op jit(solution)/shard_map/ppermute | solution.py:126
  64.6 4.9 %collective-permute-done.7 = f32[24,4]{1,0:T(8,128)S(1)} collective-permute-done((f32[24,4]{1,0:T(8,128)S(1)}, f32[24,4]{1,0:T(8,128)S(1)}, u32[]{:S(2)}, u32[]{:S(2)}) %collective-permute-start.7) | collective-permute-done | bytes 416 | tf_op jit(solution)/shard_map/ppermute | solution.py:126
  70.0 0.8 select_reduce_fusion.1
  70.7 2.6 %pad_maximum_fusion.17 = f32[4]{0:T(128)S(1)} fusion(f32[1]{0:T(128)} %bitcast.74, f32[1]{0:T(128)} %bitcast.73, f32[1]{0:T(128)} %bitcast.72, f32[1]{0:T(128)} %bitcast.71), kind=kLoop, calls=%fused_computation.216 | loop fusion | flops 12 | bytes 32 | tf_op jit(solution)/shard_map/stack | solution.py:337
  73.5 37.3 %all_to_all.6 = f32[512,1,4]{2,1,0:T(1,128)S(1)} all-to-all(f32[512,1,4]{2,1,0:T(1,128)S(1)} %broadcast_in_dim.60), channel_id=1, replica_groups=mesh['gx'=16,'gy'=32] {'gx','gy'}, dimensions={0} | all-to-all | bytes 16384 | tf_op jit(solution)/shard_map/all_to_all | solution.py:145
  110.7 0.6 reduce_sum.49
  111.4 0.7 fusion.68
  112.0 1.8 %select_add_fusion = f32[16,128]{1,0:T(8,128)} fusion(pred[16,128]{1,0:T(8,128)(4,1)S(1)} %get-tuple-element.22, f32[16,128]{1,0:T(8,128)S(1)} %get-tuple-element.21, pred[16,128]{1,0:T(8,128)(4,1)S(1)} %get-tuple-element.20, f32[]{:T(128)} %bitcast.76, f32[]{:T(128)} %bitcast.75), kind=kLoop, calls=%fused_computation.198 | loop fusion | flops 10240 | bytes 20488 | tf_op jit(solution)/shard_map/add | solution.py:347
  (103 shorter events, 4.5 us)
Async XLA Ops:
  0.6 15.7 %copy-start = (f32[19,4,16,128]{3,2,1,0:T(8,128)S(1)}, f32[19,4,16,128]{3,2,1,0:T(8,128)}, u32[]{:S(2)}) copy-start(f32[19,4,16,128]{3,2,1,0:T(8,128)} %param.5) | copy-start | bytes 1867780
  2.2 14.3 %copy-start.4 = (f32[4,16,128]{2,1,0:T(8,128)}, f32[4,16,128]{2,1,0:T(8,128)S(1)}, u32[]{:S(2)}) copy-start(f32[4,16,128]{2,1,0:T(8,128)S(1)} %get-tuple-element.73.l_ref) | copy-start | bytes 98308
  2.2 32.5 %copy-start.3 = (f32[4,16,128]{2,1,0:T(8,128)}, f32[4,16,128]{2,1,0:T(8,128)S(1)}, u32[]{:S(2)}) copy-start(f32[4,16,128]{2,1,0:T(8,128)S(1)} %get-tuple-element.74.b_ref) | copy-start | bytes 98308
  4.7 11.0 %collective-permute-start = (f32[29696]{0:T(1024)S(1)}, f32[29696]{0:T(1024)S(1)}, u32[]{:S(2)}, u32[]{:S(2)}) collective-permute-start(f32[29696]{0:T(1024)S(1)} %pad_maximum_fusion.2), channel_id=1, source_target_pairs={{0,32},{32,64},{64,96},{96,128},{128,160},{160,192},{192,224},{224... | collective-permute-start | bytes 356360 | tf_op jit(solution)/shard_map/ppermute | solution.py:128
  9.3 6.4 %collective-permute-start.1 = (f32[29696]{0:T(1024)S(1)}, f32[29696]{0:T(1024)S(1)}, u32[]{:S(2)}, u32[]{:S(2)}) collective-permute-start(f32[29696]{0:T(1024)S(1)} %pad_maximum_fusion.3), channel_id=1, source_target_pairs={{32,0},{64,32},{96,64},{128,96},{160,128},{192,160},{224,192},{256... | collective-permute-start | bytes 356360 | tf_op jit(solution)/shard_map/ppermute | solution.py:128
  15.7 0.6 copy-start.5
  20.3 6.6 %collective-permute-start.2 = (f32[4480]{0:T(1024)S(1)}, f32[4480]{0:T(1024)S(1)}, u32[]{:S(2)}, u32[]{:S(2)}) collective-permute-start(f32[4480]{0:T(1024)S(1)} %concatenate.120), channel_id=1, source_target_pairs={{0,1},{1,2},{2,3},{3,4},{4,5},{5,6},{6,7},{7,8},{8,9},{9,10},{10,1... | collective-permute-start | bytes 53768 | tf_op jit(solution)/shard_map/ppermute | solution.py:128
  24.6 5.2 %collective-permute-start.3 = (f32[4480]{0:T(1024)S(1)}, f32[4480]{0:T(1024)S(1)}, u32[]{:S(2)}, u32[]{:S(2)}) collective-permute-start(f32[4480]{0:T(1024)S(1)} %concatenate.121), channel_id=1, source_target_pairs={{1,0},{2,1},{3,2},{4,3},{5,4},{6,5},{7,6},{8,7},{9,8},{10,9},{11,1... | collective-permute-start | bytes 53768 | tf_op jit(solution)/shard_map/ppermute | solution.py:128
  32.0 3.5 %copy-start.1 = (bf16[19,4,18,128]{3,2,1,0:T(8,128)(2,1)S(1)}, bf16[19,4,18,128]{3,2,1,0:T(8,128)(2,1)}, u32[]{:S(2)}) copy-start(bf16[19,4,18,128]{3,2,1,0:T(8,128)(2,1)} %fusion.61) | copy-start | bytes 1050628
  45.5 24.5 %copy-start.6 = (s32[16,128]{1,0:T(8,128)S(1)}, s32[16,128]{1,0:T(8,128)}, u32[]{:S(2)}) copy-start(s32[16,128]{1,0:T(8,128)} %param.8) | copy-start | bytes 24580
  46.2 0.8 copy-start.2
  51.2 4.9 %collective-permute-start.4 = (f32[4,128]{1,0:T(4,128)S(1)}, f32[4,128]{1,0:T(4,128)S(1)}, u32[]{:S(2)}, u32[]{:S(2)}) collective-permute-start(f32[4,128]{1,0:T(4,128)S(1)} %get-tuple-element.82), channel_id=1, source_target_pairs={{0,32},{32,64},{64,96},{96,128},{128,160},{160,192},{192,224},{224... | collective-permute-start | bytes 6152 | tf_op jit(solution)/shard_map/ppermute | solution.py:126
  54.2 4.9 %collective-permute-start.5 = (f32[4,128]{1,0:T(4,128)S(1)}, f32[4,128]{1,0:T(4,128)S(1)}, u32[]{:S(2)}, u32[]{:S(2)}) collective-permute-start(f32[4,128]{1,0:T(4,128)S(1)} %get-tuple-element.83), channel_id=1, source_target_pairs={{32,0},{64,32},{96,64},{128,96},{160,128},{192,160},{224,192},{256... | collective-permute-start | bytes 6152 | tf_op jit(solution)/shard_map/ppermute | solution.py:126
  59.2 5.4 %collective-permute-start.6 = (f32[24,4]{1,0:T(8,128)S(1)}, f32[24,4]{1,0:T(8,128)S(1)}, u32[]{:S(2)}, u32[]{:S(2)}) collective-permute-start(f32[24,4]{1,0:T(8,128)S(1)} %get-tuple-element.80), channel_id=1, source_target_pairs={{0,1},{1,2},{2,3},{3,4},{4,5},{5,6},{6,7},{7,8},{8,9},{9,10},{10,1... | collective-permute-start | bytes 1160 | tf_op jit(solution)/shard_map/ppermute | solution.py:126
  63.2 6.3 %collective-permute-start.7 = (f32[24,4]{1,0:T(8,128)S(1)}, f32[24,4]{1,0:T(8,128)S(1)}, u32[]{:S(2)}, u32[]{:S(2)}) collective-permute-start(f32[24,4]{1,0:T(8,128)S(1)} %get-tuple-element.81), channel_id=1, source_target_pairs={{1,0},{2,1},{3,2},{4,3},{5,4},{6,5},{7,6},{8,7},{9,8},{10,9},{11,1... | collective-permute-start | bytes 1160 | tf_op jit(solution)/shard_map/ppermute | solution.py:126

commit v10 on v9

--- a/solution.py
+++ b/solution.py
@@ -123,12 +123,13 @@
 
         def send(pieces, pairs):
             if len(pieces) == 1:
-                return [lax.ppermute(pieces[0], axis, pairs)]
-            flat = jnp.concatenate([p.reshape(-1) for p in pieces])
+                got = lax.ppermute(pieces[0].astype(jnp.float32), axis, pairs)
+                return [got.astype(pieces[0].dtype)]
+            flat = jnp.concatenate([p.astype(jnp.float32).reshape(-1) for p in pieces])
             got = lax.ppermute(flat, axis, pairs)
             out, at = [], 0
             for p in pieces:
-                out.append(got[at : at + p.size].reshape(p.shape))
+                out.append(got[at : at + p.size].reshape(p.shape).astype(p.dtype))
                 at += p.size
             return out
 
@@ -306,7 +307,7 @@
         solid_mask == 1, 1.0, jnp.where(inside[None], BLOCK_LIMIT * design[None], 0.0)
     ).astype(jnp.float32)
     lever = jnp.where((solid_mask == 0) & inside[None], BLOCK_LIMIT, 0.0).astype(jnp.float32)
-    saved_one = forward_pops[1].astype(jnp.float32)
+    saved_one = forward_pops[1]
     adj_ext, saved_ext, block_ext = halo_many([adjoint_in, saved_one, blocking], [2, 1, 1])
     ext_x, ext_y = width_x + 2, width_y + 2
     rows = -(-ext_x // 8) * 8
@@ -315,7 +316,7 @@
     first, term_ext = adjoint_step(
         0,
         pulled,
-        pad_to(saved_ext, rows, cols).astype(jnp.bfloat16)[None],
+        pad_to(saved_ext, rows, cols)[None],
         pad_to(block_ext, rows, cols),
         pad_to(jnp.pad(lever, ((0, 0), (1, 1), (1, 1))), rows, cols),
     )

time: 115 us -> 113 us (0.983)
  local copies, waits for them, and re-layouts: 12.5 us -> 10.3 us
    slice x14 -> x12, local copies, waits for them, and re-layouts: 1.88 us -> 0.33 us  [send(): out.append(got[at:at + p.size].reshape(p.shape).astype(p.dtype))]
    slice x8 -> x6, local copies, waits for them, and re-layouts: 2.82 us -> 1.69 us  [halo_many(): tails.append(lax.slice_in_dim(a, size - w, size, axis=a.ndim + dim))]
    reshape x14 -> x12, local copies, waits for them, and re-layouts: 2.61 us -> 1.85 us  [the longest x8 1.02 us: send(): flat = jnp.concatenate([p.astype(jnp.float32).reshape(-1) for p in pieces])]
where the time goes in v10:
time: 113 us; the launch traced here: 112 us
  blocking collectives  37.3 us (33%)
  starting transfers between devices  25.2 us (22%)
  other arithmetic  16.6 us (15%)
  waiting for transfers between devices  11.5 us (10%)
  local copies, waits for them, and re-layouts  10.3 us (9%)
  Pallas kernels  9.91 us (9%)
  between operations  1.32 us (1%)
    all_to_all x1, blocking collectives, global_sum(): return jnp.sum(lax.all_to_all(rows, axes, 0, 0, tiled=True), axis=0)  37.3 us
    ppermute x4, starting transfers between devices, send(): got = lax.ppermute(flat, axis, pairs)  15.1 us
    ppermute x4, starting transfers between devices, send(): got = lax.ppermute(pieces[0].astype(jnp.float32), axis, pairs)  10.1 us
    pallas_call x2, Pallas kernels, adjoint_step(): pl.pallas_call(functools.partial(step_kernel, section, rows), out_shape=(...  9.91 us
    ppermute x4, waiting for transfers between devices, send(): got = lax.ppermute(pieces[0].astype(jnp.float32), axis, pairs)  7.87 us
    ppermute x4, waiting for transfers between devices, send(): got = lax.ppermute(flat, axis, pairs)  3.63 us
    another operation x1, other arithmetic, per_device(): jnp.stack([jnp.sum(smooth * region_one), jnp.sum(smooth * region_two), jn...  2.53 us
  transfers between devices with their start and end apart: 8, of which 4 were waited for; matrix products, arithmetic and copies ran while one was open for 2% of the time, Pallas kernels for 0%

profile of v10, /device:TPU:1, one launch (start us, length us, event | category | flops | bytes accessed | tf_op | source)
XLA Modules:
  0.0 112.1 jit_solution(623136824866405593)
XLA Ops:
  0.6 0.8 multiply_select_fusion
  1.4 0.8 and_select_fusion
  2.2 1.0 slice_bitcast_fusion
  3.2 0.2 fusion.37
  3.5 1.1 %fusion.71 = (f32[19,4,2,128]{3,2,1,0:T(2,128)S(1)}, f32[19,4,2,128]{3,2,1,0:T(2,128)S(1)}) fusion(f32[19,4,16,128]{3,2,1,0:T(8,128)} %param.5), kind=kLoop, calls=%fused_computation.229 | loop fusion | bytes 311296 | tf_op jit(solution)/shard_map/slice | solution.py:122
  4.6 4.6 %collective-permute-start = (f32[29696]{0:T(1024)S(1)}, f32[29696]{0:T(1024)S(1)}, u32[]{:S(2)}, u32[]{:S(2)}) collective-permute-start(f32[29696]{0:T(1024)S(1)} %pad_maximum_fusion.2), channel_id=1, source_target_pairs={{0,32},{32,64},{64,96},{96,128},{128,160},{160,192},{192,224},{224... | collective-permute-start | bytes 356360 | tf_op jit(solution)/shard_map/ppermute | solution.py:129
  9.3 5.5 %collective-permute-start.1 = (f32[29696]{0:T(1024)S(1)}, f32[29696]{0:T(1024)S(1)}, u32[]{:S(2)}, u32[]{:S(2)}) collective-permute-start(f32[29696]{0:T(1024)S(1)} %pad_maximum_fusion.3), channel_id=1, source_target_pairs={{32,0},{64,32},{96,64},{128,96},{160,128},{192,160},{224,192},{256... | collective-permute-start | bytes 356360 | tf_op jit(solution)/shard_map/ppermute | solution.py:129
  14.9 0.8 collective-permute-done.1
  15.7 0.1 pad_maximum_fusion
  15.8 0.3 fusion.70
  16.2 0.3 reshape.228
  16.5 0.2 slice_reduce_fusion.1
  16.8 0.3 pad_maximum_fusion.1
  17.1 0.8 convert_reduce_fusion.1
  17.9 0.1 reshape.245
  18.1 3.7 %collective-permute-start.2 = (f32[4480]{0:T(1024)S(1)}, f32[4480]{0:T(1024)S(1)}, u32[]{:S(2)}, u32[]{:S(2)}) collective-permute-start(f32[4480]{0:T(1024)S(1)} %concatenate.119), channel_id=1, source_target_pairs={{0,1},{1,2},{2,3},{3,4},{4,5},{5,6},{6,7},{7,8},{8,9},{9,10},{10,1... | collective-permute-start | bytes 53768 | tf_op jit(solution)/shard_map/ppermute | solution.py:129
  21.8 0.3 reshape.233
  22.4 1.3 %collective-permute-start.3 = (f32[4480]{0:T(1024)S(1)}, f32[4480]{0:T(1024)S(1)}, u32[]{:S(2)}, u32[]{:S(2)}) collective-permute-start(f32[4480]{0:T(1024)S(1)} %concatenate.120), channel_id=1, source_target_pairs={{1,0},{2,1},{3,2},{4,3},{5,4},{6,5},{7,6},{8,7},{9,8},{10,9},{11,1... | collective-permute-start | bytes 53768 | tf_op jit(solution)/shard_map/ppermute | solution.py:129
  23.7 0.7 pad.272.l_ref
  24.5 0.3 reshape.232
  24.8 2.8 %collective-permute-done.3 = f32[4480]{0:T(1024)S(1)} collective-permute-done((f32[4480]{0:T(1024)S(1)}, f32[4480]{0:T(1024)S(1)}, u32[]{:S(2)}, u32[]{:S(2)}) %collective-permute-start.3) | collective-permute-done | bytes 17952 | tf_op jit(solution)/shard_map/ppermute | solution.py:129
  27.6 0.3 reshape.237
  28.0 0.2 maximum_bitcast_fusion.16
  28.4 0.2 maximum_bitcast_fusion.13
  29.8 1.4 %pad.32.g_ref = f32[19,4,24,256]{3,2,1,0:T(8,128)} pad(f32[19,4,18,130]{3,2,1,0:T(8,128)S(1)} %fusion.34, f32[]{:T(128)} %constant.56.clone.1), padding=0_0x0_0x0_6x0_126 | pad | bytes 2579140 | tf_op jit(solution)/shard_map/jit(_pad)/pad | solution.py:300
  31.3 0.4 convert_element_type.66
  31.7 0.4 convert_element_type.67
  32.2 0.1 reshape.248
  32.4 0.1 reshape.249
  32.6 2.1 %fusion.9.f_ref = bf16[1,19,4,24,256]{4,3,2,1,0:T(8,128)(2,1)} fusion(bf16[19,4,18,1]{3,2,1,0:T(8,128)(2,1)S(1)} %convert_element_type.67, bf16[19,4,18,1]{3,2,1,0:T(8,128)(2,1)S(1)} %convert_element_type.66, bf16[19,4,1,128]{3,2,1,0:T(2,128)(2,1)S(1)} %convert_element_type.65, bf16[19,4,16,128]{3,2,1,0:T(8,128)(2,1)S(1)} %slice_bitcast_fusion, ...), kind=kLoop, calls=%fused_computation.12 | loop fusion | flops 10739712 | bytes 1289568 | tf_op jit(solution)/shard_map/broadcast_in_dim | solution.py:319
  34.7 0.8 select_maximum_fusion.b_ref
  35.4 6.6 %shard_map.68 = (f32[19,4,24,256]{3,2,1,0:T(8,128)}, f32[24,256]{1,0:T(8,128)}) custom-call(f32[19,4,24,256]{3,2,1,0:T(8,128)} %pad.32.g_ref, bf16[1,19,4,24,256]{4,3,2,1,0:T(8,128)(2,1)} %fusion.9.f_ref, f32[4,24,256]{2,1,0:T(8,128)} %select_maximum_fusion.b_ref, f32[4,24,256]{2,1,0:T(8,128)} %pad.272.l_ref), custom_call_target="tpu_custom_call" | custom-call | tf_op jit(solution)/shard_map/pallas_call | solution.py:268
  42.0 1.7 %slice_select_fusion = f32[19,4,18,130]{3,2,1,0:T(8,128)S(1)} fusion(f32[19,4,24,256]{3,2,1,0:T(8,128)} %get-tuple-element.6, pred[18,130]{1,0:T(8,128)(4,1)S(1)} %and_and_fusion.1), kind=kLoop, calls=%fused_computation.8 | loop fusion | flops 177840 | bytes 1425060 | tf_op jit(solution)/shard_map/jit(_where)/select_n | solution.py:330
  44.5 0.8 copy-done.1
  45.3 3.3 %shard_map.69 = (f32[19,4,16,128]{3,2,1,0:T(8,128)}, f32[16,128]{1,0:T(8,128)}) custom-call(f32[19,4,16,128]{3,2,1,0:T(8,128)} %copy-done.1, bf16[2,19,4,16,128]{4,3,2,1,0:T(8,128)(2,1)} %f_ref.1, f32[4,16,128]{2,1,0:T(8,128)} %copy-done.2, f32[4,16,128]{2,1,0:T(8,128)} %copy-done.3), custom_call_target="tpu_custom_call" | custom-call | tf_op jit(solution)/shard_map/pallas_call | solution.py:268
  48.7 0.8 add_multiply_fusion
  49.5 2.9 %collective-permute-start.4 = (f32[4,128]{1,0:T(4,128)S(1)}, f32[4,128]{1,0:T(4,128)S(1)}, u32[]{:S(2)}, u32[]{:S(2)}) collective-permute-start(f32[4,128]{1,0:T(4,128)S(1)} %get-tuple-element.82), channel_id=1, source_target_pairs={{0,32},{32,64},{64,96},{96,128},{128,160},{160,192},{192,224},{224... | collective-permute-start | bytes 6152 | tf_op jit(solution)/shard_map/ppermute | solution.py:126
  52.4 1.9 %collective-permute-start.5 = (f32[4,128]{1,0:T(4,128)S(1)}, f32[4,128]{1,0:T(4,128)S(1)}, u32[]{:S(2)}, u32[]{:S(2)}) collective-permute-start(f32[4,128]{1,0:T(4,128)S(1)} %get-tuple-element.83), channel_id=1, source_target_pairs={{32,0},{64,32},{96,64},{128,96},{160,128},{192,160},{224,192},{256... | collective-permute-start | bytes 6152 | tf_op jit(solution)/shard_map/ppermute | solution.py:126
  54.4 3.0 %collective-permute-done.5 = f32[4,128]{1,0:T(4,128)S(1)} collective-permute-done((f32[4,128]{1,0:T(4,128)S(1)}, f32[4,128]{1,0:T(4,128)S(1)}, u32[]{:S(2)}, u32[]{:S(2)}) %collective-permute-start.5) | collective-permute-done | bytes 2080 | tf_op jit(solution)/shard_map/ppermute | solution.py:126
  57.4 4.0 %collective-permute-start.6 = (f32[24,4]{1,0:T(8,128)S(1)}, f32[24,4]{1,0:T(8,128)S(1)}, u32[]{:S(2)}, u32[]{:S(2)}) collective-permute-start(f32[24,4]{1,0:T(8,128)S(1)} %get-tuple-element.80), channel_id=1, source_target_pairs={{0,1},{1,2},{2,3},{3,4},{4,5},{5,6},{6,7},{7,8},{8,9},{9,10},{10,1... | collective-permute-start | bytes 1160 | tf_op jit(solution)/shard_map/ppermute | solution.py:126
  61.4 1.3 %collective-permute-start.7 = (f32[24,4]{1,0:T(8,128)S(1)}, f32[24,4]{1,0:T(8,128)S(1)}, u32[]{:S(2)}, u32[]{:S(2)}) collective-permute-start(f32[24,4]{1,0:T(8,128)S(1)} %get-tuple-element.81), channel_id=1, source_target_pairs={{1,0},{2,1},{3,2},{4,3},{5,4},{6,5},{7,6},{8,7},{9,8},{10,9},{11,1... | collective-permute-start | bytes 1160 | tf_op jit(solution)/shard_map/ppermute | solution.py:126
  62.8 4.9 %collective-permute-done.7 = f32[24,4]{1,0:T(8,128)S(1)} collective-permute-done((f32[24,4]{1,0:T(8,128)S(1)}, f32[24,4]{1,0:T(8,128)S(1)}, u32[]{:S(2)}, u32[]{:S(2)}) %collective-permute-start.7) | collective-permute-done | bytes 416 | tf_op jit(solution)/shard_map/ppermute | solution.py:126
  68.2 0.8 select_reduce_fusion.1
  69.0 2.5 %pad_maximum_fusion.17 = f32[4]{0:T(128)S(1)} fusion(f32[1]{0:T(128)} %bitcast.73, f32[1]{0:T(128)} %bitcast.72, f32[1]{0:T(128)} %bitcast.71, f32[1]{0:T(128)} %bitcast.70), kind=kLoop, calls=%fused_computation.226 | loop fusion | flops 12 | bytes 32 | tf_op jit(solution)/shard_map/stack | solution.py:338
  71.7 37.3 %all_to_all.6 = f32[512,1,4]{2,1,0:T(1,128)S(1)} all-to-all(f32[512,1,4]{2,1,0:T(1,128)S(1)} %broadcast_in_dim.60), channel_id=1, replica_groups=mesh['gx'=16,'gy'=32] {'gx','gy'}, dimensions={0} | all-to-all | bytes 16384 | tf_op jit(solution)/shard_map/all_to_all | solution.py:146
  108.9 0.6 reduce_sum.49
  109.6 0.7 fusion.75
  110.2 1.8 %select_add_fusion = f32[16,128]{1,0:T(8,128)} fusion(pred[16,128]{1,0:T(8,128)(4,1)S(1)} %get-tuple-element.22, f32[16,128]{1,0:T(8,128)S(1)} %get-tuple-element.21, pred[16,128]{1,0:T(8,128)(4,1)S(1)} %get-tuple-element.20, f32[]{:T(128)} %bitcast.75, f32[]{:T(128)} %bitcast.74), kind=kLoop, calls=%fused_computation.208 | loop fusion | flops 10240 | bytes 20488 | tf_op jit(solution)/shard_map/add | solution.py:348
  (98 shorter events, 3.9 us)
Async XLA Ops:
  0.6 15.1 %copy-start = (f32[19,4,16,128]{3,2,1,0:T(8,128)S(1)}, f32[19,4,16,128]{3,2,1,0:T(8,128)}, u32[]{:S(2)}) copy-start(f32[19,4,16,128]{3,2,1,0:T(8,128)} %param.5) | copy-start | bytes 1867780
  2.2 21.5 %copy-start.3 = (f32[4,16,128]{2,1,0:T(8,128)}, f32[4,16,128]{2,1,0:T(8,128)S(1)}, u32[]{:S(2)}) copy-start(f32[4,16,128]{2,1,0:T(8,128)S(1)} %get-tuple-element.73.l_ref) | copy-start | bytes 98308
  2.2 32.4 %copy-start.2 = (f32[4,16,128]{2,1,0:T(8,128)}, f32[4,16,128]{2,1,0:T(8,128)S(1)}, u32[]{:S(2)}) copy-start(f32[4,16,128]{2,1,0:T(8,128)S(1)} %get-tuple-element.74.b_ref) | copy-start | bytes 98308
  4.6 10.2 %collective-permute-start = (f32[29696]{0:T(1024)S(1)}, f32[29696]{0:T(1024)S(1)}, u32[]{:S(2)}, u32[]{:S(2)}) collective-permute-start(f32[29696]{0:T(1024)S(1)} %pad_maximum_fusion.2), channel_id=1, source_target_pairs={{0,32},{32,64},{64,96},{96,128},{128,160},{160,192},{192,224},{224... | collective-permute-start | bytes 356360 | tf_op jit(solution)/shard_map/ppermute | solution.py:129
  9.3 6.4 %collective-permute-start.1 = (f32[29696]{0:T(1024)S(1)}, f32[29696]{0:T(1024)S(1)}, u32[]{:S(2)}, u32[]{:S(2)}) collective-permute-start(f32[29696]{0:T(1024)S(1)} %pad_maximum_fusion.3), channel_id=1, source_target_pairs={{32,0},{64,32},{96,64},{128,96},{160,128},{192,160},{224,192},{256... | collective-permute-start | bytes 356360 | tf_op jit(solution)/shard_map/ppermute | solution.py:129
  18.1 6.4 %collective-permute-start.2 = (f32[4480]{0:T(1024)S(1)}, f32[4480]{0:T(1024)S(1)}, u32[]{:S(2)}, u32[]{:S(2)}) collective-permute-start(f32[4480]{0:T(1024)S(1)} %concatenate.119), channel_id=1, source_target_pairs={{0,1},{1,2},{2,3},{3,4},{4,5},{5,6},{6,7},{7,8},{8,9},{9,10},{10,1... | collective-permute-start | bytes 53768 | tf_op jit(solution)/shard_map/ppermute | solution.py:129
  22.4 5.2 %collective-permute-start.3 = (f32[4480]{0:T(1024)S(1)}, f32[4480]{0:T(1024)S(1)}, u32[]{:S(2)}, u32[]{:S(2)}) collective-permute-start(f32[4480]{0:T(1024)S(1)} %concatenate.120), channel_id=1, source_target_pairs={{1,0},{2,1},{3,2},{4,3},{5,4},{6,5},{7,6},{8,7},{9,8},{10,9},{11,1... | collective-permute-start | bytes 53768 | tf_op jit(solution)/shard_map/ppermute | solution.py:129
  43.7 24.5 %copy-start.4 = (s32[16,128]{1,0:T(8,128)S(1)}, s32[16,128]{1,0:T(8,128)}, u32[]{:S(2)}) copy-start(s32[16,128]{1,0:T(8,128)} %param.8) | copy-start | bytes 24580
  44.5 0.8 copy-start.1
  49.5 4.9 %collective-permute-start.4 = (f32[4,128]{1,0:T(4,128)S(1)}, f32[4,128]{1,0:T(4,128)S(1)}, u32[]{:S(2)}, u32[]{:S(2)}) collective-permute-start(f32[4,128]{1,0:T(4,128)S(1)} %get-tuple-element.82), channel_id=1, source_target_pairs={{0,32},{32,64},{64,96},{96,128},{128,160},{160,192},{192,224},{224... | collective-permute-start | bytes 6152 | tf_op jit(solution)/shard_map/ppermute | solution.py:126
  52.4 4.9 %collective-permute-start.5 = (f32[4,128]{1,0:T(4,128)S(1)}, f32[4,128]{1,0:T(4,128)S(1)}, u32[]{:S(2)}, u32[]{:S(2)}) collective-permute-start(f32[4,128]{1,0:T(4,128)S(1)} %get-tuple-element.83), channel_id=1, source_target_pairs={{32,0},{64,32},{96,64},{128,96},{160,128},{192,160},{224,192},{256... | collective-permute-start | bytes 6152 | tf_op jit(solution)/shard_map/ppermute | solution.py:126
  57.4 5.4 %collective-permute-start.6 = (f32[24,4]{1,0:T(8,128)S(1)}, f32[24,4]{1,0:T(8,128)S(1)}, u32[]{:S(2)}, u32[]{:S(2)}) collective-permute-start(f32[24,4]{1,0:T(8,128)S(1)} %get-tuple-element.80), channel_id=1, source_target_pairs={{0,1},{1,2},{2,3},{3,4},{4,5},{5,6},{6,7},{7,8},{8,9},{9,10},{10,1... | collective-permute-start | bytes 1160 | tf_op jit(solution)/shard_map/ppermute | solution.py:126
  61.4 6.3 %collective-permute-start.7 = (f32[24,4]{1,0:T(8,128)S(1)}, f32[24,4]{1,0:T(8,128)S(1)}, u32[]{:S(2)}, u32[]{:S(2)}) collective-permute-start(f32[24,4]{1,0:T(8,128)S(1)} %get-tuple-element.81), channel_id=1, source_target_pairs={{1,0},{2,1},{3,2},{4,3},{5,4},{6,5},{7,6},{8,7},{9,8},{10,9},{11,1... | collective-permute-start | bytes 1160 | tf_op jit(solution)/shard_map/ppermute | solution.py:126

commit v11 on v10

--- a/solution.py
+++ b/solution.py
@@ -263,7 +263,9 @@
 
 def adjoint_step(section, pulled, forward_pops, blocking, lever):
     planes, width_x, width_y = blocking.shape
-    rows = 8 if width_x % 8 == 0 else width_x
+    rows = max(8, 2048 // width_y)
+    if width_x % rows:
+        rows = 8 if width_x % 8 == 0 else width_x
     vmem = pl.BlockSpec(memory_space=pltpu.VMEM)
     return pl.pallas_call(
         functools.partial(step_kernel, section, rows),

time: 113 us -> 113 us (level)
  no operation moved by 1% of the time
where the time goes in v11:
time: 113 us; the launch traced here: 112 us
  blocking collectives  37.3 us (33%)
  starting transfers between devices  25.2 us (22%)
  other arithmetic  16.6 us (15%)
  waiting for transfers between devices  11.5 us (10%)
  local copies, waits for them, and re-layouts  10.3 us (9%)
  Pallas kernels  9.78 us (9%)
  between operations  1.32 us (1%)
    all_to_all x1, blocking collectives, global_sum(): return jnp.sum(lax.all_to_all(rows, axes, 0, 0, tiled=True), axis=0)  37.3 us
    ppermute x4, starting transfers between devices, send(): got = lax.ppermute(flat, axis, pairs)  15.1 us
    ppermute x4, starting transfers between devices, send(): got = lax.ppermute(pieces[0].astype(jnp.float32), axis, pairs)  10.1 us
    pallas_call x2, Pallas kernels, adjoint_step(): pl.pallas_call(functools.partial(step_kernel, section, rows), out_shape=(...  9.78 us
    ppermute x4, waiting for transfers between devices, send(): got = lax.ppermute(pieces[0].astype(jnp.float32), axis, pairs)  7.87 us
    ppermute x4, waiting for transfers between devices, send(): got = lax.ppermute(flat, axis, pairs)  3.63 us
    another operation x1, other arithmetic, per_device(): jnp.stack([jnp.sum(smooth * region_one), jnp.sum(smooth * region_two), jn...  2.53 us
  transfers between devices with their start and end apart: 8, of which 4 were waited for; matrix products, arithmetic and copies ran while one was open for 2% of the time, Pallas kernels for 0%

profile of v11, /device:TPU:1, one launch (start us, length us, event | category | flops | bytes accessed | tf_op | source)
XLA Modules:
  0.0 111.9 jit_solution(10399001094499120433)
XLA Ops:
  0.6 0.8 multiply_select_fusion
  1.4 0.8 and_select_fusion
  2.2 1.0 slice_bitcast_fusion
  3.2 0.2 fusion.37
  3.5 1.1 %fusion.71 = (f32[19,4,2,128]{3,2,1,0:T(2,128)S(1)}, f32[19,4,2,128]{3,2,1,0:T(2,128)S(1)}) fusion(f32[19,4,16,128]{3,2,1,0:T(8,128)} %param.5), kind=kLoop, calls=%fused_computation.229 | loop fusion | bytes 311296 | tf_op jit(solution)/shard_map/slice | solution.py:122
  4.6 4.6 %collective-permute-start = (f32[29696]{0:T(1024)S(1)}, f32[29696]{0:T(1024)S(1)}, u32[]{:S(2)}, u32[]{:S(2)}) collective-permute-start(f32[29696]{0:T(1024)S(1)} %pad_maximum_fusion.2), channel_id=1, source_target_pairs={{0,32},{32,64},{64,96},{96,128},{128,160},{160,192},{192,224},{224... | collective-permute-start | bytes 356360 | tf_op jit(solution)/shard_map/ppermute | solution.py:129
  9.3 5.5 %collective-permute-start.1 = (f32[29696]{0:T(1024)S(1)}, f32[29696]{0:T(1024)S(1)}, u32[]{:S(2)}, u32[]{:S(2)}) collective-permute-start(f32[29696]{0:T(1024)S(1)} %pad_maximum_fusion.3), channel_id=1, source_target_pairs={{32,0},{64,32},{96,64},{128,96},{160,128},{192,160},{224,192},{256... | collective-permute-start | bytes 356360 | tf_op jit(solution)/shard_map/ppermute | solution.py:129
  14.9 0.8 collective-permute-done.1
  15.7 0.1 pad_maximum_fusion
  15.8 0.3 fusion.70
  16.2 0.3 reshape.228
  16.5 0.2 slice_reduce_fusion.1
  16.8 0.3 pad_maximum_fusion.1
  17.1 0.8 convert_reduce_fusion.1
  17.9 0.1 reshape.245
  18.1 3.7 %collective-permute-start.2 = (f32[4480]{0:T(1024)S(1)}, f32[4480]{0:T(1024)S(1)}, u32[]{:S(2)}, u32[]{:S(2)}) collective-permute-start(f32[4480]{0:T(1024)S(1)} %concatenate.119), channel_id=1, source_target_pairs={{0,1},{1,2},{2,3},{3,4},{4,5},{5,6},{6,7},{7,8},{8,9},{9,10},{10,1... | collective-permute-start | bytes 53768 | tf_op jit(solution)/shard_map/ppermute | solution.py:129
  21.8 0.3 reshape.233
  22.4 1.3 %collective-permute-start.3 = (f32[4480]{0:T(1024)S(1)}, f32[4480]{0:T(1024)S(1)}, u32[]{:S(2)}, u32[]{:S(2)}) collective-permute-start(f32[4480]{0:T(1024)S(1)} %concatenate.120), channel_id=1, source_target_pairs={{1,0},{2,1},{3,2},{4,3},{5,4},{6,5},{7,6},{8,7},{9,8},{10,9},{11,1... | collective-permute-start | bytes 53768 | tf_op jit(solution)/shard_map/ppermute | solution.py:129
  23.7 0.7 pad.272.l_ref
  24.5 0.3 reshape.232
  24.8 2.8 %collective-permute-done.3 = f32[4480]{0:T(1024)S(1)} collective-permute-done((f32[4480]{0:T(1024)S(1)}, f32[4480]{0:T(1024)S(1)}, u32[]{:S(2)}, u32[]{:S(2)}) %collective-permute-start.3) | collective-permute-done | bytes 17952 | tf_op jit(solution)/shard_map/ppermute | solution.py:129
  27.6 0.3 reshape.237
  28.0 0.2 maximum_bitcast_fusion.16
  28.4 0.2 maximum_bitcast_fusion.13
  29.8 1.4 %pad.32.g_ref = f32[19,4,24,256]{3,2,1,0:T(8,128)} pad(f32[19,4,18,130]{3,2,1,0:T(8,128)S(1)} %fusion.34, f32[]{:T(128)} %constant.56.clone.1), padding=0_0x0_0x0_6x0_126 | pad | bytes 2579140 | tf_op jit(solution)/shard_map/jit(_pad)/pad | solution.py:302
  31.3 0.4 convert_element_type.66
  31.7 0.4 convert_element_type.67
  32.2 0.1 reshape.248
  32.4 0.1 reshape.249
  32.6 2.1 %fusion.9.f_ref = bf16[1,19,4,24,256]{4,3,2,1,0:T(8,128)(2,1)} fusion(bf16[19,4,18,1]{3,2,1,0:T(8,128)(2,1)S(1)} %convert_element_type.67, bf16[19,4,18,1]{3,2,1,0:T(8,128)(2,1)S(1)} %convert_element_type.66, bf16[19,4,1,128]{3,2,1,0:T(2,128)(2,1)S(1)} %convert_element_type.65, bf16[19,4,16,128]{3,2,1,0:T(8,128)(2,1)S(1)} %slice_bitcast_fusion, ...), kind=kLoop, calls=%fused_computation.12 | loop fusion | flops 10739712 | bytes 1289568 | tf_op jit(solution)/shard_map/broadcast_in_dim | solution.py:321
  34.7 0.8 select_maximum_fusion.b_ref
  35.4 6.6 %shard_map.68 = (f32[19,4,24,256]{3,2,1,0:T(8,128)}, f32[24,256]{1,0:T(8,128)}) custom-call(f32[19,4,24,256]{3,2,1,0:T(8,128)} %pad.32.g_ref, bf16[1,19,4,24,256]{4,3,2,1,0:T(8,128)(2,1)} %fusion.9.f_ref, f32[4,24,256]{2,1,0:T(8,128)} %select_maximum_fusion.b_ref, f32[4,24,256]{2,1,0:T(8,128)} %pad.272.l_ref), custom_call_target="tpu_custom_call" | custom-call | tf_op jit(solution)/shard_map/pallas_call | solution.py:270
  42.0 1.7 %slice_select_fusion = f32[19,4,18,130]{3,2,1,0:T(8,128)S(1)} fusion(f32[19,4,24,256]{3,2,1,0:T(8,128)} %get-tuple-element.6, pred[18,130]{1,0:T(8,128)(4,1)S(1)} %and_and_fusion.1), kind=kLoop, calls=%fused_computation.8 | loop fusion | flops 177840 | bytes 1425060 | tf_op jit(solution)/shard_map/jit(_where)/select_n | solution.py:332
  44.5 0.8 copy-done.1
  45.3 3.2 %shard_map.69 = (f32[19,4,16,128]{3,2,1,0:T(8,128)}, f32[16,128]{1,0:T(8,128)}) custom-call(f32[19,4,16,128]{3,2,1,0:T(8,128)} %copy-done.1, bf16[2,19,4,16,128]{4,3,2,1,0:T(8,128)(2,1)} %f_ref.1, f32[4,16,128]{2,1,0:T(8,128)} %copy-done.2, f32[4,16,128]{2,1,0:T(8,128)} %copy-done.3), custom_call_target="tpu_custom_call" | custom-call | tf_op jit(solution)/shard_map/pallas_call | solution.py:270
  48.5 0.8 add_multiply_fusion
  49.4 2.9 %collective-permute-start.4 = (f32[4,128]{1,0:T(4,128)S(1)}, f32[4,128]{1,0:T(4,128)S(1)}, u32[]{:S(2)}, u32[]{:S(2)}) collective-permute-start(f32[4,128]{1,0:T(4,128)S(1)} %get-tuple-element.82), channel_id=1, source_target_pairs={{0,32},{32,64},{64,96},{96,128},{128,160},{160,192},{192,224},{224... | collective-permute-start | bytes 6152 | tf_op jit(solution)/shard_map/ppermute | solution.py:126
  52.3 1.9 %collective-permute-start.5 = (f32[4,128]{1,0:T(4,128)S(1)}, f32[4,128]{1,0:T(4,128)S(1)}, u32[]{:S(2)}, u32[]{:S(2)}) collective-permute-start(f32[4,128]{1,0:T(4,128)S(1)} %get-tuple-element.83), channel_id=1, source_target_pairs={{32,0},{64,32},{96,64},{128,96},{160,128},{192,160},{224,192},{256... | collective-permute-start | bytes 6152 | tf_op jit(solution)/shard_map/ppermute | solution.py:126
  54.3 3.0 %collective-permute-done.5 = f32[4,128]{1,0:T(4,128)S(1)} collective-permute-done((f32[4,128]{1,0:T(4,128)S(1)}, f32[4,128]{1,0:T(4,128)S(1)}, u32[]{:S(2)}, u32[]{:S(2)}) %collective-permute-start.5) | collective-permute-done | bytes 2080 | tf_op jit(solution)/shard_map/ppermute | solution.py:126
  57.3 4.0 %collective-permute-start.6 = (f32[24,4]{1,0:T(8,128)S(1)}, f32[24,4]{1,0:T(8,128)S(1)}, u32[]{:S(2)}, u32[]{:S(2)}) collective-permute-start(f32[24,4]{1,0:T(8,128)S(1)} %get-tuple-element.80), channel_id=1, source_target_pairs={{0,1},{1,2},{2,3},{3,4},{4,5},{5,6},{6,7},{7,8},{8,9},{9,10},{10,1... | collective-permute-start | bytes 1160 | tf_op jit(solution)/shard_map/ppermute | solution.py:126
  61.3 1.3 %collective-permute-start.7 = (f32[24,4]{1,0:T(8,128)S(1)}, f32[24,4]{1,0:T(8,128)S(1)}, u32[]{:S(2)}, u32[]{:S(2)}) collective-permute-start(f32[24,4]{1,0:T(8,128)S(1)} %get-tuple-element.81), channel_id=1, source_target_pairs={{1,0},{2,1},{3,2},{4,3},{5,4},{6,5},{7,6},{8,7},{9,8},{10,9},{11,1... | collective-permute-start | bytes 1160 | tf_op jit(solution)/shard_map/ppermute | solution.py:126
  62.7 4.9 %collective-permute-done.7 = f32[24,4]{1,0:T(8,128)S(1)} collective-permute-done((f32[24,4]{1,0:T(8,128)S(1)}, f32[24,4]{1,0:T(8,128)S(1)}, u32[]{:S(2)}, u32[]{:S(2)}) %collective-permute-start.7) | collective-permute-done | bytes 416 | tf_op jit(solution)/shard_map/ppermute | solution.py:126
  68.1 0.8 select_reduce_fusion.1
  68.8 2.5 %pad_maximum_fusion.17 = f32[4]{0:T(128)S(1)} fusion(f32[1]{0:T(128)} %bitcast.73, f32[1]{0:T(128)} %bitcast.72, f32[1]{0:T(128)} %bitcast.71, f32[1]{0:T(128)} %bitcast.70), kind=kLoop, calls=%fused_computation.226 | loop fusion | flops 12 | bytes 32 | tf_op jit(solution)/shard_map/stack | solution.py:340
  71.5 37.3 %all_to_all.6 = f32[512,1,4]{2,1,0:T(1,128)S(1)} all-to-all(f32[512,1,4]{2,1,0:T(1,128)S(1)} %broadcast_in_dim.60), channel_id=1, replica_groups=mesh['gx'=16,'gy'=32] {'gx','gy'}, dimensions={0} | all-to-all | bytes 16384 | tf_op jit(solution)/shard_map/all_to_all | solution.py:146
  108.8 0.6 reduce_sum.49
  109.4 0.7 fusion.75
  110.1 1.8 %select_add_fusion = f32[16,128]{1,0:T(8,128)} fusion(pred[16,128]{1,0:T(8,128)(4,1)S(1)} %get-tuple-element.22, f32[16,128]{1,0:T(8,128)S(1)} %get-tuple-element.21, pred[16,128]{1,0:T(8,128)(4,1)S(1)} %get-tuple-element.20, f32[]{:T(128)} %bitcast.75, f32[]{:T(128)} %bitcast.74), kind=kLoop, calls=%fused_computation.208 | loop fusion | flops 10240 | bytes 20488 | tf_op jit(solution)/shard_map/add | solution.py:350
  (98 shorter events, 3.9 us)
Async XLA Ops:
  0.6 15.1 %copy-start = (f32[19,4,16,128]{3,2,1,0:T(8,128)S(1)}, f32[19,4,16,128]{3,2,1,0:T(8,128)}, u32[]{:S(2)}) copy-start(f32[19,4,16,128]{3,2,1,0:T(8,128)} %param.5) | copy-start | bytes 1867780
  2.2 21.5 %copy-start.3 = (f32[4,16,128]{2,1,0:T(8,128)}, f32[4,16,128]{2,1,0:T(8,128)S(1)}, u32[]{:S(2)}) copy-start(f32[4,16,128]{2,1,0:T(8,128)S(1)} %get-tuple-element.73.l_ref) | copy-start | bytes 98308
  2.2 32.4 %copy-start.2 = (f32[4,16,128]{2,1,0:T(8,128)}, f32[4,16,128]{2,1,0:T(8,128)S(1)}, u32[]{:S(2)}) copy-start(f32[4,16,128]{2,1,0:T(8,128)S(1)} %get-tuple-element.74.b_ref) | copy-start | bytes 98308
  4.6 10.2 %collective-permute-start = (f32[29696]{0:T(1024)S(1)}, f32[29696]{0:T(1024)S(1)}, u32[]{:S(2)}, u32[]{:S(2)}) collective-permute-start(f32[29696]{0:T(1024)S(1)} %pad_maximum_fusion.2), channel_id=1, source_target_pairs={{0,32},{32,64},{64,96},{96,128},{128,160},{160,192},{192,224},{224... | collective-permute-start | bytes 356360 | tf_op jit(solution)/shard_map/ppermute | solution.py:129
  9.3 6.4 %collective-permute-start.1 = (f32[29696]{0:T(1024)S(1)}, f32[29696]{0:T(1024)S(1)}, u32[]{:S(2)}, u32[]{:S(2)}) collective-permute-start(f32[29696]{0:T(1024)S(1)} %pad_maximum_fusion.3), channel_id=1, source_target_pairs={{32,0},{64,32},{96,64},{128,96},{160,128},{192,160},{224,192},{256... | collective-permute-start | bytes 356360 | tf_op jit(solution)/shard_map/ppermute | solution.py:129
  18.1 6.4 %collective-permute-start.2 = (f32[4480]{0:T(1024)S(1)}, f32[4480]{0:T(1024)S(1)}, u32[]{:S(2)}, u32[]{:S(2)}) collective-permute-start(f32[4480]{0:T(1024)S(1)} %concatenate.119), channel_id=1, source_target_pairs={{0,1},{1,2},{2,3},{3,4},{4,5},{5,6},{6,7},{7,8},{8,9},{9,10},{10,1... | collective-permute-start | bytes 53768 | tf_op jit(solution)/shard_map/ppermute | solution.py:129
  22.4 5.2 %collective-permute-start.3 = (f32[4480]{0:T(1024)S(1)}, f32[4480]{0:T(1024)S(1)}, u32[]{:S(2)}, u32[]{:S(2)}) collective-permute-start(f32[4480]{0:T(1024)S(1)} %concatenate.120), channel_id=1, source_target_pairs={{1,0},{2,1},{3,2},{4,3},{5,4},{6,5},{7,6},{8,7},{9,8},{10,9},{11,1... | collective-permute-start | bytes 53768 | tf_op jit(solution)/shard_map/ppermute | solution.py:129
  43.7 24.3 %copy-start.4 = (s32[16,128]{1,0:T(8,128)S(1)}, s32[16,128]{1,0:T(8,128)}, u32[]{:S(2)}) copy-start(s32[16,128]{1,0:T(8,128)} %param.8) | copy-start | bytes 24580
  44.5 0.8 copy-start.1
  49.4 4.9 %collective-permute-start.4 = (f32[4,128]{1,0:T(4,128)S(1)}, f32[4,128]{1,0:T(4,128)S(1)}, u32[]{:S(2)}, u32[]{:S(2)}) collective-permute-start(f32[4,128]{1,0:T(4,128)S(1)} %get-tuple-element.82), channel_id=1, source_target_pairs={{0,32},{32,64},{64,96},{96,128},{128,160},{160,192},{192,224},{224... | collective-permute-start | bytes 6152 | tf_op jit(solution)/shard_map/ppermute | solution.py:126
  52.3 4.9 %collective-permute-start.5 = (f32[4,128]{1,0:T(4,128)S(1)}, f32[4,128]{1,0:T(4,128)S(1)}, u32[]{:S(2)}, u32[]{:S(2)}) collective-permute-start(f32[4,128]{1,0:T(4,128)S(1)} %get-tuple-element.83), channel_id=1, source_target_pairs={{32,0},{64,32},{96,64},{128,96},{160,128},{192,160},{224,192},{256... | collective-permute-start | bytes 6152 | tf_op jit(solution)/shard_map/ppermute | solution.py:126
  57.3 5.4 %collective-permute-start.6 = (f32[24,4]{1,0:T(8,128)S(1)}, f32[24,4]{1,0:T(8,128)S(1)}, u32[]{:S(2)}, u32[]{:S(2)}) collective-permute-start(f32[24,4]{1,0:T(8,128)S(1)} %get-tuple-element.80), channel_id=1, source_target_pairs={{0,1},{1,2},{2,3},{3,4},{4,5},{5,6},{6,7},{7,8},{8,9},{9,10},{10,1... | collective-permute-start | bytes 1160 | tf_op jit(solution)/shard_map/ppermute | solution.py:126
  61.3 6.3 %collective-permute-start.7 = (f32[24,4]{1,0:T(8,128)S(1)}, f32[24,4]{1,0:T(8,128)S(1)}, u32[]{:S(2)}, u32[]{:S(2)}) collective-permute-start(f32[24,4]{1,0:T(8,128)S(1)} %get-tuple-element.81), channel_id=1, source_target_pairs={{1,0},{2,1},{3,2},{4,3},{5,4},{6,5},{7,6},{8,7},{9,8},{10,9},{11,1... | collective-permute-start | bytes 1160 | tf_op jit(solution)/shard_map/ppermute | solution.py:126

commit v12 on v11

--- a/solution.py
+++ b/solution.py
@@ -310,7 +310,12 @@
     ).astype(jnp.float32)
     lever = jnp.where((solid_mask == 0) & inside[None], BLOCK_LIMIT, 0.0).astype(jnp.float32)
     saved_one = forward_pops[1]
-    adj_ext, saved_ext, block_ext = halo_many([adjoint_in, saved_one, blocking], [2, 1, 1])
+    adj_ext, saved_ext, solid_ext, label_ext, design_ext = halo_many(
+        [adjoint_in, saved_one, solid_mask, region_label, design], [2, 1, 1, 1, 1]
+    )
+    block_ext = jnp.where(
+        solid_ext == 1, 1.0, jnp.where((label_ext > 0)[None], BLOCK_LIMIT * design_ext[None], 0.0)
+    ).astype(jnp.float32)
     ext_x, ext_y = width_x + 2, width_y + 2
     rows = -(-ext_x // 8) * 8
     cols = -(-ext_y // 128) * 128

time: 113 us -> 115 us (1.018)
  waiting for transfers between devices: 11.5 us -> 1.44 us
  blocking collectives: 37.3 us -> 42.5 us
  starting transfers between devices: 25.2 us -> 28.6 us
  other arithmetic: 16.6 us -> 18.6 us
  local copies, waits for them, and re-layouts: 10.3 us -> 11.9 us
    ppermute x4, waiting for transfers between devices: 7.87 us -> 1.43 us  [send(): got = lax.ppermute(pieces[0].astype(jnp.float32), axis, pairs)]
    all_to_all x1, blocking collectives: 37.3 us -> 42.5 us  [global_sum(): return jnp.sum(lax.all_to_all(rows, axes, 0, 0, tiled=True), axis=0)]
    ppermute x4, waiting for transfers between devices: 3.63 us -> 0.01 us  [send(): got = lax.ppermute(flat, axis, pairs)]
    ppermute x4, starting transfers between devices: 10.1 us -> 12.6 us  [send(): got = lax.ppermute(pieces[0].astype(jnp.float32), axis, pairs)]
    convert_element_type x0 -> x7, other arithmetic: none -> 1.24 us  [the longest x3 1.08 us: send(): flat = jnp.concatenate([p.astype(jnp.float32).reshape(-1) for p in pieces])]
    pad x2 -> x3, local copies, waits for them, and re-layouts: 2.13 us -> 2.8 us  [pad_to(): return jnp.pad(a, pad)]
  transfers between devices with their start and end apart: 8 -> 8, of which waited for: 4 -> 2; matrix products, arithmetic and copies ran while one was open for 2% -> 3% of each run, Pallas kernels for 0% -> 0%
where the time goes in v12:
time: 115 us; the launch traced here: 114 us
  blocking collectives  42.5 us (37%)
  starting transfers between devices  28.6 us (25%)
  other arithmetic  18.6 us (16%)
  local copies, waits for them, and re-layouts  11.9 us (10%)
  Pallas kernels  9.77 us (8%)
  waiting for transfers between devices  1.44 us (1%)
  between operations  1.4 us (1%)
    all_to_all x1, blocking collectives, global_sum(): return jnp.sum(lax.all_to_all(rows, axes, 0, 0, tiled=True), axis=0)  42.5 us
    ppermute x4, starting transfers between devices, send(): got = lax.ppermute(flat, axis, pairs)  15.9 us
    ppermute x4, starting transfers between devices, send(): got = lax.ppermute(pieces[0].astype(jnp.float32), axis, pairs)  12.6 us
    pallas_call x2, Pallas kernels, adjoint_step(): pl.pallas_call(functools.partial(step_kernel, section, rows), out_shape=(...  9.77 us
    pad x3, local copies, waits for them, and re-layouts, pad_to(): return jnp.pad(a, pad)  2.8 us
    another operation x1, other arithmetic, per_device(): jnp.stack([jnp.sum(smooth * region_one), jnp.sum(smooth * region_two), jn...  2.5 us
  transfers between devices with their start and end apart: 8, of which 2 were waited for; matrix products, arithmetic and copies ran while one was open for 3% of the time, Pallas kernels for 0%

profile of v12, /device:TPU:1, one launch (start us, length us, event | category | flops | bytes accessed | tf_op | source)
XLA Modules:
  0.0 114.2 jit_solution(12159916649428727085)
XLA Ops:
  0.6 1.2 %fusion.72 = (f32[19,4,2,128]{3,2,1,0:T(2,128)S(1)}, f32[19,4,2,128]{3,2,1,0:T(2,128)S(1)}) fusion(f32[19,4,16,128]{3,2,1,0:T(8,128)} %param.5), kind=kLoop, calls=%fused_computation.257 | loop fusion | bytes 311296 | tf_op jit(solution)/shard_map/slice | solution.py:122
  1.8 1.0 slice_bitcast_fusion
  2.8 0.2 fusion.31
  3.1 0.7 slice_convert_fusion.13
  3.9 0.7 constant_dynamic-update-slice_fusion.23
  4.6 0.7 constant_dynamic-update-slice_fusion.21
  5.3 8.7 %collective-permute-start.1 = (f32[29952]{0:T(1024)S(1)}, f32[29952]{0:T(1024)S(1)}, u32[]{:S(2)}, u32[]{:S(2)}) collective-permute-start(f32[29952]{0:T(1024)S(1)} %get-tuple-element.97), channel_id=1, source_target_pairs={{32,0},{64,32},{96,64},{128,96},{160,128},{192,160},{224,192},{256... | collective-permute-start | bytes 359432 | tf_op jit(solution)/shard_map/ppermute | solution.py:129
  14.1 1.9 %collective-permute-start = (f32[29952]{0:T(1024)S(1)}, f32[29952]{0:T(1024)S(1)}, u32[]{:S(2)}, u32[]{:S(2)}) collective-permute-start(f32[29952]{0:T(1024)S(1)} %get-tuple-element.96), channel_id=1, source_target_pairs={{0,32},{32,64},{64,96},{96,128},{128,160},{160,192},{192,224},{224... | collective-permute-start | bytes 359432 | tf_op jit(solution)/shard_map/ppermute | solution.py:129
  16.0 0.7 multiply_select_fusion
  16.8 1.4 %compare_select_fusion = (f32[4,16,128]{2,1,0:T(8,128)}, f32[4,16,128]{2,1,0:T(8,128)S(1)}) fusion(s32[4,16,128]{2,1,0:T(8,128)} %param.7, f32[16,128]{1,0:T(8,128)S(1)} %get-tuple-element.27, pred[16,128]{1,0:T(8,128)(4,1)S(1)} %get-tuple-element.28), kind=kLoop, calls=%fused_computation.126 | loop fusion | flops 40960 | bytes 108544 | tf_op jit(solution)/shard_map/jit(_where)/select_n | solution.py:308
  18.3 0.2 pad_maximum_fusion
  18.4 0.3 fusion.71
  18.8 0.3 reshape.338
  19.1 0.3 pad_maximum_fusion.1
  19.4 0.8 convert_reduce_fusion.1
  20.4 0.2 fusion.29
  20.7 0.2 fusion.58
  20.9 0.2 slice_reduce_fusion.1
  21.2 1.3 %collective-permute-start.3 = (f32[4516]{0:T(1024)S(1)}, f32[4516]{0:T(1024)S(1)}, u32[]{:S(2)}, u32[]{:S(2)}) collective-permute-start(f32[4516]{0:T(1024)S(1)} %concatenate.150), channel_id=1, source_target_pairs={{1,0},{2,1},{3,2},{4,3},{5,4},{6,5},{7,6},{8,7},{9,8},{10,9},{11,1... | collective-permute-start | bytes 54200 | tf_op jit(solution)/shard_map/ppermute | solution.py:129
  22.5 0.3 reshape.329
  23.0 4.0 %collective-permute-start.2 = (f32[4516]{0:T(1024)S(1)}, f32[4516]{0:T(1024)S(1)}, u32[]{:S(2)}, u32[]{:S(2)}) collective-permute-start(f32[4516]{0:T(1024)S(1)} %concatenate.149), channel_id=1, source_target_pairs={{0,1},{1,2},{2,3},{3,4},{4,5},{5,6},{6,7},{7,8},{8,9},{9,10},{10,1... | collective-permute-start | bytes 54200 | tf_op jit(solution)/shard_map/ppermute | solution.py:129
  27.1 0.7 pad.277.l_ref
  27.8 0.3 reshape.344
  28.1 0.3 reshape.337
  28.7 0.2 maximum_bitcast_fusion.16
  28.9 0.2 maximum_bitcast_fusion.13
  30.3 1.4 %pad.32.g_ref = f32[19,4,24,256]{3,2,1,0:T(8,128)} pad(f32[19,4,18,130]{3,2,1,0:T(8,128)S(1)} %fusion.25, f32[]{:T(128)} %constant.28.clone.1), padding=0_0x0_0x0_6x0_126 | pad | bytes 2579140 | tf_op jit(solution)/shard_map/jit(_pad)/pad | solution.py:302
  31.8 0.4 convert_element_type.189
  32.3 0.4 convert_element_type.188
  33.9 0.7 pad.34.b_ref
  34.5 2.1 %fusion.9.f_ref = bf16[1,19,4,24,256]{4,3,2,1,0:T(8,128)(2,1)} fusion(bf16[19,4,18,1]{3,2,1,0:T(8,128)(2,1)S(1)} %convert_element_type.189, bf16[19,4,18,1]{3,2,1,0:T(8,128)(2,1)S(1)} %convert_element_type.188, bf16[19,4,1,128]{3,2,1,0:T(2,128)(2,1)S(1)} %convert_element_type.187, bf16[19,4,16,128]{3,2,1,0:T(8,128)(2,1)S(1)} %slice_bitcast_fusion, ...), kind=kLoop, calls=%fused_computation.12 | loop fusion | flops 10739712 | bytes 1289568 | tf_op jit(solution)/shard_map/broadcast_in_dim | solution.py:326
  36.6 6.6 %shard_map.68 = (f32[19,4,24,256]{3,2,1,0:T(8,128)}, f32[24,256]{1,0:T(8,128)}) custom-call(f32[19,4,24,256]{3,2,1,0:T(8,128)} %pad.32.g_ref, bf16[1,19,4,24,256]{4,3,2,1,0:T(8,128)(2,1)} %fusion.9.f_ref, f32[4,24,256]{2,1,0:T(8,128)} %pad.34.b_ref, f32[4,24,256]{2,1,0:T(8,128)} %pad.277.l_ref), custom_call_target="tpu_custom_call" | custom-call | tf_op jit(solution)/shard_map/pallas_call | solution.py:270
  43.2 1.7 %slice_select_fusion = f32[19,4,18,130]{3,2,1,0:T(8,128)S(1)} fusion(f32[19,4,24,256]{3,2,1,0:T(8,128)} %get-tuple-element.6, pred[18,130]{1,0:T(8,128)(4,1)S(1)} %and_and_fusion.1), kind=kLoop, calls=%fused_computation.8 | loop fusion | flops 177840 | bytes 1425060 | tf_op jit(solution)/shard_map/jit(_where)/select_n | solution.py:337
  45.7 0.8 copy-done.1
  46.5 3.2 %shard_map.69 = (f32[19,4,16,128]{3,2,1,0:T(8,128)}, f32[16,128]{1,0:T(8,128)}) custom-call(f32[19,4,16,128]{3,2,1,0:T(8,128)} %copy-done.1, bf16[2,19,4,16,128]{4,3,2,1,0:T(8,128)(2,1)} %f_ref.1, f32[4,16,128]{2,1,0:T(8,128)} %get-tuple-element.81.b_ref, f32[4,16,128]{2,1,0:T(8,128)} %copy-done.3), custom_call_target="tpu_custom_call" | custom-call | tf_op jit(solution)/shard_map/pallas_call | solution.py:270
  49.7 0.8 add_multiply_fusion
  50.6 3.3 %collective-permute-start.5 = (f32[4,128]{1,0:T(4,128)S(1)}, f32[4,128]{1,0:T(4,128)S(1)}, u32[]{:S(2)}, u32[]{:S(2)}) collective-permute-start(f32[4,128]{1,0:T(4,128)S(1)} %get-tuple-element.95), channel_id=1, source_target_pairs={{32,0},{64,32},{96,64},{128,96},{160,128},{192,160},{224,192},{256... | collective-permute-start | bytes 6152 | tf_op jit(solution)/shard_map/ppermute | solution.py:126
  53.9 3.5 %collective-permute-start.4 = (f32[4,128]{1,0:T(4,128)S(1)}, f32[4,128]{1,0:T(4,128)S(1)}, u32[]{:S(2)}, u32[]{:S(2)}) collective-permute-start(f32[4,128]{1,0:T(4,128)S(1)} %get-tuple-element.94), channel_id=1, source_target_pairs={{0,32},{32,64},{64,96},{96,128},{128,160},{160,192},{192,224},{224... | collective-permute-start | bytes 6152 | tf_op jit(solution)/shard_map/ppermute | solution.py:126
  57.4 0.7 collective-permute-done.4
  58.2 1.3 %collective-permute-start.7 = (f32[24,4]{1,0:T(8,128)S(1)}, f32[24,4]{1,0:T(8,128)S(1)}, u32[]{:S(2)}, u32[]{:S(2)}) collective-permute-start(f32[24,4]{1,0:T(8,128)S(1)} %get-tuple-element.93), channel_id=1, source_target_pairs={{1,0},{2,1},{3,2},{4,3},{5,4},{6,5},{7,6},{8,7},{9,8},{10,9},{11,1... | collective-permute-start | bytes 1160 | tf_op jit(solution)/shard_map/ppermute | solution.py:126
  59.4 4.6 %collective-permute-start.6 = (f32[24,4]{1,0:T(8,128)S(1)}, f32[24,4]{1,0:T(8,128)S(1)}, u32[]{:S(2)}, u32[]{:S(2)}) collective-permute-start(f32[24,4]{1,0:T(8,128)S(1)} %get-tuple-element.92), channel_id=1, source_target_pairs={{0,1},{1,2},{2,3},{3,4},{4,5},{5,6},{6,7},{7,8},{8,9},{9,10},{10,1... | collective-permute-start | bytes 1160 | tf_op jit(solution)/shard_map/ppermute | solution.py:126
  64.1 0.7 collective-permute-done.6
  65.3 0.7 select_reduce_fusion.1
  66.0 2.5 %pad_maximum_fusion.15 = f32[4]{0:T(128)S(1)} fusion(f32[1]{0:T(128)} %bitcast.85, f32[1]{0:T(128)} %bitcast.84, f32[1]{0:T(128)} %bitcast.83, f32[1]{0:T(128)} %bitcast.82), kind=kLoop, calls=%fused_computation.254 | loop fusion | flops 12 | bytes 32 | tf_op jit(solution)/shard_map/stack | solution.py:345
  68.7 42.5 %all_to_all.6 = f32[512,1,4]{2,1,0:T(1,128)S(1)} all-to-all(f32[512,1,4]{2,1,0:T(1,128)S(1)} %broadcast_in_dim.81), channel_id=1, replica_groups=mesh['gx'=16,'gy'=32] {'gx','gy'}, dimensions={0} | all-to-all | bytes 16384 | tf_op jit(solution)/shard_map/all_to_all | solution.py:146
  111.2 0.6 reduce_sum.49
  111.8 0.6 fusion.75
  112.4 1.8 %select_add_fusion = f32[16,128]{1,0:T(8,128)} fusion(pred[16,128]{1,0:T(8,128)(4,1)S(1)} %get-tuple-element.26, f32[16,128]{1,0:T(8,128)S(1)} %get-tuple-element.25, pred[16,128]{1,0:T(8,128)(4,1)S(1)} %get-tuple-element.24, f32[]{:T(128)} %bitcast.87, f32[]{:T(128)} %bitcast.86), kind=kLoop, calls=%fused_computation.210 | loop fusion | flops 10240 | bytes 20488 | tf_op jit(solution)/shard_map/add | solution.py:355
  (119 shorter events, 5.2 us)
Async XLA Ops:
  0.6 17.6 %copy-start = (f32[19,4,16,128]{3,2,1,0:T(8,128)S(1)}, f32[19,4,16,128]{3,2,1,0:T(8,128)}, u32[]{:S(2)}) copy-start(f32[19,4,16,128]{3,2,1,0:T(8,128)} %param.5) | copy-start | bytes 1867780
  5.3 12.9 %collective-permute-start.1 = (f32[29952]{0:T(1024)S(1)}, f32[29952]{0:T(1024)S(1)}, u32[]{:S(2)}, u32[]{:S(2)}) collective-permute-start(f32[29952]{0:T(1024)S(1)} %get-tuple-element.97), channel_id=1, source_target_pairs={{32,0},{64,32},{96,64},{128,96},{160,128},{192,160},{224,192},{256... | collective-permute-start | bytes 359432 | tf_op jit(solution)/shard_map/ppermute | solution.py:129
  14.1 4.2 %collective-permute-start = (f32[29952]{0:T(1024)S(1)}, f32[29952]{0:T(1024)S(1)}, u32[]{:S(2)}, u32[]{:S(2)}) collective-permute-start(f32[29952]{0:T(1024)S(1)} %get-tuple-element.96), channel_id=1, source_target_pairs={{0,32},{32,64},{64,96},{96,128},{128,160},{160,192},{192,224},{224... | collective-permute-start | bytes 359432 | tf_op jit(solution)/shard_map/ppermute | solution.py:129
  18.1 8.9 %copy-start.3 = (f32[4,16,128]{2,1,0:T(8,128)}, f32[4,16,128]{2,1,0:T(8,128)S(1)}, u32[]{:S(2)}) copy-start(f32[4,16,128]{2,1,0:T(8,128)S(1)} %get-tuple-element.82.l_ref) | copy-start | bytes 98308
  18.8 1.6 %copy-start.2 = (s32[4,16,128]{2,1,0:T(8,128)S(1)}, s32[4,16,128]{2,1,0:T(8,128)}, u32[]{:S(2)}) copy-start(s32[4,16,128]{2,1,0:T(8,128)} %param.7) | copy-start | bytes 98308
  18.8 1.9 %copy-start.4 = (s32[16,128]{1,0:T(8,128)S(1)}, s32[16,128]{1,0:T(8,128)}, u32[]{:S(2)}) copy-start(s32[16,128]{1,0:T(8,128)} %param.8) | copy-start | bytes 24580
  18.8 2.1 %copy-start.5 = (f32[16,128]{1,0:T(8,128)S(1)}, f32[16,128]{1,0:T(8,128)}, u32[]{:S(2)}) copy-start(f32[16,128]{1,0:T(8,128)} %param.9) | copy-start | bytes 24580
  21.2 6.7 %collective-permute-start.3 = (f32[4516]{0:T(1024)S(1)}, f32[4516]{0:T(1024)S(1)}, u32[]{:S(2)}, u32[]{:S(2)}) collective-permute-start(f32[4516]{0:T(1024)S(1)} %concatenate.150), channel_id=1, source_target_pairs={{1,0},{2,1},{3,2},{4,3},{5,4},{6,5},{7,6},{8,7},{9,8},{10,9},{11,1... | collective-permute-start | bytes 54200 | tf_op jit(solution)/shard_map/ppermute | solution.py:129
  23.0 5.1 %collective-permute-start.2 = (f32[4516]{0:T(1024)S(1)}, f32[4516]{0:T(1024)S(1)}, u32[]{:S(2)}, u32[]{:S(2)}) collective-permute-start(f32[4516]{0:T(1024)S(1)} %concatenate.149), channel_id=1, source_target_pairs={{0,1},{1,2},{2,3},{3,4},{4,5},{5,6},{6,7},{7,8},{8,9},{9,10},{10,1... | collective-permute-start | bytes 54200 | tf_op jit(solution)/shard_map/ppermute | solution.py:129
  45.7 0.8 copy-start.1
  50.6 6.8 %collective-permute-start.5 = (f32[4,128]{1,0:T(4,128)S(1)}, f32[4,128]{1,0:T(4,128)S(1)}, u32[]{:S(2)}, u32[]{:S(2)}) collective-permute-start(f32[4,128]{1,0:T(4,128)S(1)} %get-tuple-element.95), channel_id=1, source_target_pairs={{32,0},{64,32},{96,64},{128,96},{160,128},{192,160},{224,192},{256... | collective-permute-start | bytes 6152 | tf_op jit(solution)/shard_map/ppermute | solution.py:126
  53.9 4.2 %collective-permute-start.4 = (f32[4,128]{1,0:T(4,128)S(1)}, f32[4,128]{1,0:T(4,128)S(1)}, u32[]{:S(2)}, u32[]{:S(2)}) collective-permute-start(f32[4,128]{1,0:T(4,128)S(1)} %get-tuple-element.94), channel_id=1, source_target_pairs={{0,32},{32,64},{64,96},{96,128},{128,160},{160,192},{192,224},{224... | collective-permute-start | bytes 6152 | tf_op jit(solution)/shard_map/ppermute | solution.py:126
  58.2 5.9 %collective-permute-start.7 = (f32[24,4]{1,0:T(8,128)S(1)}, f32[24,4]{1,0:T(8,128)S(1)}, u32[]{:S(2)}, u32[]{:S(2)}) collective-permute-start(f32[24,4]{1,0:T(8,128)S(1)} %get-tuple-element.93), channel_id=1, source_target_pairs={{1,0},{2,1},{3,2},{4,3},{5,4},{6,5},{7,6},{8,7},{9,8},{10,9},{11,1... | collective-permute-start | bytes 1160 | tf_op jit(solution)/shard_map/ppermute | solution.py:126
  59.4 5.4 %collective-permute-start.6 = (f32[24,4]{1,0:T(8,128)S(1)}, f32[24,4]{1,0:T(8,128)S(1)}, u32[]{:S(2)}, u32[]{:S(2)}) collective-permute-start(f32[24,4]{1,0:T(8,128)S(1)} %get-tuple-element.92), channel_id=1, source_target_pairs={{0,1},{1,2},{2,3},{3,4},{4,5},{5,6},{6,7},{7,8},{8,9},{9,10},{10,1... | collective-permute-start | bytes 1160 | tf_op jit(solution)/shard_map/ppermute | solution.py:126
